TPU v7x, 128 devices: a whole 4x4x4 slice. The times are simulated.
128 devices in a mesh: dom: 16 (over x, z_hi, core), cls: 8 (over z_lo, y).
Axes of the slice: x: 4, y: 4, z: 4 (z_hi: 2, z_lo: 2; z = z_hi * 2 + z_lo), core: 2. Of those that a mesh axis runs over, the one named last changes fastest.
Arguments:
- particles: bfloat16 [2048, 16384], P(('dom', 'cls')), may hold values from -6 to 6
- averages: float32 [256, 16384], P('cls'), may hold values from -4 to 4
- prior_mass: float32 [256], P('cls'), may hold values from 1 to 8
- group_ids: int32 [4, 2048, 1], P(None, ('dom', 'cls')), may hold values from 0 to 7; in each aligned block of 16 rows (0 to 15, 16 to 31, ..., all dimensions but the last counted through in order) at most 6 rows name the same one
- class_ids: int32 [4, 2048], P(None, ('dom', 'cls')), may hold values from 0 to 31
- rot_ids: int32 [4, 2048], P(None, ('dom', 'cls')), may hold values from 0 to 63
- weights: bfloat16 [4, 2048], P(None, ('dom', 'cls')), may hold values from 0.25 to 4
- owners: int32 [4], replicated, may hold values from 0 to 7
Outputs:
- scores: float32 [4, 2048, 2048], P(None, ('dom', 'cls'))
- final_averages: float32 [256, 16384], P('cls')
Inputs may be any that keep to these rules, and one draw needn't show every extreme that they name: `group_ids`: in every step, at most 6 of the 16 particles of one device name one class group; in every step some device's particles reach 6 for some group.
All inputs are finite; a program needn't handle non-finite values.
Results may differ from a plain program's by a relative error of at most 0.0027.
Values may be sent and summed in bfloat16 or wider, within the bound.
No kernel may reach another device: no remote copies, remote signals or barrier semaphores. Data moves between devices by JAX's collectives and lax.ppermute only.
A program may use at most 256 MiB of HBM per device.

v0:
```python
import math

import jax
import jax.numpy as jnp
from jax import lax
from jax.sharding import PartitionSpec as P

RADII = 128
ANGLES = 128
ROT = 64
STEPS = 4
ASTEP = 2


def from_root(block, axis, owner):
    block = jnp.where(lax.axis_index(axis) == owner, block, jnp.zeros_like(block))
    return lax.psum(block, axis)


def rotate_each(images, shifts, angles):
    angle_idx = jnp.arange(angles, dtype=jnp.int32)
    index = (angle_idx[None, :] - shifts[:, None]) % angles
    return jnp.take_along_axis(images, index[:, None, :], axis=2)


def per_device(particles, averages, prior_mass, group_ids, class_ids, rot_ids, weights, owners):
    per_dev = particles.shape[0]
    pixels = particles.shape[1]
    groups = lax.axis_size("cls")
    per_group = averages.shape[0]
    capacity = per_dev * 3 // 8
    slots = groups * capacity
    cube = particles.reshape(per_dev, RADII, ANGLES)
    doubled = jnp.concatenate([cube, cube], axis=2)
    scale = 1.0 / math.sqrt(pixels)
    turns_block = min(ROT, max(8, 512 // per_dev))
    block_starts = list(range(0, ROT, turns_block))
    current = averages
    all_scores = []
    for step in range(STEPS):
        shifts = rot_ids[step] * ASTEP
        rotated = rotate_each(cube, shifts, ANGLES).reshape(per_dev, pixels)
        target = group_ids[step, :, 0]
        onehot_group = (target[:, None] == jnp.arange(groups, dtype=jnp.int32)[None, :]).astype(
            jnp.int32
        )
        rank = jnp.sum((jnp.cumsum(onehot_group, axis=0) - 1) * onehot_group, axis=1)
        slot_of = target * capacity + rank
        placing = (slot_of[None, :] == jnp.arange(slots, dtype=jnp.int32)[:, None]).astype(
            jnp.bfloat16
        )
        send_images = jnp.dot(placing, rotated, preferred_element_type=jnp.float32).astype(
            jnp.bfloat16
        )
        class_hot = (
            class_ids[step][:, None] == jnp.arange(per_group, dtype=jnp.int32)[None, :]
        ).astype(jnp.bfloat16)
        weighted_hot = class_hot * weights[step][:, None]
        send_weights = jnp.dot(placing, weighted_hot, preferred_element_type=jnp.float32).astype(
            jnp.bfloat16
        )
        got_images, got_weights = (
            lax.all_to_all(send_images, "cls", split_axis=0, concat_axis=0, tiled=True),
            lax.all_to_all(send_weights, "cls", split_axis=0, concat_axis=0, tiled=True),
        )
        partial_value = lax.dot_general(
            got_weights, got_images, (((0,), (0,)), ((), ())), preferred_element_type=jnp.float32
        )
        counts = jnp.sum(got_weights.astype(jnp.float32), axis=0)
        totals, mass = lax.psum((partial_value, counts), "dom")
        current = (prior_mass[:, None] * current + totals) / (prior_mass + mass)[:, None]
        refs = from_root(current.astype(jnp.bfloat16), "cls", owners[step])
        pieces = []
        for first in block_starts:
            count = min(turns_block, ROT - first)
            views = [
                doubled[:, :, ANGLES - turn * ASTEP : 2 * ANGLES - turn * ASTEP]
                for turn in range(first, first + count)
            ]
            rolled = jnp.stack(views, axis=1).reshape(per_dev * count, pixels)
            product = lax.dot_general(
                rolled, refs, (((1,), (1,)), ((), ())), preferred_element_type=jnp.float32
            )
            pieces.append(product.reshape(per_dev, count * per_group))
        stacked = jnp.concatenate(pieces, axis=1)
        all_scores.append(stacked * scale)
    return (jnp.stack(all_scores, axis=0), current)


def solution(mesh):
    return jax.shard_map(
        per_device,
        mesh=mesh,
        in_specs=(
            P(("dom", "cls"), None),
            P("cls", None),
            P("cls"),
            P(None, ("dom", "cls"), None),
            P(None, ("dom", "cls")),
            P(None, ("dom", "cls")),
            P(None, ("dom", "cls")),
            P(),
        ),
        out_specs=(P(None, ("dom", "cls"), None), P("cls", None)),
        check_vma=False,
    )
```

profile of v0, /device:TPU:1, one launch (start us, length us, event | category | flops | bytes accessed | tf_op | source)
XLA Modules:
  0.0 682.3 jit_solution(3866032299633491612)
XLA Ops:
  12.0 6.4 all-to-all-start.6
  20.8 11.1 %gather_fusion.3 = bf16[2048,128]{1,0:T(8,128)(2,1)S(1)} fusion(bf16[16,128,128]{1,2,0:T(8,128)(2,1)S(1)} %copy.50, s32[2048]{0:T(1024)S(1)} %get-tuple-element.115), kind=kCustom, calls=%fused_computation.3.clone | custom fusion | bytes 1064960 | tf_op jit(solution)/shard_map/jit(take_along_axis)/gather | solution.py:23
  34.1 5.1 all-to-all-start.4
  40.2 4.1 all-to-all-done.4
  44.3 3.3 all-to-all-start.2
  48.6 4.0 all-to-all-done.2
  52.6 3.3 all-to-all-start
  56.0 1.6 convolution_convert_fusion
  57.6 1.6 all_to_all.62
  59.2 1.8 all-to-all-done
  61.0 4.4 all-to-all-start.7
  65.3 11.1 %gather_fusion.2 = bf16[2048,128]{1,0:T(8,128)(2,1)S(1)} fusion(bf16[16,128,128]{1,2,0:T(8,128)(2,1)S(1)} %copy.50, s32[2048]{0:T(1024)S(1)} %get-tuple-element.116), kind=kCustom, calls=%fused_computation.2.clone | custom fusion | bytes 1064960 | tf_op jit(solution)/shard_map/jit(take_along_axis)/gather | solution.py:23
  77.4 1.7 all_to_all.58
  79.0 13.3 %all-to-all-done.7 = bf16[8,6,16384]{2,1,0:T(8,128)(2,1)} async-done(((bf16[8,6,16384]{2,1,0:T(8,128)(2,1)}), bf16[8,6,16384]{2,1,0:T(8,128)(2,1)}, u32[]{:S(2)}, u32[]{:S(2)}) %all-to-all-start.7) | async-done | bytes 1572896 | tf_op jit(solution)/shard_map/all_to_all | solution.py:63
  92.4 4.3 all-to-all-start.5
  96.8 11.1 %gather_fusion.1 = bf16[2048,128]{1,0:T(8,128)(2,1)S(1)} fusion(bf16[16,128,128]{1,2,0:T(8,128)(2,1)S(1)} %copy.50, s32[2048]{0:T(1024)S(1)} %get-tuple-element.117), kind=kCustom, calls=%fused_computation.1.clone | custom fusion | bytes 1064960 | tf_op jit(solution)/shard_map/jit(take_along_axis)/gather | solution.py:23
  109.0 1.6 all_to_all.54
  110.6 13.2 %all-to-all-done.5 = bf16[8,6,16384]{2,1,0:T(8,128)(2,1)} async-done(((bf16[8,6,16384]{2,1,0:T(8,128)(2,1)}), bf16[8,6,16384]{2,1,0:T(8,128)(2,1)}, u32[]{:S(2)}, u32[]{:S(2)}) %all-to-all-start.5) | async-done | bytes 1572896 | tf_op jit(solution)/shard_map/all_to_all | solution.py:63
  123.8 4.4 all-to-all-start.3
  128.2 11.1 %gather_fusion = bf16[2048,128]{1,0:T(8,128)(2,1)S(1)} fusion(bf16[16,128,128]{1,2,0:T(8,128)(2,1)S(1)} %copy.50, s32[2048]{0:T(1024)S(1)} %get-tuple-element.118), kind=kCustom, calls=%fused_computation.clone | custom fusion | bytes 1064960 | tf_op jit(solution)/shard_map/jit(take_along_axis)/gather | solution.py:23
  140.2 1.7 all_to_all.50
  141.9 13.3 %all-to-all-done.3 = bf16[8,6,16384]{2,1,0:T(8,128)(2,1)} async-done(((bf16[8,6,16384]{2,1,0:T(8,128)(2,1)}), bf16[8,6,16384]{2,1,0:T(8,128)(2,1)}, u32[]{:S(2)}, u32[]{:S(2)}) %all-to-all-start.3) | async-done | bytes 1572896 | tf_op jit(solution)/shard_map/all_to_all | solution.py:63
  155.2 4.4 all-to-all-start.1
  159.9 3.9 convolution_bitcast_fusion
  163.7 3.9 convolution_bitcast_fusion.1
  167.7 4.0 convolution_bitcast_fusion.2
  171.6 15.1 %all-to-all-done.1 = bf16[8,6,16384]{2,1,0:T(8,128)(2,1)} async-done(((bf16[8,6,16384]{2,1,0:T(8,128)(2,1)}), bf16[8,6,16384]{2,1,0:T(8,128)(2,1)}, u32[]{:S(2)}, u32[]{:S(2)}) %all-to-all-start.1) | async-done | bytes 1572896 | tf_op jit(solution)/shard_map/all_to_all | solution.py:63
  186.7 3.9 convolution_bitcast_fusion.3
  195.2 1.4 fusion.94
  197.9 1.4 fusion.92
  200.7 1.4 fusion.90
  202.1 1.4 fusion.89
  203.5 1.4 fusion.88
  204.9 1.4 fusion.87
  206.2 1.4 fusion.86
  208.9 1.4 fusion.84
  211.7 1.4 fusion.82
  213.1 1.4 fusion.81
  214.5 1.4 fusion.80
  216.0 34.7 %all-reduce = (f32[32]{0:T(128)S(1)}, f32[32]{0:T(128)S(1)}, f32[32]{0:T(128)S(1)}, f32[32]{0:T(128)S(1)}) all-reduce(f32[32]{0:T(128)S(1)} %convert_reduce_fusion, f32[32]{0:T(128)S(1)} %convert_reduce_fusion.1, f32[32]{0:T(128)S(1)} %convert_reduce_fusion.2, f32[32]{0:T(128)S(1)} %convert_reduce_fusion.3), channel_id=1, replica_groups=mesh['dom'=16,'cls'=8] {'dom'}, use_global_device_ids=true, to_apply=%region_22.24 | all-reduce | flops 128 | bytes 1024 | tf_op jit(solution)/shard_map/psum | solution.py:70
  250.7 146.9 %all-reduce.6.cloned.1.call-done = (f32[32,16384]{1,0:T(8,128)}, f32[32,16384]{1,0:T(8,128)}, f32[32,16384]{1,0:T(8,128)}, f32[32,16384]{1,0:T(8,128)}) async-done(((f32[32,16384]{1,0:T(8,128)}, f32[32,16384]{1,0:T(8,128)}, f32[32,16384]{1,0:T(8,128)}, f32[32,16384]{1,0:T(8,128)}), (f32[32,16384]{1,0:T(8,128)}, f32[32,16384]{1,0:T(8,128)}, f32[32,16384]{1,0:T(8,128)}, ...) | async-done | bytes 8388624 | tf_op jit(solution)/shard_map/psum | solution.py:70
  397.5 4.2 convert_select_fusion.2
  401.8 4.9 convert_select_fusion
  406.7 1.4 fusion.79
  408.1 1.4 fusion.78
  410.8 1.4 fusion.76
  416.2 1.4 fusion.72
  417.6 1.4 fusion.71
  419.0 1.4 fusion.70
  421.8 1.4 fusion.68
  424.5 1.4 fusion.66
  425.9 1.4 fusion.65
  427.2 1.4 fusion.64
  428.6 14.3 %copy.48 = bf16[16,32,128,128]{3,2,1,0:T(8,128)(2,1)} copy(bf16[16,32,128,128]{3,2,0,1:T(8,128)(2,1)} %get-tuple-element.21) | data formatting | bytes 33554432 | tf_op jit(solution)/shard_map/stack | solution.py:80
  442.9 14.2 %copy.55 = bf16[16,32,128,128]{3,2,1,0:T(8,128)(2,1)} copy(bf16[16,32,128,128]{3,2,0,1:T(8,128)(2,1)} %get-tuple-element.22) | data formatting | bytes 33554432 | tf_op jit(solution)/shard_map/stack | solution.py:80
  457.1 53.9 %all-reduce.8.cloned.1.call-done = (bf16[32,16384]{1,0:T(8,128)(2,1)}, bf16[32,16384]{1,0:T(8,128)(2,1)}, bf16[32,16384]{1,0:T(8,128)(2,1)}, bf16[32,16384]{1,0:T(8,128)(2,1)}) async-done(((bf16[32,16384]{1,0:T(8,128)(2,1)}, bf16[32,16384]{1,0:T(8,128)(2,1)}, bf16[32,16384]{1,0:T(8,128)(2,1)}, bf16[32,16384]{1,0:T(8,128)(2,1)}), (bf16[32,16384]{1,0:T(8,128)(2,1)}, bf16[32,16384]{1,0:T(8,128)(2,1)}, ...) | async-done | bytes 4194320 | tf_op jit(solution)/shard_map/psum | solution.py:17
  511.1 23.1 %fusion.14 = f32[512,32]{1,0:T(8,128)S(1)} fusion(bf16[32,16384]{1,0:T(8,128)(2,1)} %get-tuple-element.14, bf16[64,8,128,128]{3,2,1,0:T(8,128)(2,1)} %bitcast.404), kind=kOutput, calls=%fused_computation.26 | convolution fusion | flops 536870912 | bytes 17891328 | tf_op jit(solution)/shard_map/dot_general | solution.py:81
  534.2 21.5 %fusion.6 = f32[512,32]{1,0:T(8,128)S(1)} fusion(bf16[32,16384]{1,0:T(8,128)(2,1)} %get-tuple-element.14, bf16[64,8,128,128]{3,2,1,0:T(8,128)(2,1)} %bitcast.410), kind=kOutput, calls=%fused_computation.18 | convolution fusion | flops 536870912 | bytes 17891328 | tf_op jit(solution)/shard_map/dot_general | solution.py:81
  555.8 17.4 %fusion.12 = f32[512,32]{1,0:T(8,128)S(1)} fusion(bf16[32,16384]{1,0:T(8,128)(2,1)S(1)} %copy-done.3, bf16[64,8,128,128]{3,2,1,0:T(8,128)(2,1)S(1)} %bitcast.407), kind=kOutput, calls=%fused_computation.24 | convolution fusion | flops 536870912 | bytes 17891328 | tf_op jit(solution)/shard_map/dot_general | solution.py:81
  573.2 21.0 %fusion.4 = f32[512,32]{1,0:T(8,128)S(1)} fusion(bf16[32,16384]{1,0:T(8,128)(2,1)} %get-tuple-element.13, bf16[64,8,128,128]{3,2,1,0:T(8,128)(2,1)} %bitcast.411), kind=kOutput, calls=%fused_computation.16 | convolution fusion | flops 536870912 | bytes 17891328 | tf_op jit(solution)/shard_map/dot_general | solution.py:81
  594.2 18.6 %fusion.10 = f32[512,32]{1,0:T(8,128)S(1)} fusion(bf16[32,16384]{1,0:T(8,128)(2,1)} %get-tuple-element.12, bf16[64,8,128,128]{3,2,1,0:T(8,128)(2,1)S(1)} %bitcast.408), kind=kOutput, calls=%fused_computation.22 | convolution fusion | flops 536870912 | bytes 17891328 | tf_op jit(solution)/shard_map/dot_general | solution.py:81
  612.8 21.0 %fusion.2 = f32[512,32]{1,0:T(8,128)S(1)} fusion(bf16[32,16384]{1,0:T(8,128)(2,1)} %get-tuple-element.12, bf16[64,8,128,128]{3,2,1,0:T(8,128)(2,1)} %bitcast.412), kind=kOutput, calls=%fused_computation.14 | convolution fusion | flops 536870912 | bytes 17891328 | tf_op jit(solution)/shard_map/dot_general | solution.py:81
  633.8 18.4 %fusion.8 = f32[512,32]{1,0:T(8,128)S(1)} fusion(bf16[32,16384]{1,0:T(8,128)(2,1)} %get-tuple-element.11, bf16[64,8,128,128]{3,2,1,0:T(8,128)(2,1)S(1)} %bitcast.409), kind=kOutput, calls=%fused_computation.20 | convolution fusion | flops 536870912 | bytes 17891328 | tf_op jit(solution)/shard_map/dot_general | solution.py:81
  652.2 20.8 %fusion = f32[512,32]{1,0:T(8,128)S(1)} fusion(bf16[32,16384]{1,0:T(8,128)(2,1)} %get-tuple-element.11, bf16[64,8,128,128]{3,2,1,0:T(8,128)(2,1)} %bitcast.413), kind=kOutput, calls=%fused_computation.12 | convolution fusion | flops 536870912 | bytes 17891328 | tf_op jit(solution)/shard_map/dot_general | solution.py:81
  (98 shorter events, 32.2 us)
Async XLA Ops:
  12.0 22.1 %all-to-all-start.6 = ((bf16[8,6,32]{2,1,0:T(8,128)(2,1)}), bf16[8,6,32]{2,1,0:T(8,128)(2,1)S(1)}, u32[]{:S(2)}, u32[]{:S(2)}) async-start(bf16[8,6,32]{2,1,0:T(8,128)(2,1)} %all_to_all.60), calls=%async_computation.6 | async-start | bytes 32768 | tf_op jit(solution)/shard_map/all_to_all | solution.py:64
  34.1 10.2 %all-to-all-start.4 = ((bf16[8,6,32]{2,1,0:T(8,128)(2,1)}), bf16[8,6,32]{2,1,0:T(8,128)(2,1)S(1)}, u32[]{:S(2)}, u32[]{:S(2)}) async-start(bf16[8,6,32]{2,1,0:T(8,128)(2,1)} %all_to_all.56), calls=%async_computation.4 | async-start | bytes 32768 | tf_op jit(solution)/shard_map/all_to_all | solution.py:64
  44.3 8.3 %all-to-all-start.2 = ((bf16[8,6,32]{2,1,0:T(8,128)(2,1)}), bf16[8,6,32]{2,1,0:T(8,128)(2,1)S(1)}, u32[]{:S(2)}, u32[]{:S(2)}) async-start(bf16[8,6,32]{2,1,0:T(8,128)(2,1)} %all_to_all.52), calls=%async_computation.2 | async-start | bytes 32768 | tf_op jit(solution)/shard_map/all_to_all | solution.py:64
  52.6 8.3 %all-to-all-start = ((bf16[8,6,32]{2,1,0:T(8,128)(2,1)}), bf16[8,6,32]{2,1,0:T(8,128)(2,1)S(1)}, u32[]{:S(2)}, u32[]{:S(2)}) async-start(bf16[8,6,32]{2,1,0:T(8,128)(2,1)} %all_to_all.48), calls=%async_computation | async-start | bytes 32768 | tf_op jit(solution)/shard_map/all_to_all | solution.py:64
  61.0 31.4 %all-to-all-start.7 = ((bf16[8,6,16384]{2,1,0:T(8,128)(2,1)}), bf16[8,6,16384]{2,1,0:T(8,128)(2,1)}, u32[]{:S(2)}, u32[]{:S(2)}) async-start(bf16[8,6,16384]{2,1,0:T(8,128)(2,1)} %all_to_all.62), calls=%async_computation.7 | async-start | bytes 4194304 | tf_op jit(solution)/shard_map/all_to_all | solution.py:63
  92.4 31.4 %all-to-all-start.5 = ((bf16[8,6,16384]{2,1,0:T(8,128)(2,1)}), bf16[8,6,16384]{2,1,0:T(8,128)(2,1)}, u32[]{:S(2)}, u32[]{:S(2)}) async-start(bf16[8,6,16384]{2,1,0:T(8,128)(2,1)} %all_to_all.58), calls=%async_computation.5 | async-start | bytes 4194304 | tf_op jit(solution)/shard_map/all_to_all | solution.py:63
  123.8 31.4 %all-to-all-start.3 = ((bf16[8,6,16384]{2,1,0:T(8,128)(2,1)}), bf16[8,6,16384]{2,1,0:T(8,128)(2,1)}, u32[]{:S(2)}, u32[]{:S(2)}) async-start(bf16[8,6,16384]{2,1,0:T(8,128)(2,1)} %all_to_all.54), calls=%async_computation.3 | async-start | bytes 4194304 | tf_op jit(solution)/shard_map/all_to_all | solution.py:63
  155.2 31.5 %all-to-all-start.1 = ((bf16[8,6,16384]{2,1,0:T(8,128)(2,1)}), bf16[8,6,16384]{2,1,0:T(8,128)(2,1)}, u32[]{:S(2)}, u32[]{:S(2)}) async-start(bf16[8,6,16384]{2,1,0:T(8,128)(2,1)} %all_to_all.50), calls=%async_computation.1 | async-start | bytes 4194304 | tf_op jit(solution)/shard_map/all_to_all | solution.py:63
  159.6 31.0 %copy-start.1 = (s32[4]{0:T(128)S(1)}, s32[4]{0:T(128)}, u32[]{:S(2)}) copy-start(s32[4]{0:T(128)} %param.17) | copy-start | bytes 52
  159.6 237.9 %all-reduce.6.cloned.1.call-start = ((), (), s32[]{:S(2)}) async-start(), calls=%async_computation.8 | async-start | bytes 16777216 | tf_op jit(solution)/shard_map/psum | solution.py:70
  190.6 320.5 %all-reduce.8.cloned.1.call-start = ((), (), s32[]{:S(2)}) async-start(), calls=%async_computation.9 | async-start | bytes 8388608 | tf_op jit(solution)/shard_map/psum | solution.py:17
  194.0 56.7 %copy-start.2 = (f32[32]{0:T(128)S(1)}, f32[32]{0:T(128)}, u32[]{:S(2)}) copy-start(f32[32]{0:T(128)} %param.12) | copy-start | bytes 388
  195.2 202.3 %copy-start = (f32[32,16384]{1,0:T(8,128)S(1)}, f32[32,16384]{1,0:T(8,128)}, u32[]{:S(2)}) copy-start(f32[32,16384]{1,0:T(8,128)} %param.11) | copy-start | bytes 6291460
  511.1 44.7 %slice-start = ((s8[16777216]{0:T(1024)(128)(4,1)}), s8[4194304]{0:T(1024)(128)(4,1)S(1)}, s32[]{:S(2)}) async-start(s8[16777216]{0:T(1024)(128)(4,1)} %bitcast.405), calls=%async_computation.10 | async-start | bytes 8388608
  511.1 44.7 %slice-start.1 = ((s8[16777216]{0:T(1024)(128)(4,1)}), s8[4194304]{0:T(1024)(128)(4,1)S(1)}, s32[]{:S(2)}) async-start(s8[16777216]{0:T(1024)(128)(4,1)} %bitcast.405), calls=%async_computation.11 | async-start | bytes 8388608
  534.2 21.6 %copy-start.3 = (bf16[32,16384]{1,0:T(8,128)(2,1)S(1)}, bf16[32,16384]{1,0:T(8,128)(2,1)}, u32[]{:S(2)}) copy-start(bf16[32,16384]{1,0:T(8,128)(2,1)} %get-tuple-element.13) | copy-start | bytes 3145732
  534.2 21.6 %slice-start.2 = ((s8[16777216]{0:T(1024)(128)(4,1)}), s8[4194304]{0:T(1024)(128)(4,1)S(1)}, s32[]{:S(2)}) async-start(s8[16777216]{0:T(1024)(128)(4,1)} %bitcast.405), calls=%async_computation.12 | async-start | bytes 8388608
  534.2 21.6 %slice-start.3 = ((s8[16777216]{0:T(1024)(128)(4,1)}), s8[4194304]{0:T(1024)(128)(4,1)S(1)}, s32[]{:S(2)}) async-start(s8[16777216]{0:T(1024)(128)(4,1)} %bitcast.405), calls=%async_computation.13 | async-start | bytes 8388608
Sparse Core Ops, SparseCore 0:
  190.7 206.8 all-reduce.5
  406.8 104.1 all-reduce.7
where the time goes:
time: 691 us; the launch traced here: 682 us
  waiting for transfers between devices  266 us (38%)
  matrix products  182 us (26%)
  local copies, waits for them, and re-layouts  133 us (19%)
  starting transfers between devices  35.9 us (5%)
  blocking collectives  34.7 us (5%)
  between operations  17.4 us (3%)
  other arithmetic  13.8 us (2%)
    dot_general x8, matrix products, per_device(): lax.dot_general(rolled, refs, (((1,), (1,)), ((), ())), preferred_element...  162 us
    psum x1, waiting for transfers between devices, per_device(): totals, mass = lax.psum((partial_value, counts), 'dom')  147 us
    all_to_all x4, waiting for transfers between devices, per_device(): lax.all_to_all(send_images, 'cls', split_axis=0, concat_axis=0, tiled=True)  54.9 us
    psum x1, waiting for transfers between devices, from_root(): return lax.psum(block, axis)  53.9 us
    gather x8, local copies, waits for them, and re-layouts, rotate_each(): return jnp.take_along_axis(images, index[:, None, :], axis=2)  45.6 us
    unnamed x49, local copies, waits for them, and re-layouts  43.7 us
    psum x1, blocking collectives, per_device(): totals, mass = lax.psum((partial_value, counts), 'dom')  34.7 us
    another operation x3, local copies, waits for them, and re-layouts, per_device(): rolled = jnp.stack(views, axis=1).reshape(per_dev * count, pixels)  29.9 us
  transfers between devices with their start and end apart: 10, of which 9 were waited for; matrix products, arithmetic and copies ran while one was open for 20% of the time, Pallas kernels for 0%

commit v1 on v0

v1 whole, which is shorter than its diff:
```python
import math

import jax
import jax.numpy as jnp
from jax import lax
from jax.sharding import PartitionSpec as P

RADII = 128
ANGLES = 128
ROT = 64
STEPS = 4
ASTEP = 2


def rotate_each(cube, shifts):
    src = jnp.arange(ANGLES, dtype=jnp.int32)
    dst = (src[None, :, None] + shifts[:, None, None]) % ANGLES
    perm = (dst == src[None, None, :]).astype(cube.dtype)
    out = jnp.einsum("iab,ibc->iac", cube, perm, preferred_element_type=jnp.float32)
    return out.astype(cube.dtype)


def per_device(particles, averages, prior_mass, group_ids, class_ids, rot_ids, weights, owners):
    per_dev = particles.shape[0]
    pixels = particles.shape[1]
    groups = lax.axis_size("cls")
    doms = lax.axis_size("dom")
    chunk = pixels // doms
    per_group = averages.shape[0]
    capacity = per_dev * 3 // 8
    slots = groups * capacity
    me_dom = lax.axis_index("dom")
    me_cls = lax.axis_index("cls")
    cube = particles.reshape(per_dev, RADII, ANGLES)
    doubled = jnp.concatenate([cube, cube], axis=2)
    scale = 1.0 / math.sqrt(pixels)
    turns_block = min(ROT, max(8, 512 // per_dev))
    block_starts = list(range(0, ROT, turns_block))

    send_img = []
    send_wts = []
    for step in range(STEPS):
        shifts = rot_ids[step] * ASTEP
        rotated = rotate_each(cube, shifts).reshape(per_dev, pixels)
        target = group_ids[step, :, 0]
        onehot_group = (target[:, None] == jnp.arange(groups, dtype=jnp.int32)[None, :]).astype(
            jnp.int32
        )
        rank = jnp.sum((jnp.cumsum(onehot_group, axis=0) - 1) * onehot_group, axis=1)
        slot_of = target * capacity + rank
        placing = (slot_of[None, :] == jnp.arange(slots, dtype=jnp.int32)[:, None]).astype(
            jnp.bfloat16
        )
        images = jnp.dot(placing, rotated, preferred_element_type=jnp.float32).astype(jnp.bfloat16)
        images = images.reshape(groups, capacity, doms, chunk).transpose(2, 0, 1, 3)
        send_img.append(images)
        class_hot = (
            class_ids[step][:, None] == jnp.arange(per_group, dtype=jnp.int32)[None, :]
        ).astype(jnp.bfloat16)
        weighted_hot = class_hot * weights[step][:, None]
        wts = jnp.dot(placing, weighted_hot, preferred_element_type=jnp.float32).astype(
            jnp.bfloat16
        )
        wts = jnp.broadcast_to(wts.reshape(1, groups, capacity, per_group), (doms, groups, capacity, per_group))
        send_wts.append(wts)
    send_img = jnp.stack(send_img, axis=2).reshape(doms * groups, STEPS, capacity, chunk)
    send_wts = jnp.stack(send_wts, axis=2).reshape(doms * groups, STEPS, capacity, per_group)
    got_img = lax.all_to_all(send_img, ("dom", "cls"), 0, 0, tiled=True)
    got_wts = lax.all_to_all(send_wts, ("dom", "cls"), 0, 0, tiled=True)
    totals = lax.dot_general(
        got_wts, got_img, (((0, 2), (0, 2)), ((1,), (1,))), preferred_element_type=jnp.float32
    )
    mass = jnp.sum(got_wts.astype(jnp.float32), axis=(0, 2))

    current = lax.dynamic_slice_in_dim(averages, me_dom * chunk, chunk, axis=1)
    ref_chunks = []
    for step in range(STEPS):
        current = (prior_mass[:, None] * current + totals[step]) / (prior_mass + mass[step])[:, None]
        piece = current.astype(jnp.bfloat16)
        piece = jnp.where(me_cls == owners[step], piece, jnp.zeros_like(piece))
        ref_chunks.append(piece)
    ref_chunks = lax.psum(jnp.stack(ref_chunks, axis=0), "cls")
    all_refs = lax.all_gather(ref_chunks, "dom", axis=0, tiled=False)
    all_refs = all_refs.transpose(1, 2, 0, 3).reshape(STEPS, per_group, pixels)
    final = lax.all_gather(current, "dom", axis=0, tiled=False)
    final = final.transpose(1, 0, 2).reshape(per_group, pixels)

    all_scores = []
    for step in range(STEPS):
        refs = all_refs[step]
        pieces = []
        for first in block_starts:
            count = min(turns_block, ROT - first)
            views = [
                doubled[:, :, ANGLES - turn * ASTEP : 2 * ANGLES - turn * ASTEP]
                for turn in range(first, first + count)
            ]
            rolled = jnp.stack(views, axis=1).reshape(per_dev * count, pixels)
            product = lax.dot_general(
                rolled, refs, (((1,), (1,)), ((), ())), preferred_element_type=jnp.float32
            )
            pieces.append(product.reshape(per_dev, count * per_group))
        stacked = jnp.concatenate(pieces, axis=1)
        all_scores.append(stacked * scale)
    return (jnp.stack(all_scores, axis=0), final)


def solution(mesh):
    return jax.shard_map(
        per_device,
        mesh=mesh,
        in_specs=(
            P(("dom", "cls"), None),
            P("cls", None),
            P("cls"),
            P(None, ("dom", "cls"), None),
            P(None, ("dom", "cls")),
            P(None, ("dom", "cls")),
            P(None, ("dom", "cls")),
            P(),
        ),
        out_specs=(P(None, ("dom", "cls"), None), P("cls", None)),
        check_vma=False,
    )
```

time: 691 us -> 471 us (0.68)
  waiting for transfers between devices: 266 us -> 123 us
  blocking collectives: 34.7 us -> 0 us
  starting transfers between devices: 35.9 us -> 22.1 us
  local copies, waits for them, and re-layouts: 133 us -> 121 us
  matrix products: 182 us -> 172 us
    psum x2 -> x1, waiting for transfers between devices: 201 us -> 51.4 us  [per_device(): ref_chunks = lax.psum(jnp.stack(ref_chunks, axis=0), 'cls')]
    gather x8 -> x0, local copies, waits for them, and re-layouts: 45.6 us -> none  [rotate_each(): return jnp.take_along_axis(images, index[:, None, :], axis=2)]
    psum x1 -> x0, blocking collectives: 34.7 us -> none  [per_device(): totals, mass = lax.psum((partial_value, counts), 'dom')]
    unnamed x49 -> x90, local copies, waits for them, and re-layouts: 43.7 us -> 72.6 us
    all_to_all x8 -> x2, starting transfers between devices: 35.6 us -> 21.8 us  [the longest x1 11.7 us: per_device(): got_wts = lax.all_to_all(send_wts, ('dom', 'cls'), 0, 0, tiled=True)]
    another operation x3, local copies, waits for them, and re-layouts: 29.9 us -> 16.2 us  [per_device(): rolled = jnp.stack(views, axis=1).reshape(per_dev * count, pixels)]
    all_gather x0 -> x2, waiting for transfers between devices: none -> 10.8 us  [the longest x1 10.8 us: per_device(): all_refs = lax.all_gather(ref_chunks, 'dom', axis=0, tiled=False)]
    another operation x0 -> x13, local copies, waits for them, and re-layouts: none -> 10.5 us  [the longest x1 10.3 us: per_device(): jnp.stack(send_img, axis=2).reshape(doms * groups, STEPS, capacity, chunk)]
  transfers between devices with their start and end apart: 10 -> 5, of which waited for: 9 -> 3; matrix products, arithmetic and copies ran while one was open for 20% -> 24% of each run, Pallas kernels for 0% -> 0%
where the time goes in v1:
time: 471 us; the launch traced here: 467 us
  matrix products  172 us (37%)
  waiting for transfers between devices  123 us (26%)
  local copies, waits for them, and re-layouts  121 us (26%)
  starting transfers between devices  22.1 us (5%)
  between operations  18.8 us (4%)
  other arithmetic  10.2 us (2%)
    dot_general x8, matrix products, per_device(): lax.dot_general(rolled, refs, (((1,), (1,)), ((), ())), preferred_element...  157 us
    unnamed x90, local copies, waits for them, and re-layouts  72.6 us
    all_to_all x1, waiting for transfers between devices, per_device(): got_img = lax.all_to_all(send_img, ('dom', 'cls'), 0, 0, tiled=True)  60.6 us
    psum x1, waiting for transfers between devices, per_device(): ref_chunks = lax.psum(jnp.stack(ref_chunks, axis=0), 'cls')  51.4 us
    another operation x3, local copies, waits for them, and re-layouts, per_device(): rolled = jnp.stack(views, axis=1).reshape(per_dev * count, pixels)  16.2 us
    all_to_all x1, starting transfers between devices, per_device(): got_wts = lax.all_to_all(send_wts, ('dom', 'cls'), 0, 0, tiled=True)  11.7 us
    all_gather x1, waiting for transfers between devices, per_device(): all_refs = lax.all_gather(ref_chunks, 'dom', axis=0, tiled=False)  10.8 us
    another operation x1, local copies, waits for them, and re-layouts, per_device(): jnp.stack(send_img, axis=2).reshape(doms * groups, STEPS, capacity, chunk)  10.3 us
  transfers between devices with their start and end apart: 5, of which 3 were waited for; matrix products, arithmetic and copies ran while one was open for 24% of the time, Pallas kernels for 0%

profile of v1, /device:TPU:1, one launch (start us, length us, event | category | flops | bytes accessed | tf_op | source)
XLA Modules:
  0.0 466.9 jit_solution(8276902115353094044)
XLA Ops:
  14.4 1.3 reshape.477
  15.7 11.7 %all-to-all-start = ((bf16[128,2,384]{2,1,0:T(2,128)(2,1)}), bf16[128,2,384]{2,1,0:T(2,128)(2,1)S(1)}, u32[]{:S(2)}, u32[]{:S(2)}) async-start(bf16[128,2,384]{2,1,0:T(2,128)(2,1)} %reshape.477), calls=%async_computation | async-start | bytes 393216 | tf_op jit(solution)/shard_map/all_to_all | solution.py:69
  28.2 1.1 copy.284
  41.1 1.3 copy.363
  42.4 3.2 pad_maximum_fusion
  45.6 10.3 %copy.227 = bf16[128,4,6,1024]{3,1,2,0:T(4,128)(2,1)} copy(bf16[128,4,6,1024]{3,0,2,1:T(8,128)(2,1)} %pad_maximum_fusion) | data formatting | bytes 12582912 | tf_op jit(solution)/shard_map/stack | solution.py:66
  55.9 10.2 %all-to-all-start.1 = ((bf16[128,4,6,1024]{3,1,2,0:T(4,128)(2,1)}), bf16[128,4,6,1024]{3,1,2,0:T(4,128)(2,1)}, u32[]{:S(2)}, u32[]{:S(2)}) async-start(bf16[128,4,6,1024]{3,1,2,0:T(4,128)(2,1)} %copy.227), calls=%async_computation.1 | async-start | bytes 12582912 | tf_op jit(solution)/shard_map/all_to_all | solution.py:68
  71.4 1.1 fusion.104
  72.5 1.1 fusion.103
  74.6 1.0 fusion.101
  76.6 1.0 fusion.99
  78.7 1.0 fusion.97
  79.7 1.1 fusion.96
  82.8 1.1 fusion.93
  85.1 60.6 %all-to-all-done.1 = bf16[128,4,6,1024]{3,1,2,0:T(4,128)(2,1)} async-done(((bf16[128,4,6,1024]{3,1,2,0:T(4,128)(2,1)}), bf16[128,4,6,1024]{3,1,2,0:T(4,128)(2,1)}, u32[]{:S(2)}, u32[]{:S(2)}) %all-to-all-start.1) | async-done | bytes 6291488 | tf_op jit(solution)/shard_map/all_to_all | solution.py:68
  145.6 9.7 %fusion.30 = f32[4,32,1024]{2,1,0:T(8,128)S(1)} fusion(bf16[128,4,6,1024]{3,1,2,0:T(4,128)(2,1)} %all-to-all-done.1, bf16[128,4,6,32]{3,1,2,0:T(4,128)(2,1)S(1)} %bitcast.549), kind=kOutput, calls=%fused_computation.44 | convolution fusion | flops 201326592 | bytes 7012352 | tf_op jit(solution)/shard_map/dot_general | solution.py:70
  160.3 1.0 fusion.90
  161.4 1.0 fusion.89
  162.4 1.0 fusion.88
  163.4 1.0 fusion.87
  164.5 1.0 fusion.86
  165.5 1.0 fusion.85
  167.6 1.0 fusion.83
  170.6 1.0 fusion.80
  171.7 1.1 fusion.79
  173.7 1.0 fusion.77
  174.8 1.0 fusion.76
  175.8 1.1 fusion.75
  176.9 51.4 %all-reduce.2.cloned.1.call-done = bf16[1,4,32,1024]{3,2,1,0:T(8,128)(2,1)} async-done(((bf16[1,4,32,1024]{3,2,1,0:T(8,128)(2,1)}), bf16[1,4,32,1024]{3,2,1,0:T(8,128)(2,1)}) %all-reduce.2.cloned.1.call-update) | async-done | bytes 262160 | tf_op jit(solution)/shard_map/psum | solution.py:82
  229.3 14.2 %copy.209 = bf16[16,32,128,128]{3,2,1,0:T(8,128)(2,1)} copy(bf16[16,32,128,128]{3,2,0,1:T(8,128)(2,1)} %fusion.74) | data formatting | bytes 33554432 | tf_op jit(solution)/shard_map/stack | solution.py:98
  243.4 1.0 fusion.72
  245.5 1.0 fusion.70
  246.5 1.0 fusion.69
  247.6 1.0 fusion.68
  248.6 1.0 fusion.67
  249.6 1.0 fusion.66
  250.7 1.0 fusion.65
  253.8 1.0 fusion.62
  258.8 1.0 fusion.57
  260.9 1.0 fusion.55
  261.9 1.0 fusion.54
  263.0 1.0 fusion.53
  268.1 1.0 fusion.48
  273.2 1.0 fusion.43
  274.2 1.0 fusion.42
  275.3 3.2 copy.283
  278.4 10.8 %all-gather.4.cloned.1.call-done = bf16[16,4,32,1024]{3,2,1,0:T(8,128)(2,1)} async-done(((bf16[1,4,32,1024]{3,2,1,0:T(8,128)(2,1)}), bf16[16,4,32,1024]{3,2,1,0:T(8,128)(2,1)}) %all-gather.4.cloned.1.call-update) | async-done | bytes 4194320 | tf_op jit(solution)/shard_map/all_gather | solution.py:83
  289.2 2.6 fusion.172
  292.0 1.2 copy.298
  293.3 18.1 %fusion = f32[512,32]{1,0:T(8,128)} fusion(bf16[32,16384]{1,0:T(8,128)(2,1)S(1)} %bitcast.574, bf16[64,8,128,128]{3,2,1,0:T(8,128)(2,1)} %bitcast.216), kind=kOutput, calls=%fused_computation.4 | convolution fusion | flops 536870912 | bytes 17891328 | tf_op jit(solution)/shard_map/dot_general | solution.py:99
  311.4 24.1 %fusion.2 = f32[512,32]{1,0:T(8,128)} fusion(bf16[32,16384]{1,0:T(8,128)(2,1)} %bitcast.576, bf16[64,8,128,128]{3,2,1,0:T(8,128)(2,1)} %bitcast.216), kind=kOutput, calls=%fused_computation.6 | convolution fusion | flops 536870912 | bytes 17891328 | tf_op jit(solution)/shard_map/dot_general | solution.py:99
  335.5 18.4 %fusion.8 = f32[512,32]{1,0:T(8,128)S(1)} fusion(bf16[32,16384]{1,0:T(8,128)(2,1)} %bitcast.575, bf16[64,8,128,128]{3,2,1,0:T(8,128)(2,1)S(1)} %bitcast.545), kind=kOutput, calls=%fused_computation.12 | convolution fusion | flops 536870912 | bytes 17891328 | tf_op jit(solution)/shard_map/dot_general | solution.py:99
  353.9 18.8 %fusion.10 = f32[512,32]{1,0:T(8,128)S(1)} fusion(bf16[32,16384]{1,0:T(8,128)(2,1)} %bitcast.577, bf16[64,8,128,128]{3,2,1,0:T(8,128)(2,1)S(1)} %bitcast.546), kind=kOutput, calls=%fused_computation.14 | convolution fusion | flops 536870912 | bytes 17891328 | tf_op jit(solution)/shard_map/dot_general | solution.py:99
  372.7 1.1 copy.297
  373.7 23.9 %fusion.4 = f32[512,32]{1,0:T(8,128)} fusion(bf16[32,16384]{1,0:T(8,128)(2,1)} %bitcast.580, bf16[64,8,128,128]{3,2,1,0:T(8,128)(2,1)} %bitcast.216), kind=kOutput, calls=%fused_computation.8 | convolution fusion | flops 536870912 | bytes 17891328 | tf_op jit(solution)/shard_map/dot_general | solution.py:99
  397.7 18.2 %fusion.12 = f32[512,32]{1,0:T(8,128)} fusion(bf16[32,16384]{1,0:T(8,128)(2,1)S(1)} %bitcast.581, bf16[64,8,128,128]{3,2,1,0:T(8,128)(2,1)S(1)} %bitcast.547), kind=kOutput, calls=%fused_computation.16 | convolution fusion | flops 536870912 | bytes 17891328 | tf_op jit(solution)/shard_map/dot_general | solution.py:99
  416.0 17.6 %fusion.6 = f32[512,32]{1,0:T(8,128)} fusion(bf16[32,16384]{1,0:T(8,128)(2,1)S(1)} %bitcast.578, bf16[64,8,128,128]{3,2,1,0:T(8,128)(2,1)} %bitcast.216), kind=kOutput, calls=%fused_computation.10 | convolution fusion | flops 536870912 | bytes 17891328 | tf_op jit(solution)/shard_map/dot_general | solution.py:99
  433.6 17.9 %fusion.14 = f32[512,32]{1,0:T(8,128)} fusion(bf16[32,16384]{1,0:T(8,128)(2,1)S(1)} %bitcast.579, bf16[64,8,128,128]{3,2,1,0:T(8,128)(2,1)S(1)} %bitcast.548), kind=kOutput, calls=%fused_computation.18 | convolution fusion | flops 536870912 | bytes 17891328 | tf_op jit(solution)/shard_map/dot_general | solution.py:99
  451.5 1.1 concatenate.71
  452.6 1.1 concatenate.68
  453.7 1.1 concatenate.62
  454.7 1.1 concatenate.65
  455.8 1.1 concatenate.61
  456.9 1.1 concatenate.64
  (132 shorter events, 55.6 us)
Async XLA Ops:
  15.7 40.2 %all-to-all-start = ((bf16[128,2,384]{2,1,0:T(2,128)(2,1)}), bf16[128,2,384]{2,1,0:T(2,128)(2,1)S(1)}, u32[]{:S(2)}, u32[]{:S(2)}) async-start(bf16[128,2,384]{2,1,0:T(2,128)(2,1)} %reshape.477), calls=%async_computation | async-start | bytes 393216 | tf_op jit(solution)/shard_map/all_to_all | solution.py:69
  42.4 23.7 %copy-start.2 = (s32[4]{0:T(128)S(1)}, s32[4]{0:T(128)}, u32[]{:S(2)}) copy-start(s32[4]{0:T(128)} %param.15) | copy-start | bytes 52
  55.9 29.2 %copy-start.3 = (f32[32]{0:T(128)S(1)}, f32[32]{0:T(128)}, u32[]{:S(2)}) copy-start(f32[32]{0:T(128)} %param.10) | copy-start | bytes 388
  55.9 89.7 %all-to-all-start.1 = ((bf16[128,4,6,1024]{3,1,2,0:T(4,128)(2,1)}), bf16[128,4,6,1024]{3,1,2,0:T(4,128)(2,1)}, u32[]{:S(2)}, u32[]{:S(2)}) async-start(bf16[128,4,6,1024]{3,1,2,0:T(4,128)(2,1)} %copy.227), calls=%async_computation.1 | async-start | bytes 12582912 | tf_op jit(solution)/shard_map/all_to_all | solution.py:68
  66.1 162.2 %all-reduce.2.cloned.1.call-start = ((), (), s32[]{:S(2)}) async-start(), calls=%async_computation.2 | async-start | bytes 524288 | tf_op jit(solution)/shard_map/psum | solution.py:82
  158.0 117.3 %all-gather.6.cloned.1.call-start = ((), (), s32[]{:S(2)}) async-start(), calls=%async_computation.4 | async-start | bytes 2228224 | tf_op jit(solution)/shard_map/all_gather | solution.py:85
  160.3 129.0 %all-gather.4.cloned.1.call-start = ((), (), s32[]{:S(2)}) async-start(), calls=%async_computation.3 | async-start | bytes 4456448 | tf_op jit(solution)/shard_map/all_gather | solution.py:83
  292.0 1.3 copy-start
  293.3 42.2 %slice-start = ((s8[16777216]{0:T(1024)(128)(4,1)}), s8[4194304]{0:T(1024)(128)(4,1)S(1)}, s32[]{:S(2)}) async-start(s8[16777216]{0:T(1024)(128)(4,1)} %bitcast.543), calls=%async_computation.5 | async-start | bytes 8388608
  293.3 42.2 %slice-start.1 = ((s8[16777216]{0:T(1024)(128)(4,1)}), s8[4194304]{0:T(1024)(128)(4,1)S(1)}, s32[]{:S(2)}) async-start(s8[16777216]{0:T(1024)(128)(4,1)} %bitcast.543), calls=%async_computation.6 | async-start | bytes 8388608
  311.4 24.1 %slice-start.2 = ((s8[16777216]{0:T(1024)(128)(4,1)}), s8[4194304]{0:T(1024)(128)(4,1)S(1)}, s32[]{:S(2)}) async-start(s8[16777216]{0:T(1024)(128)(4,1)} %bitcast.543), calls=%async_computation.7 | async-start | bytes 8388608
  311.4 24.1 %slice-start.3 = ((s8[16777216]{0:T(1024)(128)(4,1)}), s8[4194304]{0:T(1024)(128)(4,1)S(1)}, s32[]{:S(2)}) async-start(s8[16777216]{0:T(1024)(128)(4,1)} %bitcast.543), calls=%async_computation.8 | async-start | bytes 8388608
  373.7 23.9 %copy-start.1 = (bf16[4,8,16,1024]{3,1,2,0:T(8,128)(2,1)S(1)}, bf16[4,8,16,1024]{3,1,2,0:T(8,128)(2,1)}, u32[]{:S(2)}) copy-start(bf16[4,8,16,1024]{3,1,2,0:T(8,128)(2,1)} %copy.297) | copy-start | bytes 3145732
Sparse Core Ops, SparseCore 0:
  158.1 70.0 all-reduce.1
Sparse Core Ops, SparseCore 1:
  161.4 49.9 all-gather.5
  228.3 60.8 all-gather.3

commit v2 on v1

--- a/solution.py
+++ b/solution.py
@@ -3,6 +3,8 @@
 import jax
 import jax.numpy as jnp
 from jax import lax
+from jax.experimental import pallas as pl
+from jax.experimental.pallas import tpu as pltpu
 from jax.sharding import PartitionSpec as P
 
 RADII = 128
@@ -10,6 +12,39 @@
 ROT = 64
 STEPS = 4
 ASTEP = 2
+
+
+def _scores_kernel(pt_ref, r_ref, o_ref):
+    classes = r_ref.shape[1]
+    per_dev = o_ref.shape[2]
+    angles = o_ref.shape[3]
+    pt = pt_ref[...]
+
+    def body(k, carry):
+        g = jnp.dot(pt, r_ref[0, k], preferred_element_type=jnp.float32)
+        g = pltpu.roll(g, 0, 1, stride=1, stride_axis=0)
+        o_ref[0, k] = jnp.sum(g.reshape(per_dev, angles, angles), axis=1)
+        return carry
+
+    lax.fori_loop(0, classes, body, 0)
+
+def shift_scores(cube, refs):
+    n, radii, angles = cube.shape
+    steps, classes = refs.shape[:2]
+    rev = jnp.roll(jnp.flip(cube, axis=2), 1, axis=2)
+    pt = rev.transpose(0, 2, 1).reshape(n * angles, radii)
+    flops = 2 * steps * classes * n * angles * radii * angles
+    return pl.pallas_call(
+        _scores_kernel,
+        grid=(steps,),
+        in_specs=[
+            pl.BlockSpec((n * angles, radii), lambda s: (0, 0)),
+            pl.BlockSpec((1, classes, radii, angles), lambda s: (s, 0, 0, 0)),
+        ],
+        out_specs=pl.BlockSpec((1, classes, n, angles), lambda s: (s, 0, 0, 0)),
+        out_shape=jax.ShapeDtypeStruct((steps, classes, n, angles), jnp.float32),
+        cost_estimate=pl.CostEstimate(flops=flops, transcendentals=0, bytes_accessed=pt.size * 2 + refs.size * 2 + steps * classes * n * angles * 4),
+    )(pt, refs)
 
 
 def rotate_each(cube, shifts):
@@ -32,10 +67,7 @@
     me_dom = lax.axis_index("dom")
     me_cls = lax.axis_index("cls")
     cube = particles.reshape(per_dev, RADII, ANGLES)
-    doubled = jnp.concatenate([cube, cube], axis=2)
     scale = 1.0 / math.sqrt(pixels)
-    turns_block = min(ROT, max(8, 512 // per_dev))
-    block_starts = list(range(0, ROT, turns_block))
 
     send_img = []
     send_wts = []
@@ -85,24 +117,9 @@
     final = lax.all_gather(current, "dom", axis=0, tiled=False)
     final = final.transpose(1, 0, 2).reshape(per_group, pixels)
 
-    all_scores = []
-    for step in range(STEPS):
-        refs = all_refs[step]
-        pieces = []
-        for first in block_starts:
-            count = min(turns_block, ROT - first)
-            views = [
-                doubled[:, :, ANGLES - turn * ASTEP : 2 * ANGLES - turn * ASTEP]
-                for turn in range(first, first + count)
-            ]
-            rolled = jnp.stack(views, axis=1).reshape(per_dev * count, pixels)
-            product = lax.dot_general(
-                rolled, refs, (((1,), (1,)), ((), ())), preferred_element_type=jnp.float32
-            )
-            pieces.append(product.reshape(per_dev, count * per_group))
-        stacked = jnp.concatenate(pieces, axis=1)
-        all_scores.append(stacked * scale)
-    return (jnp.stack(all_scores, axis=0), final)
+    shifted = shift_scores(cube, all_refs.reshape(STEPS, per_group, RADII, ANGLES))
+    scores = shifted[..., ::ASTEP].transpose(0, 2, 3, 1).reshape(STEPS, per_dev, ROT * per_group)
+    return (scores * scale, final)
 
 
 def solution(mesh):

time: 471 us -> 415 us (0.88)
  matrix products: 172 us -> 14.8 us
  waiting for transfers between devices: 123 us -> 200 us
  Pallas kernels: 0 us -> 65.5 us
  local copies, waits for them, and re-layouts: 121 us -> 75.4 us
    dot_general x8 -> x0, matrix products: 157 us -> none  [per_device(): lax.dot_general(rolled, refs, (((1,), (1,)), ((), ())), preferred_element...]
    unnamed x90 -> x19, local copies, waits for them, and re-layouts: 72.6 us -> 6.03 us
    pallas_call x0 -> x1, Pallas kernels: none -> 65.5 us  [shift_scores(): pl.pallas_call(_scores_kernel, grid=(steps,), in_specs=[pl.BlockSpec((n *...]
    all_gather x1, waiting for transfers between devices: 10.8 us -> 54.8 us  [per_device(): all_refs = lax.all_gather(ref_chunks, 'dom', axis=0, tiled=False)]
    slice x1 -> x3, local copies, waits for them, and re-layouts: 2.62 us -> 26.2 us  [the longest x1 24.5 us: per_device(): shifted[..., ::ASTEP].transpose(0, 2, 3, 1)]
    psum x1, waiting for transfers between devices: 51.4 us -> 69.4 us  [per_device(): ref_chunks = lax.psum(jnp.stack(ref_chunks, axis=0), 'cls')]
    all_to_all x1, waiting for transfers between devices: 60.6 us -> 75.1 us  [per_device(): got_img = lax.all_to_all(send_img, ('dom', 'cls'), 0, 0, tiled=True)]
    another operation x3 -> x1, local copies, waits for them, and re-layouts: 16.2 us -> 7.28 us  [per_device(): all_refs.reshape(STEPS, per_group, RADII, ANGLES)]
  transfers between devices with their start and end apart: 5 -> 5, of which waited for: 3 -> 3; matrix products, arithmetic and copies ran while one was open for 24% -> 9% of each run, Pallas kernels for 0% -> 0%
where the time goes in v2:
time: 415 us; the launch traced here: 407 us
  waiting for transfers between devices  200 us (48%)
  local copies, waits for them, and re-layouts  75.4 us (18%)
  Pallas kernels  65.5 us (16%)
  starting transfers between devices  22.2 us (5%)
  between operations  18.9 us (5%)
  matrix products  14.8 us (4%)
  other arithmetic  9.88 us (2%)
    all_to_all x1, waiting for transfers between devices, per_device(): got_img = lax.all_to_all(send_img, ('dom', 'cls'), 0, 0, tiled=True)  75.1 us
    psum x1, waiting for transfers between devices, per_device(): ref_chunks = lax.psum(jnp.stack(ref_chunks, axis=0), 'cls')  69.4 us
    pallas_call x1, Pallas kernels, shift_scores(): pl.pallas_call(_scores_kernel, grid=(steps,), in_specs=[pl.BlockSpec((n *...  65.5 us
    all_gather x1, waiting for transfers between devices, per_device(): all_refs = lax.all_gather(ref_chunks, 'dom', axis=0, tiled=False)  54.8 us
    slice x1, local copies, waits for them, and re-layouts, per_device(): shifted[..., ::ASTEP].transpose(0, 2, 3, 1)  24.5 us
    all_to_all x1, starting transfers between devices, per_device(): got_wts = lax.all_to_all(send_wts, ('dom', 'cls'), 0, 0, tiled=True)  11.7 us
    another operation x1, local copies, waits for them, and re-layouts, per_device(): jnp.stack(send_img, axis=2).reshape(doms * groups, STEPS, capacity, chunk)  10.3 us
    all_to_all x1, starting transfers between devices, per_device(): got_img = lax.all_to_all(send_img, ('dom', 'cls'), 0, 0, tiled=True)  10.2 us
  transfers between devices with their start and end apart: 5, of which 3 were waited for; matrix products, arithmetic and copies ran while one was open for 9% of the time, Pallas kernels for 0%

profile of v2, /device:TPU:1, one launch (start us, length us, event | category | flops | bytes accessed | tf_op | source)
XLA Modules:
  0.0 406.6 jit_solution(13778762748805252632)
XLA Ops:
  8.0 0.7 slice_bitcast_fusion.15
  9.1 0.8 slice_bitcast_fusion.14
  10.0 0.8 slice_bitcast_fusion.13
  10.8 0.2 select_reduce_fusion
  11.0 0.2 select_reduce_fusion.2
  11.2 0.7 multiply_add_fusion.3
  11.9 0.2 convolution_convert_fusion.11
  12.3 0.3 convolution_convert_fusion.10
  12.7 0.3 convolution_convert_fusion.9
  13.1 0.3 convolution_convert_fusion.8
  13.6 0.2 maximum_bitcast_fusion
  13.8 0.6 copy.154
  14.4 1.3 reshape.329
  15.7 11.7 %all-to-all-start = ((bf16[128,2,384]{2,1,0:T(2,128)(2,1)}), bf16[128,2,384]{2,1,0:T(2,128)(2,1)S(1)}, u32[]{:S(2)}, u32[]{:S(2)}) async-start(bf16[128,2,384]{2,1,0:T(2,128)(2,1)} %reshape.329), calls=%async_computation | async-start | bytes 393216 | tf_op jit(solution)/shard_map/all_to_all | solution.py:101
  27.6 0.5 fusion.5
  28.1 0.3 copy.104
  28.4 0.6 convolution_convert_fusion
  29.0 0.9 copy.122
  29.8 0.9 copy.150
  30.7 0.5 fusion.4
  31.2 0.3 copy.102
  31.5 0.6 convolution_convert_fusion.1
  32.1 0.9 copy.120
  33.0 2.0 copy.151
  35.1 0.5 fusion.3
  35.5 0.3 copy.100
  35.8 0.6 convolution_convert_fusion.2
  36.4 0.9 copy.118
  37.3 2.0 copy.152
  39.3 0.5 fusion.2
  39.8 0.3 copy.98
  40.1 0.6 convolution_convert_fusion.3
  40.7 0.9 copy.116
  41.6 1.1 copy.153
  42.7 0.3 copy-done
  43.0 0.5 copy-done.1
  43.5 3.2 pad_maximum_fusion
  46.7 10.3 %copy.106 = bf16[128,4,6,1024]{3,1,2,0:T(4,128)(2,1)} copy(bf16[128,4,6,1024]{3,0,2,1:T(8,128)(2,1)} %pad_maximum_fusion) | data formatting | bytes 12582912 | tf_op jit(solution)/shard_map/stack | solution.py:98
  56.9 10.2 %all-to-all-start.1 = ((bf16[128,4,6,1024]{3,1,2,0:T(4,128)(2,1)}), bf16[128,4,6,1024]{3,1,2,0:T(4,128)(2,1)}, u32[]{:S(2)}, u32[]{:S(2)}) async-start(bf16[128,4,6,1024]{3,1,2,0:T(4,128)(2,1)} %copy.106), calls=%async_computation.1 | async-start | bytes 12582912 | tf_op jit(solution)/shard_map/all_to_all | solution.py:100
  67.2 0.6 fusion.85
  70.4 0.4 reshape.330
  70.7 0.8 convert_reduce_fusion
  71.6 75.1 %all-to-all-done.1 = bf16[128,4,6,1024]{3,1,2,0:T(4,128)(2,1)} async-done(((bf16[128,4,6,1024]{3,1,2,0:T(4,128)(2,1)}), bf16[128,4,6,1024]{3,1,2,0:T(4,128)(2,1)}, u32[]{:S(2)}, u32[]{:S(2)}) %all-to-all-start.1) | async-done | bytes 6291488 | tf_op jit(solution)/shard_map/all_to_all | solution.py:100
  146.7 9.7 %fusion.6 = f32[4,32,1024]{2,1,0:T(8,128)S(1)} fusion(bf16[128,4,6,1024]{3,1,2,0:T(4,128)(2,1)} %all-to-all-done.1, bf16[128,4,6,32]{3,1,2,0:T(4,128)(2,1)S(1)} %bitcast.188), kind=kOutput, calls=%fused_computation.20 | convolution fusion | flops 201326592 | bytes 7012352 | tf_op jit(solution)/shard_map/dot_general | solution.py:102
  156.4 1.0 select_bitcast_fusion.3
  157.4 0.1 select_bitcast_fusion.1
  157.5 0.8 select_bitcast_fusion
  158.3 0.7 maximum_bitcast_fusion.2
  159.1 0.5 all-gather.6.cloned.1.call-update
  159.6 0.3 all-gather.4.cloned.1.call-start
  159.9 69.4 %all-reduce.2.cloned.1.call-done = bf16[1,4,32,1024]{3,2,1,0:T(8,128)(2,1)} async-done(((bf16[1,4,32,1024]{3,2,1,0:T(8,128)(2,1)}), bf16[1,4,32,1024]{3,2,1,0:T(8,128)(2,1)}) %all-reduce.2.cloned.1.call-update) | async-done | bytes 262160 | tf_op jit(solution)/shard_map/psum | solution.py:114
  229.3 0.2 slice.132
  229.5 1.5 slice.101
  231.0 0.3 maximum_bitcast_fusion.1
  231.3 1.0 copy.88
  232.3 3.2 copy.113
  235.5 54.8 %all-gather.4.cloned.1.call-done = bf16[16,4,32,1024]{3,2,1,0:T(8,128)(2,1)} async-done(((bf16[1,4,32,1024]{3,2,1,0:T(8,128)(2,1)}), bf16[16,4,32,1024]{3,2,1,0:T(8,128)(2,1)}) %all-gather.4.cloned.1.call-update) | async-done | bytes 4194320 | tf_op jit(solution)/shard_map/all_gather | solution.py:115
  290.3 6.5 %copy.109 = bf16[4,32,16,1024]{3,2,1,0:T(8,128)(2,1)} copy(bf16[4,32,16,1024]{3,1,0,2:T(8,128)(2,1)} %bitcast.201) | data formatting | bytes 8388608 | tf_op jit(solution)/shard_map/transpose | solution.py:116
  296.8 7.3 %reshape_reshape.3.r_ref = bf16[4,32,128,128]{3,2,1,0:T(8,128)(2,1)} reshape(bf16[4,32,16,1024]{3,2,1,0:T(8,128)(2,1)} %copy.109) | data formatting | bytes 8388608 | tf_op jit(solution)/shard_map/reshape;reshape | solution.py:120
  304.1 65.5 %shard_map.95 = f32[4,32,16,128]{3,2,1,0:T(8,128)} custom-call(bf16[2048,128]{1,0:T(8,128)(2,1)} %bitcast.210, bf16[4,32,128,128]{3,2,1,0:T(8,128)(2,1)} %reshape_reshape.3.r_ref), custom_call_target="tpu_custom_call" | custom-call | flops 8589934592 | bytes 5767168 | tf_op jit(solution)/shard_map/pallas_call | solution.py:37
  369.6 24.5 %slice.130 = f32[4,32,16,64]{3,2,1,0:T(8,128)S(1)} slice(f32[4,32,16,128]{3,2,1,0:T(8,128)} %shard_map.95), slice={[0:4:1], [0:32:1], [0:16:1], [0:128:2]} | slice | bytes 1048576 | tf_op jit(solution)/shard_map/slice | solution.py:121
  394.1 1.1 multiply_bitcast_fusion
  395.1 1.8 copy.110
  397.0 1.7 mul.198
  (45 shorter events, 1.4 us)
Async XLA Ops:
  13.6 13.8 %copy-start.5 = (s32[4,16]{1,0:T(4,128)S(1)}, s32[4,16]{1,0:T(4,128)}, u32[]{:S(2)}) copy-start(s32[4,16]{1,0:T(4,128)} %param.13) | copy-start | bytes 772
  13.6 13.8 %copy-start.2 = (bf16[16,16384]{1,0:T(8,128)(2,1)S(1)}, bf16[16,16384]{1,0:T(8,128)(2,1)}, u32[]{:S(2)}) copy-start(bf16[16,16384]{1,0:T(8,128)(2,1)} %param.8) | copy-start | bytes 1572868
  15.7 41.2 %all-to-all-start = ((bf16[128,2,384]{2,1,0:T(2,128)(2,1)}), bf16[128,2,384]{2,1,0:T(2,128)(2,1)S(1)}, u32[]{:S(2)}, u32[]{:S(2)}) async-start(bf16[128,2,384]{2,1,0:T(2,128)(2,1)} %reshape.329), calls=%async_computation | async-start | bytes 393216 | tf_op jit(solution)/shard_map/all_to_all | solution.py:101
  41.6 1.4 copy-start
  41.6 1.9 copy-start.1
  56.9 10.2 %copy-start.3 = (s32[4]{0:T(128)S(1)}, s32[4]{0:T(128)}, u32[]{:S(2)}) copy-start(s32[4]{0:T(128)} %param.15) | copy-start | bytes 52
  56.9 14.6 %copy-start.4 = (f32[32]{0:T(128)S(1)}, f32[32]{0:T(128)}, u32[]{:S(2)}) copy-start(f32[32]{0:T(128)} %param.10) | copy-start | bytes 388
  56.9 89.7 %all-to-all-start.1 = ((bf16[128,4,6,1024]{3,1,2,0:T(4,128)(2,1)}), bf16[128,4,6,1024]{3,1,2,0:T(4,128)(2,1)}, u32[]{:S(2)}, u32[]{:S(2)}) async-start(bf16[128,4,6,1024]{3,1,2,0:T(4,128)(2,1)} %copy.106), calls=%async_computation.1 | async-start | bytes 12582912 | tf_op jit(solution)/shard_map/all_to_all | solution.py:100
  67.1 162.2 %all-reduce.2.cloned.1.call-start = ((), (), s32[]{:S(2)}) async-start(), calls=%async_computation.2 | async-start | bytes 524288 | tf_op jit(solution)/shard_map/psum | solution.py:114
  159.0 73.3 %all-gather.6.cloned.1.call-start = ((), (), s32[]{:S(2)}) async-start(), calls=%async_computation.4 | async-start | bytes 2228224 | tf_op jit(solution)/shard_map/all_gather | solution.py:117
  159.6 130.7 %all-gather.4.cloned.1.call-start = ((), (), s32[]{:S(2)}) async-start(), calls=%async_computation.3 | async-start | bytes 4456448 | tf_op jit(solution)/shard_map/all_gather | solution.py:115
Sparse Core Ops, SparseCore 0:
  159.1 70.0 all-reduce.1
Sparse Core Ops, SparseCore 1:
  162.5 49.9 all-gather.5
  229.4 60.8 all-gather.3

commit v3 on v2

--- a/solution.py
+++ b/solution.py
@@ -14,37 +14,48 @@
 ASTEP = 2
 
 
-def _scores_kernel(pt_ref, r_ref, o_ref):
+def _scores_kernel(pt_ref, sel_ref, r_ref, o_ref):
     classes = r_ref.shape[1]
     per_dev = o_ref.shape[2]
-    angles = o_ref.shape[3]
+    lanes = o_ref.shape[3]
     pt = pt_ref[...]
+    sel = sel_ref[...]
+    rows = pt.shape[0] // per_dev
+    parts = sel.shape[1] // lanes
 
     def body(k, carry):
-        g = jnp.dot(pt, r_ref[0, k], preferred_element_type=jnp.float32)
+        split = jnp.dot(r_ref[0, k], sel, preferred_element_type=jnp.float32).astype(pt.dtype)
+        rhs = jnp.concatenate([split[:, e * lanes:(e + 1) * lanes] for e in range(parts)], axis=0)
+        g = jnp.dot(pt, rhs, preferred_element_type=jnp.float32)
         g = pltpu.roll(g, 0, 1, stride=1, stride_axis=0)
-        o_ref[0, k] = jnp.sum(g.reshape(per_dev, angles, angles), axis=1)
+        o_ref[0, k] = jnp.sum(g.reshape(per_dev, rows, lanes), axis=1)
         return carry
 
     lax.fori_loop(0, classes, body, 0)
 
-def shift_scores(cube, refs):
+def shift_scores(cube, refs, astep):
     n, radii, angles = cube.shape
     steps, classes = refs.shape[:2]
-    rev = jnp.roll(jnp.flip(cube, axis=2), 1, axis=2)
-    pt = rev.transpose(0, 2, 1).reshape(n * angles, radii)
-    flops = 2 * steps * classes * n * angles * radii * angles
+    turns = angles // astep
+    x = cube.reshape(n, radii, turns, astep)
+    x = jnp.roll(jnp.flip(x, axis=2), 1, axis=2)
+    pt = x.transpose(0, 2, 3, 1).reshape(n * turns, astep * radii)
+    b = jnp.arange(angles, dtype=jnp.int32)[:, None]
+    col = jnp.arange(astep * 128, dtype=jnp.int32)[None, :]
+    sel = (b == astep * ((col % 128) % turns) + col // 128).astype(cube.dtype)
+    flops = 2 * steps * classes * (n * turns * radii * astep * 128 + radii * angles * astep * 128)
     return pl.pallas_call(
         _scores_kernel,
         grid=(steps,),
         in_specs=[
-            pl.BlockSpec((n * angles, radii), lambda s: (0, 0)),
+            pl.BlockSpec((n * turns, radii * astep), lambda s: (0, 0)),
+            pl.BlockSpec((angles, astep * 128), lambda s: (0, 0)),
             pl.BlockSpec((1, classes, radii, angles), lambda s: (s, 0, 0, 0)),
         ],
-        out_specs=pl.BlockSpec((1, classes, n, angles), lambda s: (s, 0, 0, 0)),
-        out_shape=jax.ShapeDtypeStruct((steps, classes, n, angles), jnp.float32),
-        cost_estimate=pl.CostEstimate(flops=flops, transcendentals=0, bytes_accessed=pt.size * 2 + refs.size * 2 + steps * classes * n * angles * 4),
-    )(pt, refs)
+        out_specs=pl.BlockSpec((1, classes, n, 128), lambda s: (s, 0, 0, 0)),
+        out_shape=jax.ShapeDtypeStruct((steps, classes, n, 128), jnp.float32),
+        cost_estimate=pl.CostEstimate(flops=flops, transcendentals=0, bytes_accessed=pt.size * 2 + refs.size * 2 + steps * classes * n * 128 * 4),
+    )(pt, sel, refs)[..., :turns]
 
 
 def rotate_each(cube, shifts):
@@ -117,8 +128,8 @@
     final = lax.all_gather(current, "dom", axis=0, tiled=False)
     final = final.transpose(1, 0, 2).reshape(per_group, pixels)
 
-    shifted = shift_scores(cube, all_refs.reshape(STEPS, per_group, RADII, ANGLES))
-    scores = shifted[..., ::ASTEP].transpose(0, 2, 3, 1).reshape(STEPS, per_dev, ROT * per_group)
+    shifted = shift_scores(cube, all_refs.reshape(STEPS, per_group, RADII, ANGLES), ASTEP)
+    scores = shifted.transpose(0, 2, 3, 1).reshape(STEPS, per_dev, ROT * per_group)
     return (scores * scale, final)
 
 

time: 415 us -> 386 us (0.930); the launches traced: 407 us -> 382 us
  waiting for transfers between devices: 200 us -> 176 us
  Pallas kernels: 65.5 us -> 70.3 us
    all_gather x1, waiting for transfers between devices: 54.8 us -> 30.8 us  [per_device(): all_refs = lax.all_gather(ref_chunks, 'dom', axis=0, tiled=False)]
    pallas_call x1, Pallas kernels: 65.5 us -> 70.3 us  [shift_scores(): pl.pallas_call(_scores_kernel, grid=(steps,), in_specs=[pl.BlockSpec((n *...]
    slice x3 -> x5, local copies, waits for them, and re-layouts: 26.2 us -> 21.6 us  [shift_scores(): x = jnp.roll(jnp.flip(x, axis=2), 1, axis=2)]
    unnamed x19 -> x25, local copies, waits for them, and re-layouts: 6.03 us -> 9.94 us
  transfers between devices with their start and end apart: 5 -> 5, of which waited for: 3 -> 3; matrix products, arithmetic and copies ran while one was open for 9% -> 15% of each run, Pallas kernels for 0% -> 0%
where the time goes in v3:
time: 386 us; the launch traced here: 382 us
  waiting for transfers between devices  176 us (46%)
  local copies, waits for them, and re-layouts  71.7 us (19%)
  Pallas kernels  70.3 us (18%)
  starting transfers between devices  22.1 us (6%)
  between operations  18.7 us (5%)
  matrix products  14.8 us (4%)
  other arithmetic  8.37 us (2%)
    all_to_all x1, waiting for transfers between devices, per_device(): got_img = lax.all_to_all(send_img, ('dom', 'cls'), 0, 0, tiled=True)  75.1 us
    pallas_call x1, Pallas kernels, shift_scores(): pl.pallas_call(_scores_kernel, grid=(steps,), in_specs=[pl.BlockSpec((n *...  70.3 us
    psum x1, waiting for transfers between devices, per_device(): ref_chunks = lax.psum(jnp.stack(ref_chunks, axis=0), 'cls')  69.5 us
    all_gather x1, waiting for transfers between devices, per_device(): all_refs = lax.all_gather(ref_chunks, 'dom', axis=0, tiled=False)  30.8 us
    slice x5, local copies, waits for them, and re-layouts, shift_scores(): x = jnp.roll(jnp.flip(x, axis=2), 1, axis=2)  21.6 us
    all_to_all x1, starting transfers between devices, per_device(): got_wts = lax.all_to_all(send_wts, ('dom', 'cls'), 0, 0, tiled=True)  11.7 us
    all_to_all x1, starting transfers between devices, per_device(): got_img = lax.all_to_all(send_img, ('dom', 'cls'), 0, 0, tiled=True)  10.2 us
    unnamed x25, local copies, waits for them, and re-layouts  9.94 us
  transfers between devices with their start and end apart: 5, of which 3 were waited for; matrix products, arithmetic and copies ran while one was open for 15% of the time, Pallas kernels for 0%

profile of v3, /device:TPU:1, one launch (start us, length us, event | category | flops | bytes accessed | tf_op | source)
XLA Modules:
  0.0 381.9 jit_solution(13396961271017312365)
XLA Ops:
  8.0 0.7 slice_bitcast_fusion.15
  9.1 0.8 slice_bitcast_fusion.14
  10.0 0.8 slice_bitcast_fusion.13
  11.2 0.7 multiply_add_fusion.3
  11.9 0.2 convolution_convert_fusion.8
  12.3 0.3 convolution_convert_fusion.9
  12.7 0.3 convolution_convert_fusion.10
  13.1 0.3 convolution_convert_fusion.11
  13.6 0.2 maximum_bitcast_fusion
  13.8 0.6 copy.168
  14.4 1.3 reshape.401
  15.7 11.7 %all-to-all-start = ((bf16[128,2,384]{2,1,0:T(2,128)(2,1)}), bf16[128,2,384]{2,1,0:T(2,128)(2,1)S(1)}, u32[]{:S(2)}, u32[]{:S(2)}) async-start(bf16[128,2,384]{2,1,0:T(2,128)(2,1)} %reshape.401), calls=%async_computation | async-start | bytes 393216 | tf_op jit(solution)/shard_map/all_to_all | solution.py:112
  27.6 0.5 fusion.5
  28.1 0.3 copy.115
  28.4 0.6 convolution_convert_fusion
  29.0 0.9 copy.134
  29.8 2.0 copy.163
  31.9 0.5 fusion.4
  32.4 0.3 copy.113
  32.6 0.6 convolution_convert_fusion.1
  33.2 0.9 copy.132
  34.1 2.0 copy.164
  36.2 0.5 fusion.3
  36.7 0.3 copy.111
  37.0 0.6 convolution_convert_fusion.2
  37.6 0.9 copy.130
  38.4 2.0 copy.165
  40.5 0.5 fusion.2
  41.0 0.3 copy.109
  41.2 0.6 convolution_convert_fusion.3
  41.8 0.9 copy.128
  42.7 1.3 copy.166
  44.2 0.5 copy-done.1
  44.7 0.8 pad_maximum_fusion
  45.5 7.5 %copy.117 = bf16[128,4,6,1024]{3,1,2,0:T(4,128)(2,1)} copy(bf16[128,4,6,1024]{3,0,2,1:T(8,128)(2,1)S(1)} %pad_maximum_fusion) | data formatting | bytes 12582912 | tf_op jit(solution)/shard_map/stack | solution.py:109
  53.1 10.2 %all-to-all-start.1 = ((bf16[128,4,6,1024]{3,1,2,0:T(4,128)(2,1)}), bf16[128,4,6,1024]{3,1,2,0:T(4,128)(2,1)}, u32[]{:S(2)}, u32[]{:S(2)}) async-start(bf16[128,4,6,1024]{3,1,2,0:T(4,128)(2,1)} %copy.117), calls=%async_computation.1 | async-start | bytes 12582912 | tf_op jit(solution)/shard_map/all_to_all | solution.py:111
  63.3 0.7 fusion.92
  66.5 0.4 reshape.402
  66.8 0.8 convert_reduce_fusion
  67.7 75.1 %all-to-all-done.1 = bf16[128,4,6,1024]{3,1,2,0:T(4,128)(2,1)} async-done(((bf16[128,4,6,1024]{3,1,2,0:T(4,128)(2,1)}), bf16[128,4,6,1024]{3,1,2,0:T(4,128)(2,1)}, u32[]{:S(2)}, u32[]{:S(2)}) %all-to-all-start.1) | async-done | bytes 6291488 | tf_op jit(solution)/shard_map/all_to_all | solution.py:111
  142.8 9.7 %fusion.6 = f32[4,32,1024]{2,1,0:T(8,128)S(1)} fusion(bf16[128,4,6,1024]{3,1,2,0:T(4,128)(2,1)} %all-to-all-done.1, bf16[128,4,6,32]{3,1,2,0:T(4,128)(2,1)S(1)} %bitcast.192), kind=kOutput, calls=%fused_computation.20 | convolution fusion | flops 201326592 | bytes 7012352 | tf_op jit(solution)/shard_map/dot_general | solution.py:113
  152.5 1.1 select_bitcast_fusion.3
  153.7 0.8 select_bitcast_fusion
  154.4 0.7 maximum_bitcast_fusion.2
  155.2 0.5 all-gather.6.cloned.1.call-update
  155.8 0.2 all-gather.4.cloned.1.call-start
  156.0 69.5 %all-reduce.2.cloned.1.call-done = bf16[1,4,32,1024]{3,2,1,0:T(8,128)(2,1)} async-done(((bf16[1,4,32,1024]{3,2,1,0:T(8,128)(2,1)}), bf16[1,4,32,1024]{3,2,1,0:T(8,128)(2,1)}) %all-reduce.2.cloned.1.call-update) | async-done | bytes 262160 | tf_op jit(solution)/shard_map/psum | solution.py:125
  225.5 3.1 copy.96
  228.6 6.9 %slice.132 = bf16[16,128,63,2]{0,3,2,1:T(2,128)(2,1)} slice(bf16[16,128,64,2]{0,3,2,1:T(2,128)(2,1)} %bitcast.186), slice={[0:16], [0:128], [1:64], [0:2]} | slice | bytes 1032192 | tf_op jit(solution)/shard_map/jit(_roll_static)/slice | solution.py:41
  235.5 0.9 slice.131
  236.4 6.9 %slice.101 = bf16[16,128,63,2]{0,3,2,1:T(2,128)(2,1)} reverse(bf16[16,128,63,2]{0,3,2,1:T(2,128)(2,1)} %slice.132), dimensions={2} | reverse | bytes 1032192 | tf_op jit(solution)/shard_map/jit(_roll_static)/slice | solution.py:41
  243.4 6.8 %copy.98 = bf16[16,128,63,2]{1,2,3,0:T(8,128)(2,1)S(1)} copy(bf16[16,128,63,2]{0,3,2,1:T(2,128)(2,1)} %slice.101) | data formatting | bytes 1032192 | tf_op jit(solution)/shard_map/jit(_roll_static)/slice | solution.py:41
  250.2 0.2 maximum_bitcast_fusion.1
  250.4 0.5 copy.99
  251.0 0.9 copy.167
  251.8 0.6 fusion.31.sel_ref
  252.5 3.2 copy.124
  255.6 30.8 %all-gather.4.cloned.1.call-done = bf16[16,4,32,1024]{3,2,1,0:T(8,128)(2,1)} async-done(((bf16[1,4,32,1024]{3,2,1,0:T(8,128)(2,1)}), bf16[16,4,32,1024]{3,2,1,0:T(8,128)(2,1)}) %all-gather.4.cloned.1.call-update) | async-done | bytes 4194320 | tf_op jit(solution)/shard_map/all_gather | solution.py:126
  286.5 6.5 %copy.120 = bf16[4,32,16,1024]{3,2,1,0:T(8,128)(2,1)} copy(bf16[4,32,16,1024]{3,1,0,2:T(8,128)(2,1)} %bitcast.205) | data formatting | bytes 8388608 | tf_op jit(solution)/shard_map/transpose | solution.py:127
  293.0 7.3 %reshape_reshape.7.r_ref = bf16[4,32,128,128]{3,2,1,0:T(8,128)(2,1)} reshape(bf16[4,32,16,1024]{3,2,1,0:T(8,128)(2,1)} %copy.120) | data formatting | bytes 8388608 | tf_op jit(solution)/shard_map/reshape;reshape | solution.py:131
  300.3 70.3 %shard_map.95 = f32[4,32,16,128]{3,2,1,0:T(8,128)} custom-call(bf16[1024,256]{1,0:T(8,128)(2,1)} %bitcast.215, bf16[128,256]{1,0:T(8,128)(2,1)} %fusion.31.sel_ref, bf16[4,32,128,128]{3,2,1,0:T(8,128)(2,1)} %reshape_reshape.7.r_ref), custom_call_target="tpu_custom_call" | custom-call | flops 9663676416 | bytes 5767168 | tf_op jit(solution)/shard_map/pallas_call | solution.py:47
  370.5 1.3 fusion.9
  371.9 0.6 copy.121
  372.5 1.8 mul.211
  (55 shorter events, 2.2 us)
Async XLA Ops:
  13.6 13.8 %copy-start.3 = (bf16[16,16384]{1,0:T(8,128)(2,1)S(1)}, bf16[16,16384]{1,0:T(8,128)(2,1)}, u32[]{:S(2)}) copy-start(bf16[16,16384]{1,0:T(8,128)(2,1)} %param.8) | copy-start | bytes 1572868
  13.8 13.7 %copy-start.7 = (s32[4,16]{1,0:T(4,128)S(1)}, s32[4,16]{1,0:T(4,128)}, u32[]{:S(2)}) copy-start(s32[4,16]{1,0:T(4,128)} %param.13) | copy-start | bytes 772
  15.7 37.3 %all-to-all-start = ((bf16[128,2,384]{2,1,0:T(2,128)(2,1)}), bf16[128,2,384]{2,1,0:T(2,128)(2,1)S(1)}, u32[]{:S(2)}, u32[]{:S(2)}) async-start(bf16[128,2,384]{2,1,0:T(2,128)(2,1)} %reshape.401), calls=%async_computation | async-start | bytes 393216 | tf_op jit(solution)/shard_map/all_to_all | solution.py:112
  41.8 2.2 copy-start.2
  42.7 1.5 copy-start
  42.7 2.0 copy-start.1
  53.0 10.2 %copy-start.5 = (s32[4]{0:T(128)S(1)}, s32[4]{0:T(128)}, u32[]{:S(2)}) copy-start(s32[4]{0:T(128)} %param.15) | copy-start | bytes 52
  53.0 14.6 %copy-start.6 = (f32[32]{0:T(128)S(1)}, f32[32]{0:T(128)}, u32[]{:S(2)}) copy-start(f32[32]{0:T(128)} %param.10) | copy-start | bytes 388
  53.1 89.7 %all-to-all-start.1 = ((bf16[128,4,6,1024]{3,1,2,0:T(4,128)(2,1)}), bf16[128,4,6,1024]{3,1,2,0:T(4,128)(2,1)}, u32[]{:S(2)}, u32[]{:S(2)}) async-start(bf16[128,4,6,1024]{3,1,2,0:T(4,128)(2,1)} %copy.117), calls=%async_computation.1 | async-start | bytes 12582912 | tf_op jit(solution)/shard_map/all_to_all | solution.py:111
  63.2 162.2 %all-reduce.2.cloned.1.call-start = ((), (), s32[]{:S(2)}) async-start(), calls=%async_computation.2 | async-start | bytes 524288 | tf_op jit(solution)/shard_map/psum | solution.py:125
  152.5 73.0 %copy-start.4 = (bf16[16,16384]{1,0:T(8,128)(2,1)S(1)}, bf16[16,16384]{1,0:T(8,128)(2,1)}, u32[]{:S(2)}) copy-start(bf16[16,16384]{1,0:T(8,128)(2,1)} %param.8) | copy-start | bytes 1572868
  155.2 97.3 %all-gather.6.cloned.1.call-start = ((), (), s32[]{:S(2)}) async-start(), calls=%async_computation.4 | async-start | bytes 2228224 | tf_op jit(solution)/shard_map/all_gather | solution.py:128
  155.8 130.7 %all-gather.4.cloned.1.call-start = ((), (), s32[]{:S(2)}) async-start(), calls=%async_computation.3 | async-start | bytes 4456448 | tf_op jit(solution)/shard_map/all_gather | solution.py:126
Sparse Core Ops, SparseCore 0:
  155.3 70.0 all-reduce.1
Sparse Core Ops, SparseCore 1:
  158.6 49.9 all-gather.5
  225.6 60.8 all-gather.3

commit v4 on v3

--- a/solution.py
+++ b/solution.py
@@ -119,11 +119,14 @@
     ref_chunks = []
     for step in range(STEPS):
         current = (prior_mass[:, None] * current + totals[step]) / (prior_mass + mass[step])[:, None]
-        piece = current.astype(jnp.bfloat16)
-        piece = jnp.where(me_cls == owners[step], piece, jnp.zeros_like(piece))
-        ref_chunks.append(piece)
-    ref_chunks = lax.psum(jnp.stack(ref_chunks, axis=0), "cls")
-    all_refs = lax.all_gather(ref_chunks, "dom", axis=0, tiled=False)
+        ref_chunks.append(current.astype(jnp.bfloat16))
+    rows = chunk // ANGLES
+    ref_chunks = jnp.stack(ref_chunks, axis=0).reshape(STEPS, per_group, groups, rows // groups * ANGLES)
+    got_refs = lax.all_to_all(ref_chunks.transpose(2, 0, 1, 3), "cls", 0, 0, tiled=True)
+    owner_hot = (owners[None, :] == jnp.arange(groups, dtype=jnp.int32)[:, None]).astype(jnp.bfloat16)
+    mine = jnp.einsum("gs,gskp->skp", owner_hot, got_refs, preferred_element_type=jnp.float32)
+    mine = mine.astype(jnp.bfloat16)
+    all_refs = lax.all_gather(mine, ("dom", "cls"), axis=0, tiled=False)
     all_refs = all_refs.transpose(1, 2, 0, 3).reshape(STEPS, per_group, pixels)
     final = lax.all_gather(current, "dom", axis=0, tiled=False)
     final = final.transpose(1, 0, 2).reshape(per_group, pixels)

time: 386 us -> 602 us (1.56)
  waiting for transfers between devices: 176 us -> 399 us
  local copies, waits for them, and re-layouts: 71.7 us -> 64.3 us
    all_gather x1, waiting for transfers between devices: 30.8 us -> 304 us  [per_device(): all_refs = lax.all_gather(mine, ('dom', 'cls'), axis=0, tiled=False)]
    psum x1 -> x0, waiting for transfers between devices: 69.5 us -> none  [per_device(): ref_chunks = lax.psum(jnp.stack(ref_chunks, axis=0), 'cls')]
    all_gather x1, waiting for transfers between devices: 0.01 us -> 10.9 us  [per_device(): final = lax.all_gather(current, 'dom', axis=0, tiled=False)]
    another operation x1 -> x4, local copies, waits for them, and re-layouts: 7.29 us -> 0.05 us  [per_device(): jnp.stack(ref_chunks, axis=0)]
    all_gather x0 -> x1, local copies, waits for them, and re-layouts: none -> 6.86 us  [per_device(): all_refs = lax.all_gather(mine, ('dom', 'cls'), axis=0, tiled=False)]
    transpose x1 -> x0, local copies, waits for them, and re-layouts: 6.53 us -> none  [per_device(): all_refs = all_refs.transpose(1, 2, 0, 3).reshape(STEPS, per_group, pixels)]
  transfers between devices with their start and end apart: 5 -> 5, of which waited for: 3 -> 4; matrix products, arithmetic and copies ran while one was open for 15% -> 10% of each run, Pallas kernels for 0% -> 0%
where the time goes in v4:
time: 602 us; the launch traced here: 598 us
  waiting for transfers between devices  399 us (66%)
  Pallas kernels  70.2 us (12%)
  local copies, waits for them, and re-layouts  64.3 us (11%)
  starting transfers between devices  26 us (4%)
  matrix products  15.1 us (3%)
  between operations  14.8 us (2%)
  other arithmetic  9 us (1%)
    all_gather x1, waiting for transfers between devices, per_device(): all_refs = lax.all_gather(mine, ('dom', 'cls'), axis=0, tiled=False)  304 us
    all_to_all x1, waiting for transfers between devices, per_device(): got_img = lax.all_to_all(send_img, ('dom', 'cls'), 0, 0, tiled=True)  78.3 us
    pallas_call x1, Pallas kernels, shift_scores(): pl.pallas_call(_scores_kernel, grid=(steps,), in_specs=[pl.BlockSpec((n *...  70.2 us
    slice x5, local copies, waits for them, and re-layouts, shift_scores(): x = jnp.roll(jnp.flip(x, axis=2), 1, axis=2)  21.6 us
  transfers between devices with their start and end apart: 5, of which 4 were waited for; matrix products, arithmetic and copies ran while one was open for 10% of the time, Pallas kernels for 0%

profile of v4, /device:TPU:1, one launch (start us, length us, event | category | flops | bytes accessed | tf_op | source)
XLA Modules:
  0.0 598.2 jit_solution(18282229904379002752)
XLA Ops:
  7.2 0.7 slice_bitcast_fusion.15
  8.3 0.8 slice_bitcast_fusion.14
  9.1 0.8 slice_bitcast_fusion.13
  10.3 0.7 multiply_add_fusion.3
  11.1 0.2 convolution_convert_fusion.8
  11.4 0.3 convolution_convert_fusion.9
  11.8 0.3 convolution_convert_fusion.10
  12.2 0.3 convolution_convert_fusion.11
  12.8 0.2 maximum_bitcast_fusion
  13.0 0.6 copy.190
  13.6 1.3 reshape.414
  14.9 11.7 %all-to-all-start = ((bf16[128,2,384]{2,1,0:T(2,128)(2,1)}), bf16[128,2,384]{2,1,0:T(2,128)(2,1)S(1)}, u32[]{:S(2)}, u32[]{:S(2)}) async-start(bf16[128,2,384]{2,1,0:T(2,128)(2,1)} %reshape.414), calls=%async_computation | async-start | bytes 393216 | tf_op jit(solution)/shard_map/all_to_all | solution.py:112
  26.8 0.5 fusion.5
  27.3 0.3 copy.122
  27.6 0.6 convolution_convert_fusion
  28.1 0.9 copy.148
  29.0 2.0 copy.185
  31.0 0.5 fusion.4
  31.5 0.3 copy.120
  31.8 0.6 convolution_convert_fusion.1
  32.4 0.9 copy.146
  33.3 2.0 copy.186
  35.4 0.5 fusion.3
  35.9 0.3 copy.118
  36.1 0.6 convolution_convert_fusion.2
  36.7 0.9 copy.144
  37.6 2.0 copy.187
  39.6 0.5 fusion.2
  40.1 0.3 copy.116
  40.4 0.6 convolution_convert_fusion.3
  41.0 0.9 copy.142
  41.9 1.3 copy.188
  43.4 0.5 copy-done.1
  43.9 0.8 pad_maximum_fusion
  44.7 7.5 %copy.124 = bf16[128,4,6,1024]{3,1,2,0:T(4,128)(2,1)} copy(bf16[128,4,6,1024]{3,0,2,1:T(8,128)(2,1)S(1)} %pad_maximum_fusion) | data formatting | bytes 12582912 | tf_op jit(solution)/shard_map/stack | solution.py:109
  52.2 10.2 %all-to-all-start.1 = ((bf16[128,4,6,1024]{3,1,2,0:T(4,128)(2,1)}), bf16[128,4,6,1024]{3,1,2,0:T(4,128)(2,1)}, u32[]{:S(2)}, u32[]{:S(2)}) async-start(bf16[128,4,6,1024]{3,1,2,0:T(4,128)(2,1)} %copy.124), calls=%async_computation.1 | async-start | bytes 12582912 | tf_op jit(solution)/shard_map/all_to_all | solution.py:111
  62.4 0.4 reshape.415
  62.8 0.8 convert_reduce_fusion
  63.7 78.3 %all-to-all-done.1 = bf16[128,4,6,1024]{3,1,2,0:T(4,128)(2,1)} async-done(((bf16[128,4,6,1024]{3,1,2,0:T(4,128)(2,1)}), bf16[128,4,6,1024]{3,1,2,0:T(4,128)(2,1)}, u32[]{:S(2)}, u32[]{:S(2)}) %all-to-all-start.1) | async-done | bytes 6291488 | tf_op jit(solution)/shard_map/all_to_all | solution.py:111
  142.0 9.7 %fusion.6 = f32[4,32,1024]{2,1,0:T(8,128)S(1)} fusion(bf16[128,4,6,1024]{3,1,2,0:T(4,128)(2,1)} %all-to-all-done.1, bf16[128,4,6,32]{3,1,2,0:T(4,128)(2,1)S(1)} %bitcast.202), kind=kOutput, calls=%fused_computation.21 | convolution fusion | flops 201326592 | bytes 7012352 | tf_op jit(solution)/shard_map/dot_general | solution.py:113
  151.7 1.1 convert_bitcast_fusion.3
  152.9 0.8 convert_bitcast_fusion
  153.8 0.7 maximum_bitcast_fusion.2
  154.5 3.9 all-to-all-start.2
  158.4 0.2 all-gather.5.cloned.1.call-start
  158.8 5.9 all-to-all-done.2
  164.7 0.3 fusion.23
  165.0 0.6 convert_element_type.120
  165.6 3.1 copy.103
  168.7 6.9 %slice.116 = bf16[16,128,63,2]{0,3,2,1:T(2,128)(2,1)} slice(bf16[16,128,64,2]{0,3,2,1:T(2,128)(2,1)} %bitcast.196), slice={[0:16], [0:128], [1:64], [0:2]} | slice | bytes 1032192 | tf_op jit(solution)/shard_map/jit(_roll_static)/slice | solution.py:41
  175.7 0.9 slice.115
  176.6 7.0 %slice.89 = bf16[16,128,63,2]{0,3,2,1:T(2,128)(2,1)} reverse(bf16[16,128,63,2]{0,3,2,1:T(2,128)(2,1)} %slice.116), dimensions={2} | reverse | bytes 1032192 | tf_op jit(solution)/shard_map/jit(_roll_static)/slice | solution.py:41
  183.5 6.8 %copy.105 = bf16[16,128,63,2]{1,2,3,0:T(8,128)(2,1)S(1)} copy(bf16[16,128,63,2]{0,3,2,1:T(2,128)(2,1)} %slice.89) | data formatting | bytes 1032192 | tf_op jit(solution)/shard_map/jit(_roll_static)/slice | solution.py:41
  190.6 0.5 copy.106
  191.1 0.9 copy.189
  192.0 0.7 fusion.33.sel_ref
  192.7 10.9 %all-gather.7.cloned.1.call-done = f32[512,1024]{1,0:T(8,128)} async-done(((f32[32,1024]{1,0:T(8,128)}), f32[512,1024]{1,0:T(8,128)}) %all-gather.7.cloned.1.call-update) | async-done | bytes 2097168 | tf_op jit(solution)/shard_map/all_gather | solution.py:131
  203.5 3.2 copy.138
  206.7 303.7 %all-gather.5.cloned.1.call-done = bf16[512,32,128]{2,1,0:T(8,128)(2,1)} async-done(((bf16[4,32,128]{2,1,0:T(8,128)(2,1)}), bf16[512,32,128]{2,1,0:T(8,128)(2,1)}) %all-gather.5.cloned.1.call-update) | async-done | bytes 4194320 | tf_op jit(solution)/shard_map/all_gather | solution.py:129
  510.4 6.9 %copy.184 = bf16[128,4,32,128]{3,0,2,1:T(8,128)(2,1)} copy(bf16[128,4,32,128]{3,2,1,0:T(8,128)(2,1)} %bitcast.215) | data formatting | bytes 8388608 | tf_op jit(solution)/shard_map/all_gather | solution.py:129
  517.2 70.2 %shard_map.95 = f32[4,32,16,128]{3,2,1,0:T(8,128)} custom-call(bf16[1024,256]{1,0:T(8,128)(2,1)} %bitcast.226, bf16[128,256]{1,0:T(8,128)(2,1)} %fusion.33.sel_ref, bf16[4,32,128,128]{3,2,1,0:T(8,128)(2,1)} %bitcast.216), custom_call_target="tpu_custom_call" | custom-call | flops 9663676416 | bytes 5767168 | tf_op jit(solution)/shard_map/pallas_call | solution.py:47
  587.5 1.3 fusion.9
  588.8 0.6 copy.132
  589.4 1.8 mul.211
  (64 shorter events, 2.6 us)
Async XLA Ops:
  12.7 13.8 %copy-start.3 = (bf16[16,16384]{1,0:T(8,128)(2,1)S(1)}, bf16[16,16384]{1,0:T(8,128)(2,1)}, u32[]{:S(2)}) copy-start(bf16[16,16384]{1,0:T(8,128)(2,1)} %param.8) | copy-start | bytes 1572868
  13.0 13.7 %copy-start.6 = (s32[4,16]{1,0:T(4,128)S(1)}, s32[4,16]{1,0:T(4,128)}, u32[]{:S(2)}) copy-start(s32[4,16]{1,0:T(4,128)} %param.13) | copy-start | bytes 772
  14.9 37.3 %all-to-all-start = ((bf16[128,2,384]{2,1,0:T(2,128)(2,1)}), bf16[128,2,384]{2,1,0:T(2,128)(2,1)S(1)}, u32[]{:S(2)}, u32[]{:S(2)}) async-start(bf16[128,2,384]{2,1,0:T(2,128)(2,1)} %reshape.414), calls=%async_computation | async-start | bytes 393216 | tf_op jit(solution)/shard_map/all_to_all | solution.py:112
  41.0 2.2 copy-start.2
  41.9 1.5 copy-start
  41.9 2.0 copy-start.1
  52.2 11.4 %copy-start.5 = (f32[32]{0:T(128)S(1)}, f32[32]{0:T(128)}, u32[]{:S(2)}) copy-start(f32[32]{0:T(128)} %param.10) | copy-start | bytes 388
  52.2 89.8 %all-to-all-start.1 = ((bf16[128,4,6,1024]{3,1,2,0:T(4,128)(2,1)}), bf16[128,4,6,1024]{3,1,2,0:T(4,128)(2,1)}, u32[]{:S(2)}, u32[]{:S(2)}) async-start(bf16[128,4,6,1024]{3,1,2,0:T(4,128)(2,1)} %copy.124), calls=%async_computation.1 | async-start | bytes 12582912 | tf_op jit(solution)/shard_map/all_to_all | solution.py:111
  62.4 141.2 %all-gather.7.cloned.1.call-start = ((), (), s32[]{:S(2)}) async-start(), calls=%async_computation.4 | async-start | bytes 2228224 | tf_op jit(solution)/shard_map/all_gather | solution.py:131
  151.6 7.0 %copy-start.7 = (s32[4]{0:T(128)S(1)}, s32[4]{0:T(128)}, u32[]{:S(2)}) copy-start(s32[4]{0:T(128)} %param.15) | copy-start | bytes 52
  151.7 14.0 %copy-start.4 = (bf16[16,16384]{1,0:T(8,128)(2,1)S(1)}, bf16[16,16384]{1,0:T(8,128)(2,1)}, u32[]{:S(2)}) copy-start(bf16[16,16384]{1,0:T(8,128)(2,1)} %param.8) | copy-start | bytes 1572868
  154.5 10.2 %all-to-all-start.2 = ((bf16[8,4,32,128]{3,2,1,0:T(8,128)(2,1)}), bf16[8,4,32,128]{3,2,1,0:T(8,128)(2,1)S(1)}, u32[]{:S(2)}, u32[]{:S(2)}) async-start(bf16[8,4,32,128]{3,2,1,0:T(8,128)(2,1)} %maximum_bitcast_fusion.2), calls=%async_computation.2 | async-start | bytes 524288 | tf_op jit(solution)/shard_map/all_to_all | solution.py:125
  158.4 351.9 %all-gather.5.cloned.1.call-start = ((), (), s32[]{:S(2)}) async-start(), calls=%async_computation.3 | async-start | bytes 4227072 | tf_op jit(solution)/shard_map/all_gather | solution.py:129
Sparse Core Ops, SparseCore 0:
  153.8 49.7 all-gather.6
  205.2 305.0 all-gather.4

commit v5 on v4

--- a/solution.py
+++ b/solution.py
@@ -126,8 +126,9 @@
     owner_hot = (owners[None, :] == jnp.arange(groups, dtype=jnp.int32)[:, None]).astype(jnp.bfloat16)
     mine = jnp.einsum("gs,gskp->skp", owner_hot, got_refs, preferred_element_type=jnp.float32)
     mine = mine.astype(jnp.bfloat16)
-    all_refs = lax.all_gather(mine, ("dom", "cls"), axis=0, tiled=False)
-    all_refs = all_refs.transpose(1, 2, 0, 3).reshape(STEPS, per_group, pixels)
+    owner_chunk = lax.all_gather(mine, "cls", axis=0, tiled=False)
+    all_refs = lax.all_gather(owner_chunk, "dom", axis=0, tiled=False)
+    all_refs = all_refs.transpose(2, 3, 0, 1, 4).reshape(STEPS, per_group, pixels)
     final = lax.all_gather(current, "dom", axis=0, tiled=False)
     final = final.transpose(1, 0, 2).reshape(per_group, pixels)
 

time: 602 us -> 352 us (0.58)
  waiting for transfers between devices: 399 us -> 125 us
  blocking collectives: 0 us -> 25.2 us
    all_gather x1, waiting for transfers between devices: 304 us -> 40.2 us  [per_device(): all_refs = lax.all_gather(owner_chunk, 'dom', axis=0, tiled=False)]
    all_gather x0 -> x1, blocking collectives: none -> 25.2 us  [per_device(): owner_chunk = lax.all_gather(mine, 'cls', axis=0, tiled=False)]
    all_gather x1, waiting for transfers between devices: 10.9 us -> 0.01 us  [per_device(): final = lax.all_gather(current, 'dom', axis=0, tiled=False)]
  transfers between devices with their start and end apart: 5 -> 5, of which waited for: 4 -> 3; matrix products, arithmetic and copies ran while one was open for 10% -> 16% of each run, Pallas kernels for 0% -> 0%
where the time goes in v5:
time: 352 us; the launch traced here: 349 us
  waiting for transfers between devices  125 us (36%)
  Pallas kernels  70.5 us (20%)
  local copies, waits for them, and re-layouts  64.3 us (18%)
  starting transfers between devices  25.8 us (7%)
  blocking collectives  25.2 us (7%)
  matrix products  15.1 us (4%)
  between operations  14.8 us (4%)
  other arithmetic  8.34 us (2%)
    all_to_all x1, waiting for transfers between devices, per_device(): got_img = lax.all_to_all(send_img, ('dom', 'cls'), 0, 0, tiled=True)  78.3 us
    pallas_call x1, Pallas kernels, shift_scores(): pl.pallas_call(_scores_kernel, grid=(steps,), in_specs=[pl.BlockSpec((n *...  70.5 us
    all_gather x1, waiting for transfers between devices, per_device(): all_refs = lax.all_gather(owner_chunk, 'dom', axis=0, tiled=False)  40.2 us
    all_gather x1, blocking collectives, per_device(): owner_chunk = lax.all_gather(mine, 'cls', axis=0, tiled=False)  25.2 us
    slice x5, local copies, waits for them, and re-layouts, shift_scores(): x = jnp.roll(jnp.flip(x, axis=2), 1, axis=2)  21.6 us
    all_to_all x1, starting transfers between devices, per_device(): got_wts = lax.all_to_all(send_wts, ('dom', 'cls'), 0, 0, tiled=True)  11.7 us
    all_to_all x1, starting transfers between devices, per_device(): got_img = lax.all_to_all(send_img, ('dom', 'cls'), 0, 0, tiled=True)  10.2 us
    unnamed x29, local copies, waits for them, and re-layouts  9.99 us
  transfers between devices with their start and end apart: 5, of which 3 were waited for; matrix products, arithmetic and copies ran while one was open for 16% of the time, Pallas kernels for 0%

profile of v5, /device:TPU:1, one launch (start us, length us, event | category | flops | bytes accessed | tf_op | source)
XLA Modules:
  0.0 348.7 jit_solution(16917208861539538892)
XLA Ops:
  7.2 0.7 slice_bitcast_fusion.15
  8.3 0.8 slice_bitcast_fusion.14
  9.1 0.8 slice_bitcast_fusion.13
  10.3 0.7 multiply_add_fusion.3
  11.1 0.2 convolution_convert_fusion.8
  11.4 0.3 convolution_convert_fusion.9
  11.8 0.3 convolution_convert_fusion.10
  12.2 0.3 convolution_convert_fusion.11
  12.8 0.2 maximum_bitcast_fusion
  13.0 0.6 copy.190
  13.6 1.3 reshape.415
  14.9 11.7 %all-to-all-start = ((bf16[128,2,384]{2,1,0:T(2,128)(2,1)}), bf16[128,2,384]{2,1,0:T(2,128)(2,1)S(1)}, u32[]{:S(2)}, u32[]{:S(2)}) async-start(bf16[128,2,384]{2,1,0:T(2,128)(2,1)} %reshape.415), calls=%async_computation | async-start | bytes 393216 | tf_op jit(solution)/shard_map/all_to_all | solution.py:112
  26.8 0.5 fusion.5
  27.3 0.3 copy.122
  27.6 0.6 convolution_convert_fusion
  28.1 0.9 copy.148
  29.0 2.0 copy.185
  31.0 0.5 fusion.4
  31.5 0.3 copy.120
  31.8 0.6 convolution_convert_fusion.1
  32.4 0.9 copy.146
  33.3 2.0 copy.186
  35.4 0.5 fusion.3
  35.9 0.3 copy.118
  36.1 0.6 convolution_convert_fusion.2
  36.7 0.9 copy.144
  37.6 2.0 copy.187
  39.6 0.5 fusion.2
  40.1 0.3 copy.116
  40.4 0.6 convolution_convert_fusion.3
  41.0 0.9 copy.142
  41.9 1.3 copy.188
  43.2 0.2 copy-done
  43.4 0.5 copy-done.1
  43.9 0.8 pad_maximum_fusion
  44.7 7.5 %copy.124 = bf16[128,4,6,1024]{3,1,2,0:T(4,128)(2,1)} copy(bf16[128,4,6,1024]{3,0,2,1:T(8,128)(2,1)S(1)} %pad_maximum_fusion) | data formatting | bytes 12582912 | tf_op jit(solution)/shard_map/stack | solution.py:109
  52.2 10.2 %all-to-all-start.1 = ((bf16[128,4,6,1024]{3,1,2,0:T(4,128)(2,1)}), bf16[128,4,6,1024]{3,1,2,0:T(4,128)(2,1)}, u32[]{:S(2)}, u32[]{:S(2)}) async-start(bf16[128,4,6,1024]{3,1,2,0:T(4,128)(2,1)} %copy.124), calls=%async_computation.1 | async-start | bytes 12582912 | tf_op jit(solution)/shard_map/all_to_all | solution.py:111
  62.4 0.4 reshape.416
  62.8 0.8 convert_reduce_fusion
  63.7 78.3 %all-to-all-done.1 = bf16[128,4,6,1024]{3,1,2,0:T(4,128)(2,1)} async-done(((bf16[128,4,6,1024]{3,1,2,0:T(4,128)(2,1)}), bf16[128,4,6,1024]{3,1,2,0:T(4,128)(2,1)}, u32[]{:S(2)}, u32[]{:S(2)}) %all-to-all-start.1) | async-done | bytes 6291488 | tf_op jit(solution)/shard_map/all_to_all | solution.py:111
  142.0 9.7 %fusion.6 = f32[4,32,1024]{2,1,0:T(8,128)S(1)} fusion(bf16[128,4,6,1024]{3,1,2,0:T(4,128)(2,1)} %all-to-all-done.1, bf16[128,4,6,32]{3,1,2,0:T(4,128)(2,1)S(1)} %bitcast.205), kind=kOutput, calls=%fused_computation.21 | convolution fusion | flops 201326592 | bytes 7012352 | tf_op jit(solution)/shard_map/dot_general | solution.py:113
  151.7 1.0 convert_bitcast_fusion.3
  152.8 0.8 convert_bitcast_fusion
  153.7 0.7 maximum_bitcast_fusion.2
  154.5 3.9 %all-to-all-start.2 = ((bf16[8,4,32,128]{3,2,1,0:T(8,128)(2,1)}), bf16[8,4,32,128]{3,2,1,0:T(8,128)(2,1)S(1)}, u32[]{:S(2)}, u32[]{:S(2)}) async-start(bf16[8,4,32,128]{3,2,1,0:T(8,128)(2,1)} %maximum_bitcast_fusion.2), calls=%async_computation.2 | async-start | bytes 524288 | tf_op jit(solution)/shard_map/all_to_all | solution.py:125
  158.6 6.1 %all-to-all-done.2 = bf16[8,4,32,128]{3,2,1,0:T(8,128)(2,1)S(1)} async-done(((bf16[8,4,32,128]{3,2,1,0:T(8,128)(2,1)}), bf16[8,4,32,128]{3,2,1,0:T(8,128)(2,1)S(1)}, u32[]{:S(2)}, u32[]{:S(2)}) %all-to-all-start.2) | async-done | bytes 262176 | tf_op jit(solution)/shard_map/all_to_all | solution.py:125
  164.7 0.3 fusion.23
  165.0 25.2 %all-gather = bf16[32,32,128]{2,1,0:T(8,128)(2,1)} all-gather(bf16[4,32,128]{2,1,0:T(8,128)(2,1)S(1)} %convert_element_type.120), channel_id=2, replica_groups=mesh['dom'=16,'cls'=8] {'cls'}, dimensions={0}, use_global_device_ids=true | all-gather | bytes 294912 | tf_op jit(solution)/shard_map/all_gather | solution.py:129
  190.2 3.1 copy.103
  193.3 6.9 %slice.116 = bf16[16,128,63,2]{0,3,2,1:T(2,128)(2,1)} slice(bf16[16,128,64,2]{0,3,2,1:T(2,128)(2,1)} %bitcast.199), slice={[0:16], [0:128], [1:64], [0:2]} | slice | bytes 1032192 | tf_op jit(solution)/shard_map/jit(_roll_static)/slice | solution.py:41
  200.3 0.9 slice.115
  201.2 7.0 %slice.89 = bf16[16,128,63,2]{0,3,2,1:T(2,128)(2,1)} reverse(bf16[16,128,63,2]{0,3,2,1:T(2,128)(2,1)} %slice.116), dimensions={2} | reverse | bytes 1032192 | tf_op jit(solution)/shard_map/jit(_roll_static)/slice | solution.py:41
  208.1 6.8 %copy.105 = bf16[16,128,63,2]{1,2,3,0:T(8,128)(2,1)S(1)} copy(bf16[16,128,63,2]{0,3,2,1:T(2,128)(2,1)} %slice.89) | data formatting | bytes 1032192 | tf_op jit(solution)/shard_map/jit(_roll_static)/slice | solution.py:41
  215.0 0.2 maximum_bitcast_fusion.1
  215.2 0.5 copy.106
  215.7 0.9 copy.189
  216.6 0.7 fusion.33.sel_ref
  217.3 3.2 copy.138
  220.4 40.2 %all-gather.6.cloned.1.call-done = bf16[128,4,32,128]{3,2,1,0:T(8,128)(2,1)} async-done(((bf16[8,4,32,128]{3,2,1,0:T(8,128)(2,1)}), bf16[128,4,32,128]{3,2,1,0:T(8,128)(2,1)}) %all-gather.6.cloned.1.call-update) | async-done | bytes 4194320 | tf_op jit(solution)/shard_map/all_gather | solution.py:130
  260.6 6.9 %copy.184 = bf16[16,8,4,32,128]{4,1,0,3,2:T(8,128)(2,1)} copy(bf16[16,8,4,32,128]{4,3,2,1,0:T(8,128)(2,1)} %bitcast.218) | data formatting | bytes 8388608 | tf_op jit(solution)/shard_map/all_gather | solution.py:130
  267.5 70.5 %shard_map.95 = f32[4,32,16,128]{3,2,1,0:T(8,128)} custom-call(bf16[1024,256]{1,0:T(8,128)(2,1)} %bitcast.230, bf16[128,256]{1,0:T(8,128)(2,1)} %fusion.33.sel_ref, bf16[4,32,128,128]{3,2,1,0:T(8,128)(2,1)} %bitcast.219), custom_call_target="tpu_custom_call" | custom-call | flops 9663676416 | bytes 5767168 | tf_op jit(solution)/shard_map/pallas_call | solution.py:47
  338.0 1.3 fusion.9
  339.3 0.6 copy.132
  340.0 1.8 mul.211
  (65 shorter events, 2.2 us)
Async XLA Ops:
  12.7 13.8 %copy-start.3 = (bf16[16,16384]{1,0:T(8,128)(2,1)S(1)}, bf16[16,16384]{1,0:T(8,128)(2,1)}, u32[]{:S(2)}) copy-start(bf16[16,16384]{1,0:T(8,128)(2,1)} %param.8) | copy-start | bytes 1572868
  13.0 13.7 %copy-start.6 = (s32[4,16]{1,0:T(4,128)S(1)}, s32[4,16]{1,0:T(4,128)}, u32[]{:S(2)}) copy-start(s32[4,16]{1,0:T(4,128)} %param.13) | copy-start | bytes 772
  14.9 37.3 %all-to-all-start = ((bf16[128,2,384]{2,1,0:T(2,128)(2,1)}), bf16[128,2,384]{2,1,0:T(2,128)(2,1)S(1)}, u32[]{:S(2)}, u32[]{:S(2)}) async-start(bf16[128,2,384]{2,1,0:T(2,128)(2,1)} %reshape.415), calls=%async_computation | async-start | bytes 393216 | tf_op jit(solution)/shard_map/all_to_all | solution.py:112
  41.0 2.2 copy-start.2
  41.9 1.5 copy-start
  41.9 2.0 copy-start.1
  52.2 11.4 %copy-start.5 = (f32[32]{0:T(128)S(1)}, f32[32]{0:T(128)}, u32[]{:S(2)}) copy-start(f32[32]{0:T(128)} %param.10) | copy-start | bytes 388
  52.2 89.8 %all-to-all-start.1 = ((bf16[128,4,6,1024]{3,1,2,0:T(4,128)(2,1)}), bf16[128,4,6,1024]{3,1,2,0:T(4,128)(2,1)}, u32[]{:S(2)}, u32[]{:S(2)}) async-start(bf16[128,4,6,1024]{3,1,2,0:T(4,128)(2,1)} %copy.124), calls=%async_computation.1 | async-start | bytes 12582912 | tf_op jit(solution)/shard_map/all_to_all | solution.py:111
  62.4 154.9 %all-gather.8.cloned.1.call-start = ((), (), s32[]{:S(2)}) async-start(), calls=%async_computation.4 | async-start | bytes 2228224 | tf_op jit(solution)/shard_map/all_gather | solution.py:132
  151.6 6.8 %copy-start.7 = (s32[4]{0:T(128)S(1)}, s32[4]{0:T(128)}, u32[]{:S(2)}) copy-start(s32[4]{0:T(128)} %param.15) | copy-start | bytes 52
  152.7 37.5 %copy-start.4 = (bf16[16,16384]{1,0:T(8,128)(2,1)S(1)}, bf16[16,16384]{1,0:T(8,128)(2,1)}, u32[]{:S(2)}) copy-start(bf16[16,16384]{1,0:T(8,128)(2,1)} %param.8) | copy-start | bytes 1572868
  154.5 10.2 %all-to-all-start.2 = ((bf16[8,4,32,128]{3,2,1,0:T(8,128)(2,1)}), bf16[8,4,32,128]{3,2,1,0:T(8,128)(2,1)S(1)}, u32[]{:S(2)}, u32[]{:S(2)}) async-start(bf16[8,4,32,128]{3,2,1,0:T(8,128)(2,1)} %maximum_bitcast_fusion.2), calls=%async_computation.2 | async-start | bytes 524288 | tf_op jit(solution)/shard_map/all_to_all | solution.py:125
  158.4 102.3 %all-gather.6.cloned.1.call-start = ((), (), s32[]{:S(2)}) async-start(), calls=%async_computation.3 | async-start | bytes 4456448 | tf_op jit(solution)/shard_map/all_gather | solution.py:130
Sparse Core Ops, SparseCore 0:
  153.7 49.9 all-gather.7
  206.1 54.5 all-gather.5

commit v6 on v4

--- a/solution.py
+++ b/solution.py
@@ -18,10 +18,10 @@
     classes = r_ref.shape[1]
     per_dev = o_ref.shape[2]
     lanes = o_ref.shape[3]
-    pt = pt_ref[...]
+    parts = pt_ref.shape[0]
+    pt = jnp.concatenate([pt_ref[e] for e in range(parts)], axis=1)
     sel = sel_ref[...]
     rows = pt.shape[0] // per_dev
-    parts = sel.shape[1] // lanes
 
     def body(k, carry):
         split = jnp.dot(r_ref[0, k], sel, preferred_element_type=jnp.float32).astype(pt.dtype)
@@ -33,13 +33,17 @@
 
     lax.fori_loop(0, classes, body, 0)
 
+
 def shift_scores(cube, refs, astep):
     n, radii, angles = cube.shape
     steps, classes = refs.shape[:2]
     turns = angles // astep
-    x = cube.reshape(n, radii, turns, astep)
-    x = jnp.roll(jnp.flip(x, axis=2), 1, axis=2)
-    pt = x.transpose(0, 2, 3, 1).reshape(n * turns, astep * radii)
+    b = jnp.arange(angles, dtype=jnp.int32)[None, None, :]
+    e = jnp.arange(astep, dtype=jnp.int32)[:, None, None]
+    m = jnp.arange(turns, dtype=jnp.int32)[None, :, None]
+    pick = (b == astep * ((turns - m) % turns) + e).astype(cube.dtype)
+    pt = jnp.einsum("emb,iab->eima", pick, cube, preferred_element_type=jnp.float32)
+    pt = pt.astype(cube.dtype).reshape(astep, n * turns, radii)
     b = jnp.arange(angles, dtype=jnp.int32)[:, None]
     col = jnp.arange(astep * 128, dtype=jnp.int32)[None, :]
     sel = (b == astep * ((col % 128) % turns) + col // 128).astype(cube.dtype)
@@ -48,7 +52,7 @@
         _scores_kernel,
         grid=(steps,),
         in_specs=[
-            pl.BlockSpec((n * turns, radii * astep), lambda s: (0, 0)),
+            pl.BlockSpec((astep, n * turns, radii), lambda s: (0, 0, 0)),
             pl.BlockSpec((angles, astep * 128), lambda s: (0, 0)),
             pl.BlockSpec((1, classes, radii, angles), lambda s: (s, 0, 0, 0)),
         ],
@@ -126,8 +130,9 @@
     owner_hot = (owners[None, :] == jnp.arange(groups, dtype=jnp.int32)[:, None]).astype(jnp.bfloat16)
     mine = jnp.einsum("gs,gskp->skp", owner_hot, got_refs, preferred_element_type=jnp.float32)
     mine = mine.astype(jnp.bfloat16)
-    all_refs = lax.all_gather(mine, ("dom", "cls"), axis=0, tiled=False)
-    all_refs = all_refs.transpose(1, 2, 0, 3).reshape(STEPS, per_group, pixels)
+    owner_chunk = lax.all_gather(mine, "cls", axis=2, tiled=False)
+    all_refs = lax.all_gather(owner_chunk, "dom", axis=2, tiled=False)
+    all_refs = all_refs.reshape(STEPS, per_group, pixels)
     final = lax.all_gather(current, "dom", axis=0, tiled=False)
     final = final.transpose(1, 0, 2).reshape(per_group, pixels)
 

time: 602 us -> 344 us (0.57)
  waiting for transfers between devices: 399 us -> 157 us
  local copies, waits for them, and re-layouts: 64.3 us -> 32 us
  blocking collectives: 0 us -> 20.7 us
    all_gather x1, waiting for transfers between devices: 304 us -> 56.6 us  [per_device(): all_refs = lax.all_gather(owner_chunk, 'dom', axis=2, tiled=False)]
    slice x5 -> x0, local copies, waits for them, and re-layouts: 21.6 us -> none  [shift_scores(): x = jnp.roll(jnp.flip(x, axis=2), 1, axis=2)]
    all_gather x0 -> x1, blocking collectives: none -> 20.7 us  [per_device(): owner_chunk = lax.all_gather(mine, 'cls', axis=2, tiled=False)]
    all_gather x1 -> x0, local copies, waits for them, and re-layouts: 6.86 us -> none  [per_device(): all_refs = lax.all_gather(mine, ('dom', 'cls'), axis=0, tiled=False)]
where the time goes in v6:
time: 344 us; the launch traced here: 343 us
  waiting for transfers between devices  157 us (46%)
  Pallas kernels  69.2 us (20%)
  local copies, waits for them, and re-layouts  32 us (9%)
  starting transfers between devices  25.8 us (8%)
  blocking collectives  20.7 us (6%)
  matrix products  16.2 us (5%)
  between operations  14.6 us (4%)
  other arithmetic  8.12 us (2%)
    all_to_all x1, waiting for transfers between devices, per_device(): got_img = lax.all_to_all(send_img, ('dom', 'cls'), 0, 0, tiled=True)  78.3 us
    pallas_call x1, Pallas kernels, shift_scores(): pl.pallas_call(_scores_kernel, grid=(steps,), in_specs=[pl.BlockSpec((ast...  69.2 us
    all_gather x1, waiting for transfers between devices, per_device(): all_refs = lax.all_gather(owner_chunk, 'dom', axis=2, tiled=False)  56.6 us
    all_gather x1, blocking collectives, per_device(): owner_chunk = lax.all_gather(mine, 'cls', axis=2, tiled=False)  20.7 us
    all_gather x1, waiting for transfers between devices, per_device(): final = lax.all_gather(current, 'dom', axis=0, tiled=False)  15.6 us
    all_to_all x1, starting transfers between devices, per_device(): got_wts = lax.all_to_all(send_wts, ('dom', 'cls'), 0, 0, tiled=True)  11.7 us
    all_to_all x1, starting transfers between devices, per_device(): got_img = lax.all_to_all(send_img, ('dom', 'cls'), 0, 0, tiled=True)  10.2 us
    dot_general x1, matrix products, per_device(): lax.dot_general(got_wts, got_img, (((0, 2), (0, 2)), ((1,), (1,))), prefe...  9.67 us
  transfers between devices with their start and end apart: 5, of which 4 were waited for; matrix products, arithmetic and copies ran while one was open for 10% of the time, Pallas kernels for 0%

profile of v6, /device:TPU:1, one launch (start us, length us, event | category | flops | bytes accessed | tf_op | source)
XLA Modules:
  0.0 343.3 jit_solution(1687813309445801728)
XLA Ops:
  7.2 0.7 slice_bitcast_fusion.15
  8.3 0.8 slice_bitcast_fusion.14
  9.1 0.8 slice_bitcast_fusion.13
  10.0 0.2 select_reduce_fusion
  10.2 0.2 select_reduce_fusion.2
  10.3 0.7 multiply_add_fusion.3
  11.1 0.2 convolution_convert_fusion.12
  11.3 0.1 copy.88
  11.4 0.3 convolution_convert_fusion.11
  11.8 0.3 convolution_convert_fusion.10
  12.1 0.1 copy.92
  12.2 0.3 convolution_convert_fusion.9
  12.8 0.2 maximum_bitcast_fusion
  13.0 0.6 copy.168
  13.6 1.3 reshape.466
  14.9 11.7 %all-to-all-start = ((bf16[128,2,384]{2,1,0:T(2,128)(2,1)}), bf16[128,2,384]{2,1,0:T(2,128)(2,1)S(1)}, u32[]{:S(2)}, u32[]{:S(2)}) async-start(bf16[128,2,384]{2,1,0:T(2,128)(2,1)} %reshape.466), calls=%async_computation | async-start | bytes 393216 | tf_op jit(solution)/shard_map/all_to_all | solution.py:116
  26.8 0.5 fusion.5
  27.3 0.3 copy.103
  27.6 0.6 convolution_convert_fusion
  28.1 0.9 copy.129
  29.0 2.0 copy.164
  31.0 0.5 fusion.4
  31.5 0.3 copy.101
  31.8 0.6 convolution_convert_fusion.1
  32.4 0.9 copy.127
  33.3 2.0 copy.165
  35.4 0.5 fusion.3
  35.9 0.3 copy.99
  36.2 0.6 convolution_convert_fusion.2
  36.7 0.9 copy.125
  37.6 2.0 copy.166
  39.6 0.5 fusion.2
  40.1 0.3 copy.97
  40.4 0.6 convolution_convert_fusion.3
  41.0 0.9 copy.123
  41.9 1.1 copy.167
  43.0 0.4 copy-done.2
  43.4 0.5 copy-done.3
  43.9 0.8 pad_maximum_fusion
  44.7 7.5 %copy.105 = bf16[128,4,6,1024]{3,1,2,0:T(4,128)(2,1)} copy(bf16[128,4,6,1024]{3,0,2,1:T(8,128)(2,1)S(1)} %pad_maximum_fusion) | data formatting | bytes 12582912 | tf_op jit(solution)/shard_map/stack | solution.py:113
  52.2 10.2 %all-to-all-start.1 = ((bf16[128,4,6,1024]{3,1,2,0:T(4,128)(2,1)}), bf16[128,4,6,1024]{3,1,2,0:T(4,128)(2,1)}, u32[]{:S(2)}, u32[]{:S(2)}) async-start(bf16[128,4,6,1024]{3,1,2,0:T(4,128)(2,1)} %copy.105), calls=%async_computation.1 | async-start | bytes 12582912 | tf_op jit(solution)/shard_map/all_to_all | solution.py:115
  62.5 0.4 reshape.467
  62.8 0.8 convert_reduce_fusion
  63.7 78.3 %all-to-all-done.1 = bf16[128,4,6,1024]{3,1,2,0:T(4,128)(2,1)} async-done(((bf16[128,4,6,1024]{3,1,2,0:T(4,128)(2,1)}), bf16[128,4,6,1024]{3,1,2,0:T(4,128)(2,1)}, u32[]{:S(2)}, u32[]{:S(2)}) %all-to-all-start.1) | async-done | bytes 6291488 | tf_op jit(solution)/shard_map/all_to_all | solution.py:115
  142.0 9.7 %fusion.6 = f32[4,32,1024]{2,1,0:T(8,128)S(1)} fusion(bf16[128,4,6,1024]{3,1,2,0:T(4,128)(2,1)} %all-to-all-done.1, bf16[128,4,6,32]{3,1,2,0:T(4,128)(2,1)S(1)} %bitcast.206), kind=kOutput, calls=%fused_computation.21 | convolution fusion | flops 201326592 | bytes 7012352 | tf_op jit(solution)/shard_map/dot_general | solution.py:117
  151.7 1.0 convert_bitcast_fusion.3
  152.7 0.1 convert_bitcast_fusion.1
  152.8 0.7 convert_bitcast_fusion
  153.8 0.7 maximum_bitcast_fusion.1
  154.5 3.9 %all-to-all-start.2 = ((bf16[8,4,32,128]{3,2,1,0:T(8,128)(2,1)}), bf16[8,4,32,128]{3,2,1,0:T(8,128)(2,1)S(1)}, u32[]{:S(2)}, u32[]{:S(2)}) async-start(bf16[8,4,32,128]{3,2,1,0:T(8,128)(2,1)} %maximum_bitcast_fusion.1), calls=%async_computation.2 | async-start | bytes 524288 | tf_op jit(solution)/shard_map/all_to_all | solution.py:129
  158.5 0.1 copy.116
  158.6 6.1 %all-to-all-done.2 = bf16[8,4,32,128]{3,2,1,0:T(8,128)(2,1)S(1)} async-done(((bf16[8,4,32,128]{3,2,1,0:T(8,128)(2,1)}), bf16[8,4,32,128]{3,2,1,0:T(8,128)(2,1)S(1)}, u32[]{:S(2)}, u32[]{:S(2)}) %all-to-all-start.2) | async-done | bytes 262176 | tf_op jit(solution)/shard_map/all_to_all | solution.py:129
  164.7 0.3 fusion.23
  165.0 20.7 %all-gather = bf16[4,32,1024]{2,1,0:T(8,128)(2,1)S(1)} all-gather(bf16[4,32,128]{2,1,0:T(8,128)(2,1)S(1)} %convert_element_type.129), channel_id=2, replica_groups=mesh['dom'=16,'cls'=8] {'cls'}, dimensions={2}, use_global_device_ids=true | all-gather | bytes 294912 | tf_op jit(solution)/shard_map/all_gather | solution.py:133
  185.7 0.7 copy.134
  186.5 0.6 fusion.33.sel_ref
  187.2 1.1 convolution_convert_fusion.8
  188.3 15.6 %all-gather.8.cloned.1.call-done = f32[512,1024]{1,0:T(8,128)} async-done(((f32[32,1024]{1,0:T(8,128)}), f32[512,1024]{1,0:T(8,128)}) %all-gather.8.cloned.1.call-update) | async-done | bytes 2097168 | tf_op jit(solution)/shard_map/all_gather | solution.py:136
  203.9 3.2 copy.119
  207.0 56.6 %all-gather.6.cloned.1.call-done.r_ref = bf16[4,32,128,128]{3,2,1,0:T(8,128)(2,1)} async-done(((bf16[4,32,8,128]{3,2,1,0:T(8,128)(2,1)}), bf16[4,32,128,128]{3,2,1,0:T(8,128)(2,1)}) %all-gather.6.cloned.1.call-update) | async-done | bytes 4194320 | tf_op jit(solution)/shard_map/all_gather | solution.py:134
  263.6 69.2 %shard_map.95 = f32[4,32,16,128]{3,2,1,0:T(8,128)} custom-call(bf16[2,1024,128]{2,1,0:T(8,128)(2,1)} %bitcast.228, bf16[128,256]{1,0:T(8,128)(2,1)} %fusion.33.sel_ref, bf16[4,32,128,128]{3,2,1,0:T(8,128)(2,1)} %all-gather.6.cloned.1.call-done.r_ref), custom_call_target="tpu_custom_call" | custom-call | flops 9663676416 | bytes 5767168 | tf_op jit(solution)/shard_map/pallas_call | solution.py:51
  332.8 1.3 fusion.9
  334.1 0.6 copy.112
  334.8 1.8 mul.224
  (61 shorter events, 1.4 us)
Async XLA Ops:
  12.8 13.8 %copy-start.7 = (s32[4,16]{1,0:T(4,128)S(1)}, s32[4,16]{1,0:T(4,128)}, u32[]{:S(2)}) copy-start(s32[4,16]{1,0:T(4,128)} %param.13) | copy-start | bytes 772
  12.8 13.8 %copy-start.5 = (bf16[16,16384]{1,0:T(8,128)(2,1)S(1)}, bf16[16,16384]{1,0:T(8,128)(2,1)}, u32[]{:S(2)}) copy-start(bf16[16,16384]{1,0:T(8,128)(2,1)} %param.8) | copy-start | bytes 1572868
  14.9 37.4 %all-to-all-start = ((bf16[128,2,384]{2,1,0:T(2,128)(2,1)}), bf16[128,2,384]{2,1,0:T(2,128)(2,1)S(1)}, u32[]{:S(2)}, u32[]{:S(2)}) async-start(bf16[128,2,384]{2,1,0:T(2,128)(2,1)} %reshape.466), calls=%async_computation | async-start | bytes 393216 | tf_op jit(solution)/shard_map/all_to_all | solution.py:116
  26.7 13.0 %copy-start = (bf16[2,8,128,128]{3,2,1,0:T(8,128)(2,1)}, bf16[2,8,128,128]{3,2,1,0:T(8,128)(2,1)S(1)}, u32[]{:S(2)}) copy-start(bf16[2,8,128,128]{3,2,1,0:T(8,128)(2,1)S(1)} %copy.120) | copy-start | bytes 1572868
  41.0 2.0 copy-start.4
  41.9 1.5 copy-start.2
  41.9 2.0 copy-start.3
  52.2 11.4 %copy-start.6 = (f32[32]{0:T(128)S(1)}, f32[32]{0:T(128)}, u32[]{:S(2)}) copy-start(f32[32]{0:T(128)} %param.10) | copy-start | bytes 388
  52.2 89.8 %all-to-all-start.1 = ((bf16[128,4,6,1024]{3,1,2,0:T(4,128)(2,1)}), bf16[128,4,6,1024]{3,1,2,0:T(4,128)(2,1)}, u32[]{:S(2)}, u32[]{:S(2)}) async-start(bf16[128,4,6,1024]{3,1,2,0:T(4,128)(2,1)} %copy.105), calls=%async_computation.1 | async-start | bytes 12582912 | tf_op jit(solution)/shard_map/all_to_all | solution.py:115
  62.4 141.5 %all-gather.8.cloned.1.call-start = ((), (), s32[]{:S(2)}) async-start(), calls=%async_computation.4 | async-start | bytes 2228224 | tf_op jit(solution)/shard_map/all_gather | solution.py:136
  151.7 6.8 %copy-start.8 = (s32[4]{0:T(128)S(1)}, s32[4]{0:T(128)}, u32[]{:S(2)}) copy-start(s32[4]{0:T(128)} %param.15) | copy-start | bytes 52
  152.8 34.3 %copy-start.1 = (bf16[2,8,128,128]{3,2,1,0:T(8,128)(2,1)S(1)}, bf16[2,8,128,128]{3,2,1,0:T(8,128)(2,1)}, u32[]{:S(2)}) copy-start(bf16[2,8,128,128]{3,2,1,0:T(8,128)(2,1)} %copy-done) | copy-start | bytes 1572868
  154.5 10.2 %all-to-all-start.2 = ((bf16[8,4,32,128]{3,2,1,0:T(8,128)(2,1)}), bf16[8,4,32,128]{3,2,1,0:T(8,128)(2,1)S(1)}, u32[]{:S(2)}, u32[]{:S(2)}) async-start(bf16[8,4,32,128]{3,2,1,0:T(8,128)(2,1)} %maximum_bitcast_fusion.1), calls=%async_computation.2 | async-start | bytes 524288 | tf_op jit(solution)/shard_map/all_to_all | solution.py:129
  158.4 105.2 %all-gather.6.cloned.1.call-start = ((), (), s32[]{:S(2)}) async-start(), calls=%async_computation.3 | async-start | bytes 4456448 | tf_op jit(solution)/shard_map/all_gather | solution.py:134
Sparse Core Ops, SparseCore 0:
  153.7 50.1 all-gather.7
  206.1 57.4 all-gather.5

commit v7 on v6

--- a/solution.py
+++ b/solution.py
@@ -34,9 +34,8 @@
     lax.fori_loop(0, classes, body, 0)
 
 
-def shift_scores(cube, refs, astep):
+def scores_operands(cube, astep):
     n, radii, angles = cube.shape
-    steps, classes = refs.shape[:2]
     turns = angles // astep
     b = jnp.arange(angles, dtype=jnp.int32)[None, None, :]
     e = jnp.arange(astep, dtype=jnp.int32)[:, None, None]
@@ -47,12 +46,18 @@
     b = jnp.arange(angles, dtype=jnp.int32)[:, None]
     col = jnp.arange(astep * 128, dtype=jnp.int32)[None, :]
     sel = (b == astep * ((col % 128) % turns) + col // 128).astype(cube.dtype)
-    flops = 2 * steps * classes * (n * turns * radii * astep * 128 + radii * angles * astep * 128)
+    return pt, sel
+
+
+def shift_scores(pt, sel, refs, n, turns):
+    astep, rows, radii = pt.shape
+    steps, classes, _, angles = refs.shape
+    flops = 2 * steps * classes * (rows * radii * astep * 128 + radii * angles * astep * 128)
     return pl.pallas_call(
         _scores_kernel,
         grid=(steps,),
         in_specs=[
-            pl.BlockSpec((astep, n * turns, radii), lambda s: (0, 0, 0)),
+            pl.BlockSpec((astep, rows, radii), lambda s: (0, 0, 0)),
             pl.BlockSpec((angles, astep * 128), lambda s: (0, 0)),
             pl.BlockSpec((1, classes, radii, angles), lambda s: (s, 0, 0, 0)),
         ],
@@ -84,8 +89,11 @@
     cube = particles.reshape(per_dev, RADII, ANGLES)
     scale = 1.0 / math.sqrt(pixels)
 
-    send_img = []
-    send_wts = []
+    pt, sel = scores_operands(cube, ASTEP)
+    rows = chunk // ANGLES
+    current = lax.dynamic_slice_in_dim(averages, me_dom * chunk, chunk, axis=1)
+    owner_hot = (owners[None, :] == jnp.arange(groups, dtype=jnp.int32)[:, None]).astype(jnp.bfloat16)
+    all_scores = []
     for step in range(STEPS):
         shifts = rot_ids[step] * ASTEP
         rotated = rotate_each(cube, shifts).reshape(per_dev, pixels)
@@ -100,7 +108,7 @@
         )
         images = jnp.dot(placing, rotated, preferred_element_type=jnp.float32).astype(jnp.bfloat16)
         images = images.reshape(groups, capacity, doms, chunk).transpose(2, 0, 1, 3)
-        send_img.append(images)
+        images = images.reshape(doms * groups, capacity, chunk)
         class_hot = (
             class_ids[step][:, None] == jnp.arange(per_group, dtype=jnp.int32)[None, :]
         ).astype(jnp.bfloat16)
@@ -109,35 +117,26 @@
             jnp.bfloat16
         )
         wts = jnp.broadcast_to(wts.reshape(1, groups, capacity, per_group), (doms, groups, capacity, per_group))
-        send_wts.append(wts)
-    send_img = jnp.stack(send_img, axis=2).reshape(doms * groups, STEPS, capacity, chunk)
-    send_wts = jnp.stack(send_wts, axis=2).reshape(doms * groups, STEPS, capacity, per_group)
-    got_img = lax.all_to_all(send_img, ("dom", "cls"), 0, 0, tiled=True)
-    got_wts = lax.all_to_all(send_wts, ("dom", "cls"), 0, 0, tiled=True)
-    totals = lax.dot_general(
-        got_wts, got_img, (((0, 2), (0, 2)), ((1,), (1,))), preferred_element_type=jnp.float32
-    )
-    mass = jnp.sum(got_wts.astype(jnp.float32), axis=(0, 2))
-
-    current = lax.dynamic_slice_in_dim(averages, me_dom * chunk, chunk, axis=1)
-    ref_chunks = []
-    for step in range(STEPS):
-        current = (prior_mass[:, None] * current + totals[step]) / (prior_mass + mass[step])[:, None]
-        ref_chunks.append(current.astype(jnp.bfloat16))
-    rows = chunk // ANGLES
-    ref_chunks = jnp.stack(ref_chunks, axis=0).reshape(STEPS, per_group, groups, rows // groups * ANGLES)
-    got_refs = lax.all_to_all(ref_chunks.transpose(2, 0, 1, 3), "cls", 0, 0, tiled=True)
-    owner_hot = (owners[None, :] == jnp.arange(groups, dtype=jnp.int32)[:, None]).astype(jnp.bfloat16)
-    mine = jnp.einsum("gs,gskp->skp", owner_hot, got_refs, preferred_element_type=jnp.float32)
-    mine = mine.astype(jnp.bfloat16)
-    owner_chunk = lax.all_gather(mine, "cls", axis=2, tiled=False)
-    all_refs = lax.all_gather(owner_chunk, "dom", axis=2, tiled=False)
-    all_refs = all_refs.reshape(STEPS, per_group, pixels)
+        wts = wts.reshape(doms * groups, capacity, per_group)
+        got_img = lax.all_to_all(images, ("dom", "cls"), 0, 0, tiled=True)
+        got_wts = lax.all_to_all(wts, ("dom", "cls"), 0, 0, tiled=True)
+        totals = lax.dot_general(
+            got_wts, got_img, (((0, 1), (0, 1)), ((), ())), preferred_element_type=jnp.float32
+        )
+        mass = jnp.sum(got_wts.astype(jnp.float32), axis=(0, 1))
+        current = (prior_mass[:, None] * current + totals) / (prior_mass + mass)[:, None]
+        piece = current.astype(jnp.bfloat16).reshape(per_group, groups, rows // groups * ANGLES)
+        got_refs = lax.all_to_all(piece.transpose(1, 0, 2), "cls", 0, 0, tiled=True)
+        mine = jnp.einsum("g,gkp->kp", owner_hot[:, step], got_refs, preferred_element_type=jnp.float32)
+        mine = mine.astype(jnp.bfloat16)
+        owner_chunk = lax.all_gather(mine, "cls", axis=1, tiled=False)
+        refs = lax.all_gather(owner_chunk, "dom", axis=1, tiled=False)
+        refs = refs.reshape(1, per_group, RADII, ANGLES)
+        all_scores.append(shift_scores(pt, sel, refs, per_dev, ROT)[0])
+    current, _ = lax.optimization_barrier((current, refs))
     final = lax.all_gather(current, "dom", axis=0, tiled=False)
     final = final.transpose(1, 0, 2).reshape(per_group, pixels)
-
-    shifted = shift_scores(cube, all_refs.reshape(STEPS, per_group, RADII, ANGLES), ASTEP)
-    scores = shifted.transpose(0, 2, 3, 1).reshape(STEPS, per_dev, ROT * per_group)
+    scores = jnp.stack(all_scores, axis=0).transpose(0, 2, 3, 1).reshape(STEPS, per_dev, ROT * per_group)
     return (scores * scale, final)
 
 

time: 344 us -> 506 us (1.47)
  blocking collectives: 20.7 us -> 101 us
  waiting for transfers between devices: 157 us -> 203 us
  starting transfers between devices: 25.8 us -> 50.9 us
  Pallas kernels: 69.2 us -> 75.6 us
  matrix products: 16.2 us -> 22.3 us
    all_gather x1 -> x4, blocking collectives: 20.7 us -> 78.2 us  [per_device(): owner_chunk = lax.all_gather(mine, 'cls', axis=1, tiled=False)]
    all_to_all x3 -> x9, waiting for transfers between devices: 84.4 us -> 132 us  [the longest x4 90.5 us: per_device(): got_img = lax.all_to_all(images, ('dom', 'cls'), 0, 0, tiled=True)]
    all_to_all x3 -> x9, starting transfers between devices: 25.8 us -> 50.4 us  [the longest x4 25 us: per_device(): got_wts = lax.all_to_all(wts, ('dom', 'cls'), 0, 0, tiled=True)]
    all_to_all x0 -> x3, blocking collectives: none -> 22.9 us  [per_device(): got_refs = lax.all_to_all(piece.transpose(1, 0, 2), 'cls', 0, 0, tiled=True)]
    all_gather x1 -> x4, waiting for transfers between devices: 56.6 us -> 43.7 us  [per_device(): refs = lax.all_gather(owner_chunk, 'dom', axis=1, tiled=False)]
    all_gather x1, waiting for transfers between devices: 15.6 us -> 27.1 us  [per_device(): final = lax.all_gather(current, 'dom', axis=0, tiled=False)]
    transpose x0 -> x4, local copies, waits for them, and re-layouts: none -> 8.84 us  [per_device(): images = images.reshape(groups, capacity, doms, chunk).transpose(2, 0, 1, 3)]
    another operation x17 -> x0, local copies, waits for them, and re-layouts: 7.78 us -> none  [the longest x1 7.51 us: per_device(): jnp.stack(send_img, axis=2).reshape(doms * groups, STEPS, capacity, chunk)]
  transfers between devices with their start and end apart: 5 -> 14, of which waited for: 4 -> 12; matrix products, arithmetic and copies ran while one was open for 10% -> 9% of each run, Pallas kernels for 0% -> 15%
where the time goes in v7:
time: 506 us; the launch traced here: 504 us
  waiting for transfers between devices  203 us (40%)
  blocking collectives  101 us (20%)
  Pallas kernels  75.6 us (15%)
  starting transfers between devices  50.9 us (10%)
  local copies, waits for them, and re-layouts  31.2 us (6%)
  matrix products  22.3 us (4%)
  between operations  14.3 us (3%)
  other arithmetic  5.75 us (1%)
    all_to_all x4, waiting for transfers between devices, per_device(): got_img = lax.all_to_all(images, ('dom', 'cls'), 0, 0, tiled=True)  90.5 us
    all_gather x4, blocking collectives, per_device(): owner_chunk = lax.all_gather(mine, 'cls', axis=1, tiled=False)  78.2 us
    pallas_call x4, Pallas kernels, shift_scores(): pl.pallas_call(_scores_kernel, grid=(steps,), in_specs=[pl.BlockSpec((ast...  75.6 us
    all_gather x4, waiting for transfers between devices, per_device(): refs = lax.all_gather(owner_chunk, 'dom', axis=1, tiled=False)  43.7 us
    all_to_all x4, waiting for transfers between devices, per_device(): got_wts = lax.all_to_all(wts, ('dom', 'cls'), 0, 0, tiled=True)  36.7 us
    all_gather x1, waiting for transfers between devices, per_device(): final = lax.all_gather(current, 'dom', axis=0, tiled=False)  27.1 us
    all_to_all x4, starting transfers between devices, per_device(): got_wts = lax.all_to_all(wts, ('dom', 'cls'), 0, 0, tiled=True)  25 us
    all_to_all x3, blocking collectives, per_device(): got_refs = lax.all_to_all(piece.transpose(1, 0, 2), 'cls', 0, 0, tiled=True)  22.9 us
  transfers between devices with their start and end apart: 14, of which 12 were waited for; matrix products, arithmetic and copies ran while one was open for 9% of the time, Pallas kernels for 15%

profile of v7, /device:TPU:1, one launch (start us, length us, event | category | flops | bytes accessed | tf_op | source)
XLA Modules:
  0.0 504.5 jit_solution(5922451766332834752)
XLA Ops:
  7.2 0.8 slice_bitcast_fusion.11
  8.4 0.8 slice_bitcast_fusion.9
  9.2 0.8 slice_bitcast_fusion.10
  10.4 0.7 multiply_add_fusion.3
  11.6 0.8 copy.67
  12.4 11.5 %all-to-all-start.9 = ((bf16[128,6,32]{2,1,0:T(8,128)(2,1)}), bf16[128,6,32]{2,1,0:T(8,128)(2,1)S(1)}, u32[]{:S(2)}, u32[]{:S(2)}) async-start(bf16[128,6,32]{2,1,0:T(8,128)(2,1)} %copy.67), calls=%async_computation.9 | async-start | bytes 524288 | tf_op jit(solution)/shard_map/all_to_all | solution.py:122
  25.5 0.8 copy.59
  26.3 8.9 %all-to-all-done.9 = bf16[128,6,32]{2,1,0:T(8,128)(2,1)S(1)} async-done(((bf16[128,6,32]{2,1,0:T(8,128)(2,1)}), bf16[128,6,32]{2,1,0:T(8,128)(2,1)S(1)}, u32[]{:S(2)}, u32[]{:S(2)}) %all-to-all-start.9) | async-done | bytes 49184 | tf_op jit(solution)/shard_map/all_to_all | solution.py:122
  35.2 4.2 all-to-all-start.6
  39.6 0.9 copy.51
  40.6 10.2 %all-to-all-done.6 = bf16[128,6,32]{2,1,0:T(8,128)(2,1)S(1)} async-done(((bf16[128,6,32]{2,1,0:T(8,128)(2,1)}), bf16[128,6,32]{2,1,0:T(8,128)(2,1)S(1)}, u32[]{:S(2)}, u32[]{:S(2)}) %all-to-all-start.6) | async-done | bytes 49184 | tf_op jit(solution)/shard_map/all_to_all | solution.py:122
  50.7 4.2 all-to-all-start.3
  55.0 0.8 copy.43
  56.1 10.2 %all-to-all-done.3 = bf16[128,6,32]{2,1,0:T(8,128)(2,1)S(1)} async-done(((bf16[128,6,32]{2,1,0:T(8,128)(2,1)}), bf16[128,6,32]{2,1,0:T(8,128)(2,1)S(1)}, u32[]{:S(2)}, u32[]{:S(2)}) %all-to-all-start.3) | async-done | bytes 49184 | tf_op jit(solution)/shard_map/all_to_all | solution.py:122
  66.3 5.2 %all-to-all-start = ((bf16[128,6,32]{2,1,0:T(8,128)(2,1)}), bf16[128,6,32]{2,1,0:T(8,128)(2,1)}, u32[]{:S(2)}, u32[]{:S(2)}) async-start(bf16[128,6,32]{2,1,0:T(8,128)(2,1)} %copy.43), calls=%async_computation | async-start | bytes 524288 | tf_op jit(solution)/shard_map/all_to_all | solution.py:122
  72.1 0.9 copy.92
  73.0 2.2 copy.45
  75.2 7.4 %all-to-all-done = bf16[128,6,32]{2,1,0:T(8,128)(2,1)} async-done(((bf16[128,6,32]{2,1,0:T(8,128)(2,1)}), bf16[128,6,32]{2,1,0:T(8,128)(2,1)}, u32[]{:S(2)}, u32[]{:S(2)}) %all-to-all-start) | async-done | bytes 49184 | tf_op jit(solution)/shard_map/all_to_all | solution.py:122
  82.6 4.2 all-to-all-start.1
  86.8 1.3 fusion.9
  88.1 1.3 copy.52
  90.0 0.9 copy.95
  90.8 2.2 copy.53
  93.0 24.2 %all-to-all-done.1 = bf16[128,6,1024]{2,1,0:T(8,128)(2,1)S(1)} async-done(((bf16[128,6,1024]{2,1,0:T(8,128)(2,1)}), bf16[128,6,1024]{2,1,0:T(8,128)(2,1)S(1)}, u32[]{:S(2)}, u32[]{:S(2)}) %all-to-all-start.1) | async-done | bytes 1572896 | tf_op jit(solution)/shard_map/all_to_all | solution.py:121
  117.2 5.9 %all-to-all-start.4 = ((bf16[128,6,1024]{2,1,0:T(8,128)(2,1)}), bf16[128,6,1024]{2,1,0:T(8,128)(2,1)}, u32[]{:S(2)}, u32[]{:S(2)}) async-start(bf16[128,6,1024]{2,1,0:T(8,128)(2,1)} %bitcast.29), calls=%async_computation.4 | async-start | bytes 4194304 | tf_op jit(solution)/shard_map/all_to_all | solution.py:121
  123.2 1.3 fusion.10
  124.5 1.3 copy.60
  126.4 0.9 copy.98
  127.3 2.2 copy.61
  129.5 23.7 %all-to-all-done.4 = bf16[128,6,1024]{2,1,0:T(8,128)(2,1)} async-done(((bf16[128,6,1024]{2,1,0:T(8,128)(2,1)}), bf16[128,6,1024]{2,1,0:T(8,128)(2,1)}, u32[]{:S(2)}, u32[]{:S(2)}) %all-to-all-start.4) | async-done | bytes 1572896 | tf_op jit(solution)/shard_map/all_to_all | solution.py:121
  153.2 5.9 %all-to-all-start.7 = ((bf16[128,6,1024]{2,1,0:T(8,128)(2,1)}), bf16[128,6,1024]{2,1,0:T(8,128)(2,1)}, u32[]{:S(2)}, u32[]{:S(2)}) async-start(bf16[128,6,1024]{2,1,0:T(8,128)(2,1)} %bitcast.44), calls=%async_computation.7 | async-start | bytes 4194304 | tf_op jit(solution)/shard_map/all_to_all | solution.py:121
  159.1 1.3 fusion.11
  160.4 1.3 copy.68
  162.3 0.9 copy.101
  163.1 2.2 copy.69
  165.3 23.8 %all-to-all-done.7 = bf16[128,6,1024]{2,1,0:T(8,128)(2,1)} async-done(((bf16[128,6,1024]{2,1,0:T(8,128)(2,1)}), bf16[128,6,1024]{2,1,0:T(8,128)(2,1)}, u32[]{:S(2)}, u32[]{:S(2)}) %all-to-all-start.7) | async-done | bytes 1572896 | tf_op jit(solution)/shard_map/all_to_all | solution.py:121
  189.2 6.0 %all-to-all-start.10 = ((bf16[128,6,1024]{2,1,0:T(8,128)(2,1)}), bf16[128,6,1024]{2,1,0:T(8,128)(2,1)}, u32[]{:S(2)}, u32[]{:S(2)}) async-start(bf16[128,6,1024]{2,1,0:T(8,128)(2,1)} %bitcast.59), calls=%async_computation.10 | async-start | bytes 4194304 | tf_op jit(solution)/shard_map/all_to_all | solution.py:121
  195.7 1.1 convert_reduce_fusion.3
  196.8 2.8 fusion.45
  199.6 3.4 fusion.39
  203.1 3.4 fusion.33
  206.5 18.8 %all-to-all-done.10 = bf16[128,6,1024]{2,1,0:T(8,128)(2,1)} async-done(((bf16[128,6,1024]{2,1,0:T(8,128)(2,1)}), bf16[128,6,1024]{2,1,0:T(8,128)(2,1)}, u32[]{:S(2)}, u32[]{:S(2)}) %all-to-all-start.10) | async-done | bytes 1572896 | tf_op jit(solution)/shard_map/all_to_all | solution.py:121
  225.3 3.4 fusion.27
  228.7 0.7 bitcast_bitcast_fusion
  229.4 3.4 all-to-all-start.11
  232.9 5.0 all-to-all-done.11
  238.0 19.2 %all-gather.6 = bf16[32,1024]{1,0:T(8,128)(2,1)S(1)} all-gather(bf16[32,128]{1,0:T(8,128)(2,1)S(1)} %convert_element_type.159), channel_id=8, replica_groups=mesh['dom'=16,'cls'=8] {'cls'}, dimensions={1}, use_global_device_ids=true | all-gather | bytes 73728 | tf_op jit(solution)/shard_map/all_gather | solution.py:132
  257.9 7.6 %all_to_all.60 = bf16[8,32,128]{2,1,0:T(8,128)(2,1)S(1)} all-to-all(bf16[8,32,128]{2,1,0:T(8,128)(2,1)S(1)} %bitcast_bitcast_fusion.1), channel_id=1, replica_groups=mesh['dom'=16,'cls'=8] {'cls'}, dimensions={0} | all-to-all | bytes 131072 | tf_op jit(solution)/shard_map/all_to_all | solution.py:129
  265.7 19.5 %all-gather.4 = bf16[32,1024]{1,0:T(8,128)(2,1)S(1)} all-gather(bf16[32,128]{1,0:T(8,128)(2,1)S(1)} %convert_element_type.151), channel_id=6, replica_groups=mesh['dom'=16,'cls'=8] {'cls'}, dimensions={1}, use_global_device_ids=true | all-gather | bytes 73728 | tf_op jit(solution)/shard_map/all_gather | solution.py:132
  285.9 7.7 %all_to_all.61 = bf16[8,32,128]{2,1,0:T(8,128)(2,1)S(1)} all-to-all(bf16[8,32,128]{2,1,0:T(8,128)(2,1)S(1)} %bitcast_bitcast_fusion.2), channel_id=1, replica_groups=mesh['dom'=16,'cls'=8] {'cls'}, dimensions={0} | all-to-all | bytes 131072 | tf_op jit(solution)/shard_map/all_to_all | solution.py:129
  293.8 19.4 %all-gather.2 = bf16[32,1024]{1,0:T(8,128)(2,1)S(1)} all-gather(bf16[32,128]{1,0:T(8,128)(2,1)S(1)} %convert_element_type.143), channel_id=4, replica_groups=mesh['dom'=16,'cls'=8] {'cls'}, dimensions={1}, use_global_device_ids=true | all-gather | bytes 73728 | tf_op jit(solution)/shard_map/all_gather | solution.py:132
  313.9 7.7 %all_to_all.62 = bf16[8,32,128]{2,1,0:T(8,128)(2,1)S(1)} all-to-all(bf16[8,32,128]{2,1,0:T(8,128)(2,1)S(1)} %bitcast_bitcast_fusion.3), channel_id=1, replica_groups=mesh['dom'=16,'cls'=8] {'cls'}, dimensions={0} | all-to-all | bytes 131072 | tf_op jit(solution)/shard_map/all_to_all | solution.py:129
  321.7 20.1 %all-gather = bf16[32,1024]{1,0:T(8,128)(2,1)S(1)} all-gather(bf16[32,128]{1,0:T(8,128)(2,1)S(1)} %convert_element_type.135), channel_id=2, replica_groups=mesh['dom'=16,'cls'=8] {'cls'}, dimensions={1}, use_global_device_ids=true | all-gather | bytes 73728 | tf_op jit(solution)/shard_map/all_gather | solution.py:132
  343.7 1.1 convolution_convert_fusion.8
  344.9 18.9 %shard_map.98 = f32[1,32,16,128]{3,2,1,0:T(8,128)} custom-call(bf16[2,1024,128]{2,1,0:T(8,128)(2,1)} %bitcast.239, bf16[128,256]{1,0:T(8,128)(2,1)} %fusion.65.sel_ref, bf16[1,32,128,128]{3,2,1,0:T(8,128)(2,1)} %bitcast.260), custom_call_target="tpu_custom_call" | custom-call | flops 2415919104 | bytes 1835008 | tf_op jit(solution)/shard_map/pallas_call | solution.py:56
  363.7 18.9 %shard_map.97 = f32[1,32,16,128]{3,2,1,0:T(8,128)} custom-call(bf16[2,1024,128]{2,1,0:T(8,128)(2,1)} %bitcast.240, bf16[128,256]{1,0:T(8,128)(2,1)} %fusion.65.sel_ref, bf16[1,32,128,128]{3,2,1,0:T(8,128)(2,1)} %bitcast.261), custom_call_target="tpu_custom_call" | custom-call | flops 2415919104 | bytes 1835008 | tf_op jit(solution)/shard_map/pallas_call | solution.py:56
  382.6 16.4 %all-gather.17.cloned.1.call-done = bf16[32,128,128]{2,1,0:T(8,128)(2,1)} async-done(((bf16[32,8,128]{2,1,0:T(8,128)(2,1)}), bf16[32,128,128]{2,1,0:T(8,128)(2,1)}) %all-gather.17.cloned.1.call-update) | async-done | bytes 1048592 | tf_op jit(solution)/shard_map/all_gather | solution.py:133
  399.0 18.9 %shard_map.96 = f32[1,32,16,128]{3,2,1,0:T(8,128)} custom-call(bf16[2,1024,128]{2,1,0:T(8,128)(2,1)} %bitcast.241, bf16[128,256]{1,0:T(8,128)(2,1)} %fusion.65.sel_ref, bf16[1,32,128,128]{3,2,1,0:T(8,128)(2,1)} %bitcast.262), custom_call_target="tpu_custom_call" | custom-call | flops 2415919104 | bytes 1835008 | tf_op jit(solution)/shard_map/pallas_call | solution.py:56
  417.9 27.3 %all-gather.15.cloned.1.call-done = bf16[32,128,128]{2,1,0:T(8,128)(2,1)} async-done(((bf16[32,8,128]{2,1,0:T(8,128)(2,1)}), bf16[32,128,128]{2,1,0:T(8,128)(2,1)}) %all-gather.15.cloned.1.call-update) | async-done | bytes 1048592 | tf_op jit(solution)/shard_map/all_gather | solution.py:133
  445.2 19.0 %shard_map.95 = f32[1,32,16,128]{3,2,1,0:T(8,128)} custom-call(bf16[2,1024,128]{2,1,0:T(8,128)(2,1)} %bitcast.242, bf16[128,256]{1,0:T(8,128)(2,1)} %fusion.65.sel_ref, bf16[1,32,128,128]{3,2,1,0:T(8,128)(2,1)} %bitcast.263), custom_call_target="tpu_custom_call" | custom-call | flops 2415919104 | bytes 1835008 | tf_op jit(solution)/shard_map/pallas_call | solution.py:56
  464.2 1.1 fusion.48
  465.9 1.8 mul.230
  467.6 27.1 %all-gather.23.cloned.1.call-done = f32[512,1024]{1,0:T(8,128)} async-done(((f32[32,1024]{1,0:T(8,128)}), f32[512,1024]{1,0:T(8,128)}) %all-gather.23.cloned.1.call-update) | async-done | bytes 2097168 | tf_op jit(solution)/shard_map/all_gather | solution.py:137
  494.8 3.2 copy.88
  (105 shorter events, 11.5 us)
Async XLA Ops:
  7.2 17.6 %copy-start.11 = (s32[4,16]{1,0:T(4,128)S(1)}, s32[4,16]{1,0:T(4,128)}, u32[]{:S(2)}) copy-start(s32[4,16]{1,0:T(4,128)} %param.13) | copy-start | bytes 772
  7.2 17.6 %copy-start.4 = (bf16[16,16384]{1,0:T(8,128)(2,1)S(1)}, bf16[16,16384]{1,0:T(8,128)(2,1)}, u32[]{:S(2)}) copy-start(bf16[16,16384]{1,0:T(8,128)(2,1)} %param.8) | copy-start | bytes 1572868
  12.4 22.8 %all-to-all-start.9 = ((bf16[128,6,32]{2,1,0:T(8,128)(2,1)}), bf16[128,6,32]{2,1,0:T(8,128)(2,1)S(1)}, u32[]{:S(2)}, u32[]{:S(2)}) async-start(bf16[128,6,32]{2,1,0:T(8,128)(2,1)} %copy.67), calls=%async_computation.9 | async-start | bytes 524288 | tf_op jit(solution)/shard_map/all_to_all | solution.py:122
  35.2 15.6 %all-to-all-start.6 = ((bf16[128,6,32]{2,1,0:T(8,128)(2,1)}), bf16[128,6,32]{2,1,0:T(8,128)(2,1)S(1)}, u32[]{:S(2)}, u32[]{:S(2)}) async-start(bf16[128,6,32]{2,1,0:T(8,128)(2,1)} %copy.59), calls=%async_computation.6 | async-start | bytes 524288 | tf_op jit(solution)/shard_map/all_to_all | solution.py:122
  50.7 4.2 copy-start
  50.7 15.6 %all-to-all-start.3 = ((bf16[128,6,32]{2,1,0:T(8,128)(2,1)}), bf16[128,6,32]{2,1,0:T(8,128)(2,1)S(1)}, u32[]{:S(2)}, u32[]{:S(2)}) async-start(bf16[128,6,32]{2,1,0:T(8,128)(2,1)} %copy.51), calls=%async_computation.3 | async-start | bytes 524288 | tf_op jit(solution)/shard_map/all_to_all | solution.py:122
  66.3 6.7 %copy-start.2 = (bf16[128,6,32]{2,1,0:T(8,128)(2,1)}, bf16[128,6,32]{2,1,0:T(8,128)(2,1)S(1)}, u32[]{:S(2)}) copy-start(bf16[128,6,32]{2,1,0:T(8,128)(2,1)S(1)} %all-to-all-done.3) | copy-start | bytes 147460
  66.3 16.3 %all-to-all-start = ((bf16[128,6,32]{2,1,0:T(8,128)(2,1)}), bf16[128,6,32]{2,1,0:T(8,128)(2,1)}, u32[]{:S(2)}, u32[]{:S(2)}) async-start(bf16[128,6,32]{2,1,0:T(8,128)(2,1)} %copy.43), calls=%async_computation | async-start | bytes 524288 | tf_op jit(solution)/shard_map/all_to_all | solution.py:122
  82.6 34.6 %all-to-all-start.1 = ((bf16[128,6,1024]{2,1,0:T(8,128)(2,1)}), bf16[128,6,1024]{2,1,0:T(8,128)(2,1)S(1)}, u32[]{:S(2)}, u32[]{:S(2)}) async-start(bf16[128,6,1024]{2,1,0:T(8,128)(2,1)} %bitcast.13), calls=%async_computation.1 | async-start | bytes 4194304 | tf_op jit(solution)/shard_map/all_to_all | solution.py:121
  117.2 36.0 %all-to-all-start.4 = ((bf16[128,6,1024]{2,1,0:T(8,128)(2,1)}), bf16[128,6,1024]{2,1,0:T(8,128)(2,1)}, u32[]{:S(2)}, u32[]{:S(2)}) async-start(bf16[128,6,1024]{2,1,0:T(8,128)(2,1)} %bitcast.29), calls=%async_computation.4 | async-start | bytes 4194304 | tf_op jit(solution)/shard_map/all_to_all | solution.py:121
  153.2 36.0 %all-to-all-start.7 = ((bf16[128,6,1024]{2,1,0:T(8,128)(2,1)}), bf16[128,6,1024]{2,1,0:T(8,128)(2,1)}, u32[]{:S(2)}, u32[]{:S(2)}) async-start(bf16[128,6,1024]{2,1,0:T(8,128)(2,1)} %bitcast.44), calls=%async_computation.7 | async-start | bytes 4194304 | tf_op jit(solution)/shard_map/all_to_all | solution.py:121
  189.2 6.2 %copy-start.1 = (bf16[128,6,32]{2,1,0:T(8,128)(2,1)S(1)}, bf16[128,6,32]{2,1,0:T(8,128)(2,1)}, u32[]{:S(2)}) copy-start(bf16[128,6,32]{2,1,0:T(8,128)(2,1)} %copy-done) | copy-start | bytes 147460
  189.2 6.4 %copy-start.3 = (bf16[128,6,32]{2,1,0:T(8,128)(2,1)S(1)}, bf16[128,6,32]{2,1,0:T(8,128)(2,1)}, u32[]{:S(2)}) copy-start(bf16[128,6,32]{2,1,0:T(8,128)(2,1)} %copy-done.2) | copy-start | bytes 147460
  189.2 7.6 %copy-start.12 = (f32[32]{0:T(128)S(1)}, f32[32]{0:T(128)}, u32[]{:S(2)}) copy-start(f32[32]{0:T(128)} %param.10) | copy-start | bytes 388
  189.2 36.1 %all-to-all-start.10 = ((bf16[128,6,1024]{2,1,0:T(8,128)(2,1)}), bf16[128,6,1024]{2,1,0:T(8,128)(2,1)}, u32[]{:S(2)}, u32[]{:S(2)}) async-start(bf16[128,6,1024]{2,1,0:T(8,128)(2,1)} %bitcast.59), calls=%async_computation.10 | async-start | bytes 4194304 | tf_op jit(solution)/shard_map/all_to_all | solution.py:121
  199.6 3.5 copy-start.9
  203.1 29.7 %copy-start.13 = (s32[4]{0:T(128)S(1)}, s32[4]{0:T(128)}, u32[]{:S(2)}) copy-start(s32[4]{0:T(128)} %param.15) | copy-start | bytes 52
  225.3 88.6 %copy-start.10 = (f32[32,1024]{1,0:T(8,128)S(1)}, f32[32,1024]{1,0:T(8,128)}, u32[]{:S(2)}) copy-start(f32[32,1024]{1,0:T(8,128)} %copy-done.9) | copy-start | bytes 393220
  228.7 114.1 %copy-start.5 = (f32[32,1024]{1,0:T(8,128)}, f32[32,1024]{1,0:T(8,128)S(1)}, u32[]{:S(2)}) copy-start(f32[32,1024]{1,0:T(8,128)S(1)} %fusion.27) | copy-start | bytes 393220
  229.4 8.5 %all-to-all-start.11 = ((bf16[8,32,128]{2,1,0:T(8,128)(2,1)}), bf16[8,32,128]{2,1,0:T(8,128)(2,1)S(1)}, u32[]{:S(2)}, u32[]{:S(2)}) async-start(bf16[8,32,128]{2,1,0:T(8,128)(2,1)} %bitcast_bitcast_fusion), calls=%async_computation.11 | async-start | bytes 131072 | tf_op jit(solution)/shard_map/all_to_all | solution.py:129
  232.8 110.0 %all-gather.21.cloned.1.call-start = ((), (), s32[]{:S(2)}) async-start(), calls=%async_computation.15 | async-start | bytes 1114112 | tf_op jit(solution)/shard_map/all_gather | solution.py:133
  257.9 105.9 %all-gather.19.cloned.1.call-start = ((), (), s32[]{:S(2)}) async-start(), calls=%async_computation.14 | async-start | bytes 1114112 | tf_op jit(solution)/shard_map/all_gather | solution.py:133
  285.9 113.1 %all-gather.17.cloned.1.call-start = ((), (), s32[]{:S(2)}) async-start(), calls=%async_computation.13 | async-start | bytes 1114112 | tf_op jit(solution)/shard_map/all_gather | solution.py:133
  313.8 131.4 %all-gather.15.cloned.1.call-start = ((), (), s32[]{:S(2)}) async-start(), calls=%async_computation.12 | async-start | bytes 1114112 | tf_op jit(solution)/shard_map/all_gather | solution.py:133
  342.5 152.3 %all-gather.23.cloned.1.call-start = ((), (), s32[]{:S(2)}) async-start(), calls=%async_computation.16 | async-start | bytes 2228224 | tf_op jit(solution)/shard_map/all_gather | solution.py:137
  445.2 19.0 %copy-start.6 = (f32[1,32,16,128]{3,2,1,0:T(8,128)S(1)}, f32[1,32,16,128]{3,2,1,0:T(8,128)}, u32[]{:S(2)}) copy-start(f32[1,32,16,128]{3,2,1,0:T(8,128)} %shard_map.98) | copy-start | bytes 786436
  445.2 19.0 %copy-start.7 = (f32[1,32,16,128]{3,2,1,0:T(8,128)S(1)}, f32[1,32,16,128]{3,2,1,0:T(8,128)}, u32[]{:S(2)}) copy-start(f32[1,32,16,128]{3,2,1,0:T(8,128)} %shard_map.97) | copy-start | bytes 786436
  445.2 19.0 %copy-start.8 = (f32[1,32,16,128]{3,2,1,0:T(8,128)S(1)}, f32[1,32,16,128]{3,2,1,0:T(8,128)}, u32[]{:S(2)}) copy-start(f32[1,32,16,128]{3,2,1,0:T(8,128)} %shard_map.96) | copy-start | bytes 786436
Sparse Core Ops, SparseCore 0:
  258.0 47.8 all-gather.20
  308.2 44.0 all-gather.18
  354.5 44.4 all-gather.16
  401.1 44.0 all-gather.14
  447.4 47.2 all-gather.22

commit v8 on v6

--- a/solution.py
+++ b/solution.py
@@ -133,6 +133,7 @@
     owner_chunk = lax.all_gather(mine, "cls", axis=2, tiled=False)
     all_refs = lax.all_gather(owner_chunk, "dom", axis=2, tiled=False)
     all_refs = all_refs.reshape(STEPS, per_group, pixels)
+    current, all_refs = lax.optimization_barrier((current, all_refs))
     final = lax.all_gather(current, "dom", axis=0, tiled=False)
     final = final.transpose(1, 0, 2).reshape(per_group, pixels)
 

time: 344 us -> 349 us (1.015)
  local copies, waits for them, and re-layouts: 32 us -> 44.8 us
  waiting for transfers between devices: 157 us -> 149 us
    all_gather x1, waiting for transfers between devices: 15.6 us -> 0.01 us  [per_device(): final = lax.all_gather(current, 'dom', axis=0, tiled=False)]
    all_gather x1, waiting for transfers between devices: 56.6 us -> 64.2 us  [per_device(): all_refs = lax.all_gather(owner_chunk, 'dom', axis=2, tiled=False)]
    reshape x0 -> x1, local copies, waits for them, and re-layouts: none -> 7.28 us  [per_device(): all_refs = all_refs.reshape(STEPS, per_group, pixels)]
    unnamed x30 -> x31, local copies, waits for them, and re-layouts: 6.93 us -> 12.4 us
  transfers between devices with their start and end apart: 5 -> 5, of which waited for: 4 -> 3; matrix products, arithmetic and copies ran while one was open for 10% -> 11% of each run, Pallas kernels for 0% -> 20%
where the time goes in v8:
time: 349 us; the launch traced here: 348 us
  waiting for transfers between devices  149 us (43%)
  Pallas kernels  69.2 us (20%)
  local copies, waits for them, and re-layouts  44.8 us (13%)
  starting transfers between devices  25.8 us (7%)
  blocking collectives  20.7 us (6%)
  matrix products  16.2 us (5%)
  between operations  14.6 us (4%)
  other arithmetic  8.12 us (2%)
    all_to_all x1, waiting for transfers between devices, per_device(): got_img = lax.all_to_all(send_img, ('dom', 'cls'), 0, 0, tiled=True)  78.4 us
    pallas_call x1, Pallas kernels, shift_scores(): pl.pallas_call(_scores_kernel, grid=(steps,), in_specs=[pl.BlockSpec((ast...  69.2 us
    all_gather x1, waiting for transfers between devices, per_device(): all_refs = lax.all_gather(owner_chunk, 'dom', axis=2, tiled=False)  64.2 us
    all_gather x1, blocking collectives, per_device(): owner_chunk = lax.all_gather(mine, 'cls', axis=2, tiled=False)  20.7 us
    unnamed x31, local copies, waits for them, and re-layouts  12.4 us
    all_to_all x1, starting transfers between devices, per_device(): got_wts = lax.all_to_all(send_wts, ('dom', 'cls'), 0, 0, tiled=True)  11.7 us
    all_to_all x1, starting transfers between devices, per_device(): got_img = lax.all_to_all(send_img, ('dom', 'cls'), 0, 0, tiled=True)  10.2 us
    dot_general x1, matrix products, per_device(): lax.dot_general(got_wts, got_img, (((0, 2), (0, 2)), ((1,), (1,))), prefe...  9.67 us
  transfers between devices with their start and end apart: 5, of which 3 were waited for; matrix products, arithmetic and copies ran while one was open for 11% of the time, Pallas kernels for 20%

profile of v8, /device:TPU:1, one launch (start us, length us, event | category | flops | bytes accessed | tf_op | source)
XLA Modules:
  0.0 348.1 jit_solution(16886719245386313641)
XLA Ops:
  7.2 0.7 slice_bitcast_fusion.15
  8.3 0.8 slice_bitcast_fusion.14
  9.1 0.8 slice_bitcast_fusion.13
  10.0 0.2 select_reduce_fusion
  10.2 0.2 select_reduce_fusion.2
  10.3 0.7 multiply_add_fusion.3
  11.1 0.2 convolution_convert_fusion.12
  11.3 0.1 copy.88
  11.4 0.3 convolution_convert_fusion.11
  11.8 0.3 convolution_convert_fusion.10
  12.2 0.3 convolution_convert_fusion.9
  12.8 0.2 maximum_bitcast_fusion
  13.0 0.6 copy.169
  13.6 1.3 reshape.474
  14.9 11.7 %all-to-all-start = ((bf16[128,2,384]{2,1,0:T(2,128)(2,1)}), bf16[128,2,384]{2,1,0:T(2,128)(2,1)S(1)}, u32[]{:S(2)}, u32[]{:S(2)}) async-start(bf16[128,2,384]{2,1,0:T(2,128)(2,1)} %reshape.474), calls=%async_computation | async-start | bytes 393216 | tf_op jit(solution)/shard_map/all_to_all | solution.py:116
  26.8 0.5 fusion.5
  27.3 0.3 copy.103
  27.6 0.6 convolution_convert_fusion
  28.1 0.9 copy.129
  29.0 2.0 copy.165
  31.0 0.5 fusion.4
  31.5 0.3 copy.101
  31.8 0.6 convolution_convert_fusion.1
  32.4 0.9 copy.127
  33.3 2.0 copy.166
  35.4 0.5 fusion.3
  35.9 0.3 copy.99
  36.2 0.6 convolution_convert_fusion.2
  36.7 0.9 copy.125
  37.6 2.0 copy.167
  39.6 0.5 fusion.2
  40.1 0.3 copy.97
  40.4 0.6 convolution_convert_fusion.3
  41.0 0.9 copy.123
  41.9 1.1 copy.168
  43.0 0.4 copy-done.2
  43.4 0.5 copy-done.3
  43.9 0.8 pad_maximum_fusion
  44.7 7.5 %copy.105 = bf16[128,4,6,1024]{3,1,2,0:T(4,128)(2,1)} copy(bf16[128,4,6,1024]{3,0,2,1:T(8,128)(2,1)S(1)} %pad_maximum_fusion) | data formatting | bytes 12582912 | tf_op jit(solution)/shard_map/stack | solution.py:113
  52.2 10.2 %all-to-all-start.1 = ((bf16[128,4,6,1024]{3,1,2,0:T(4,128)(2,1)}), bf16[128,4,6,1024]{3,1,2,0:T(4,128)(2,1)}, u32[]{:S(2)}, u32[]{:S(2)}) async-start(bf16[128,4,6,1024]{3,1,2,0:T(4,128)(2,1)} %copy.105), calls=%async_computation.1 | async-start | bytes 12582912 | tf_op jit(solution)/shard_map/all_to_all | solution.py:115
  62.4 0.4 reshape.475
  62.8 0.8 convert_reduce_fusion
  63.6 78.4 %all-to-all-done.1 = bf16[128,4,6,1024]{3,1,2,0:T(4,128)(2,1)} async-done(((bf16[128,4,6,1024]{3,1,2,0:T(4,128)(2,1)}), bf16[128,4,6,1024]{3,1,2,0:T(4,128)(2,1)}, u32[]{:S(2)}, u32[]{:S(2)}) %all-to-all-start.1) | async-done | bytes 6291488 | tf_op jit(solution)/shard_map/all_to_all | solution.py:115
  142.0 9.7 %fusion.6 = f32[4,32,1024]{2,1,0:T(8,128)S(1)} fusion(bf16[128,4,6,1024]{3,1,2,0:T(4,128)(2,1)} %all-to-all-done.1, bf16[128,4,6,32]{3,1,2,0:T(4,128)(2,1)S(1)} %bitcast.213), kind=kOutput, calls=%fused_computation.21 | convolution fusion | flops 201326592 | bytes 7012352 | tf_op jit(solution)/shard_map/dot_general | solution.py:117
  151.7 1.0 convert_bitcast_fusion.3
  152.7 0.1 convert_bitcast_fusion.1
  152.8 0.7 convert_bitcast_fusion
  153.7 0.7 maximum_bitcast_fusion.1
  154.5 3.9 %all-to-all-start.2 = ((bf16[8,4,32,128]{3,2,1,0:T(8,128)(2,1)}), bf16[8,4,32,128]{3,2,1,0:T(8,128)(2,1)S(1)}, u32[]{:S(2)}, u32[]{:S(2)}) async-start(bf16[8,4,32,128]{3,2,1,0:T(8,128)(2,1)} %maximum_bitcast_fusion.1), calls=%async_computation.2 | async-start | bytes 524288 | tf_op jit(solution)/shard_map/all_to_all | solution.py:129
  158.4 0.1 copy.116
  158.6 6.1 %all-to-all-done.2 = bf16[8,4,32,128]{3,2,1,0:T(8,128)(2,1)S(1)} async-done(((bf16[8,4,32,128]{3,2,1,0:T(8,128)(2,1)}), bf16[8,4,32,128]{3,2,1,0:T(8,128)(2,1)S(1)}, u32[]{:S(2)}, u32[]{:S(2)}) %all-to-all-start.2) | async-done | bytes 262176 | tf_op jit(solution)/shard_map/all_to_all | solution.py:129
  164.7 0.3 fusion.23
  164.9 20.7 %all-gather = bf16[4,32,1024]{2,1,0:T(8,128)(2,1)S(1)} all-gather(bf16[4,32,128]{2,1,0:T(8,128)(2,1)S(1)} %convert_element_type.129), channel_id=2, replica_groups=mesh['dom'=16,'cls'=8] {'cls'}, dimensions={2}, use_global_device_ids=true | all-gather | bytes 294912 | tf_op jit(solution)/shard_map/all_gather | solution.py:133
  185.6 0.8 copy.134
  186.4 64.2 %all-gather.6.cloned.1.call-done = bf16[4,32,128,128]{3,2,1,0:T(8,128)(2,1)} async-done(((bf16[4,32,8,128]{3,2,1,0:T(8,128)(2,1)}), bf16[4,32,128,128]{3,2,1,0:T(8,128)(2,1)}) %all-gather.6.cloned.1.call-update) | async-done | bytes 4194320 | tf_op jit(solution)/shard_map/all_gather | solution.py:134
  250.6 7.3 %reshape.461 = bf16[4,32,16384]{2,1,0:T(8,128)(2,1)} reshape(bf16[4,32,128,128]{3,2,1,0:T(8,128)(2,1)} %all-gather.6.cloned.1.call-done) | data formatting | bytes 8388608 | tf_op jit(solution)/shard_map/reshape | solution.py:135
  258.0 0.6 fusion.33.sel_ref
  258.6 1.1 convolution_convert_fusion.8
  259.8 5.4 %copy.135 = bf16[16,8,128,128]{3,2,1,0:T(8,128)(2,1)} copy(bf16[16,8,128,128]{3,1,2,0:T(8,128)(2,1)} %bitcast.212) | data formatting | bytes 8388608
  265.2 69.2 %shard_map.95 = f32[4,32,16,128]{3,2,1,0:T(8,128)} custom-call(bf16[2,1024,128]{2,1,0:T(8,128)(2,1)} %bitcast.236, bf16[128,256]{1,0:T(8,128)(2,1)} %fusion.33.sel_ref, bf16[4,32,128,128]{3,2,1,0:T(8,128)(2,1)} %bitcast.226), custom_call_target="tpu_custom_call" | custom-call | flops 9663676416 | bytes 5767168 | tf_op jit(solution)/shard_map/pallas_call | solution.py:51
  334.4 1.3 fusion.9
  335.7 0.6 copy.112
  336.3 1.8 mul.224
  338.1 3.2 copy.119
  (63 shorter events, 1.5 us)
Async XLA Ops:
  12.8 13.8 %copy-start.7 = (s32[4,16]{1,0:T(4,128)S(1)}, s32[4,16]{1,0:T(4,128)}, u32[]{:S(2)}) copy-start(s32[4,16]{1,0:T(4,128)} %param.13) | copy-start | bytes 772
  12.8 13.8 %copy-start.5 = (bf16[16,16384]{1,0:T(8,128)(2,1)S(1)}, bf16[16,16384]{1,0:T(8,128)(2,1)}, u32[]{:S(2)}) copy-start(bf16[16,16384]{1,0:T(8,128)(2,1)} %param.8) | copy-start | bytes 1572868
  14.9 37.4 %all-to-all-start = ((bf16[128,2,384]{2,1,0:T(2,128)(2,1)}), bf16[128,2,384]{2,1,0:T(2,128)(2,1)S(1)}, u32[]{:S(2)}, u32[]{:S(2)}) async-start(bf16[128,2,384]{2,1,0:T(2,128)(2,1)} %reshape.474), calls=%async_computation | async-start | bytes 393216 | tf_op jit(solution)/shard_map/all_to_all | solution.py:116
  26.7 13.0 %copy-start = (bf16[2,8,128,128]{3,2,1,0:T(8,128)(2,1)}, bf16[2,8,128,128]{3,2,1,0:T(8,128)(2,1)S(1)}, u32[]{:S(2)}) copy-start(bf16[2,8,128,128]{3,2,1,0:T(8,128)(2,1)S(1)} %copy.120) | copy-start | bytes 1572868
  41.0 2.0 copy-start.4
  41.9 1.5 copy-start.2
  41.9 2.0 copy-start.3
  52.2 11.4 %copy-start.6 = (f32[32]{0:T(128)S(1)}, f32[32]{0:T(128)}, u32[]{:S(2)}) copy-start(f32[32]{0:T(128)} %param.10) | copy-start | bytes 388
  52.2 89.8 %all-to-all-start.1 = ((bf16[128,4,6,1024]{3,1,2,0:T(4,128)(2,1)}), bf16[128,4,6,1024]{3,1,2,0:T(4,128)(2,1)}, u32[]{:S(2)}, u32[]{:S(2)}) async-start(bf16[128,4,6,1024]{3,1,2,0:T(4,128)(2,1)} %copy.105), calls=%async_computation.1 | async-start | bytes 12582912 | tf_op jit(solution)/shard_map/all_to_all | solution.py:115
  151.7 6.7 %copy-start.8 = (s32[4]{0:T(128)S(1)}, s32[4]{0:T(128)}, u32[]{:S(2)}) copy-start(s32[4]{0:T(128)} %param.15) | copy-start | bytes 52
  154.5 10.2 %all-to-all-start.2 = ((bf16[8,4,32,128]{3,2,1,0:T(8,128)(2,1)}), bf16[8,4,32,128]{3,2,1,0:T(8,128)(2,1)S(1)}, u32[]{:S(2)}, u32[]{:S(2)}) async-start(bf16[8,4,32,128]{3,2,1,0:T(8,128)(2,1)} %maximum_bitcast_fusion.1), calls=%async_computation.2 | async-start | bytes 524288 | tf_op jit(solution)/shard_map/all_to_all | solution.py:129
  158.4 92.3 %all-gather.6.cloned.1.call-start = ((), (), s32[]{:S(2)}) async-start(), calls=%async_computation.3 | async-start | bytes 4456448 | tf_op jit(solution)/shard_map/all_gather | solution.py:134
  186.4 72.3 %copy-start.1 = (bf16[2,8,128,128]{3,2,1,0:T(8,128)(2,1)S(1)}, bf16[2,8,128,128]{3,2,1,0:T(8,128)(2,1)}, u32[]{:S(2)}) copy-start(bf16[2,8,128,128]{3,2,1,0:T(8,128)(2,1)} %copy-done) | copy-start | bytes 1572868
  186.4 151.7 %all-gather.8.cloned.1.call-start = ((), (), s32[]{:S(2)}) async-start(), calls=%async_computation.4 | async-start | bytes 2228224 | tf_op jit(solution)/shard_map/all_gather | solution.py:137
Sparse Core Ops, SparseCore 0:
  186.5 64.1 all-gather.5
  258.1 47.4 all-gather.7

commit v9 on v6

--- a/solution.py
+++ b/solution.py
@@ -14,25 +14,31 @@
 ASTEP = 2
 
 
-def _scores_kernel(pt_ref, sel_ref, r_ref, o_ref):
+def _scores_kernel(pt_ref, sel_ref, r_ref, o_ref, split_ref):
     classes = r_ref.shape[1]
+    radii = r_ref.shape[2]
     per_dev = o_ref.shape[2]
     lanes = o_ref.shape[3]
     parts = pt_ref.shape[0]
     pt = jnp.concatenate([pt_ref[e] for e in range(parts)], axis=1)
-    sel = sel_ref[...]
     rows = pt.shape[0] // per_dev
+    r_all = r_ref[0].reshape(classes * radii, r_ref.shape[3])
+    split_ref[...] = jnp.dot(r_all, sel_ref[...], preferred_element_type=jnp.float32).astype(split_ref.dtype)
 
-    def body(k, carry):
-        split = jnp.dot(r_ref[0, k], sel, preferred_element_type=jnp.float32).astype(pt.dtype)
-        rhs = jnp.concatenate([split[:, e * lanes:(e + 1) * lanes] for e in range(parts)], axis=0)
+    def body(j, carry):
+        halves = []
+        for h in range(2):
+            base = pl.multiple_of((2 * j + h) * radii, radii)
+            blk = split_ref[pl.ds(base, radii), :]
+            halves.append(jnp.concatenate([blk[:, e * lanes:(e + 1) * lanes] for e in range(parts)], axis=0))
+        rhs = jnp.concatenate(halves, axis=1)
         g = jnp.dot(pt, rhs, preferred_element_type=jnp.float32)
-        g = pltpu.roll(g, 0, 1, stride=1, stride_axis=0)
-        o_ref[0, k] = jnp.sum(g.reshape(per_dev, rows, lanes), axis=1)
+        for h in range(2):
+            gh = pltpu.roll(g[:, h * lanes:(h + 1) * lanes], 0, 1, stride=1, stride_axis=0)
+            o_ref[0, 2 * j + h] = jnp.sum(gh.reshape(per_dev, rows, lanes), axis=1)
         return carry
 
-    lax.fori_loop(0, classes, body, 0)
-
+    lax.fori_loop(0, classes // 2, body, 0)
 
 def shift_scores(cube, refs, astep):
     n, radii, angles = cube.shape
@@ -58,6 +64,7 @@
         ],
         out_specs=pl.BlockSpec((1, classes, n, 128), lambda s: (s, 0, 0, 0)),
         out_shape=jax.ShapeDtypeStruct((steps, classes, n, 128), jnp.float32),
+        scratch_shapes=[pltpu.VMEM((classes * radii, astep * 128), cube.dtype)],
         cost_estimate=pl.CostEstimate(flops=flops, transcendentals=0, bytes_accessed=pt.size * 2 + refs.size * 2 + steps * classes * n * 128 * 4),
     )(pt, sel, refs)[..., :turns]
 

time: 344 us -> 312 us (0.907)
  Pallas kernels: 69.2 us -> 37.6 us
    pallas_call x1, Pallas kernels: 69.2 us -> 37.6 us  [shift_scores(): pl.pallas_call(_scores_kernel, grid=(steps,), in_specs=[pl.BlockSpec((ast...]
where the time goes in v9:
time: 312 us
  waiting for transfers between devices  156 us (50%)
  Pallas kernels  37.6 us (12%)
  local copies, waits for them, and re-layouts  32 us (10%)
  starting transfers between devices  25.8 us (8%)
  blocking collectives  21.5 us (7%)
  matrix products  16.2 us (5%)
  between operations  14.6 us (5%)
  other arithmetic  8.12 us (3%)
    all_to_all x1, waiting for transfers between devices, per_device(): got_img = lax.all_to_all(send_img, ('dom', 'cls'), 0, 0, tiled=True)  78.3 us
    all_gather x1, waiting for transfers between devices, per_device(): all_refs = lax.all_gather(owner_chunk, 'dom', axis=2, tiled=False)  56.5 us
    pallas_call x1, Pallas kernels, shift_scores(): pl.pallas_call(_scores_kernel, grid=(steps,), in_specs=[pl.BlockSpec((ast...  37.6 us
    all_gather x1, blocking collectives, per_device(): owner_chunk = lax.all_gather(mine, 'cls', axis=2, tiled=False)  21.5 us
    all_gather x1, waiting for transfers between devices, per_device(): final = lax.all_gather(current, 'dom', axis=0, tiled=False)  14.9 us
    all_to_all x1, starting transfers between devices, per_device(): got_wts = lax.all_to_all(send_wts, ('dom', 'cls'), 0, 0, tiled=True)  11.7 us
    all_to_all x1, starting transfers between devices, per_device(): got_img = lax.all_to_all(send_img, ('dom', 'cls'), 0, 0, tiled=True)  10.2 us
    dot_general x1, matrix products, per_device(): lax.dot_general(got_wts, got_img, (((0, 2), (0, 2)), ((1,), (1,))), prefe...  9.67 us
  transfers between devices with their start and end apart: 5, of which 4 were waited for; matrix products, arithmetic and copies ran while one was open for 10% of the time, Pallas kernels for 0%

profile of v9, /device:TPU:1, one launch (start us, length us, event | category | flops | bytes accessed | tf_op | source)
XLA Modules:
  0.0 311.8 jit_solution(15009698977868491530)
XLA Ops:
  7.2 0.7 slice_bitcast_fusion.15
  8.3 0.8 slice_bitcast_fusion.14
  9.1 0.8 slice_bitcast_fusion.13
  10.0 0.2 select_reduce_fusion
  10.2 0.2 select_reduce_fusion.2
  10.3 0.7 multiply_add_fusion.3
  11.1 0.2 convolution_convert_fusion.12
  11.3 0.1 copy.88
  11.4 0.3 convolution_convert_fusion.11
  11.8 0.3 convolution_convert_fusion.10
  12.1 0.1 copy.92
  12.2 0.3 convolution_convert_fusion.9
  12.8 0.2 maximum_bitcast_fusion
  13.0 0.6 copy.168
  13.6 1.3 reshape.466
  14.9 11.7 %all-to-all-start = ((bf16[128,2,384]{2,1,0:T(2,128)(2,1)}), bf16[128,2,384]{2,1,0:T(2,128)(2,1)S(1)}, u32[]{:S(2)}, u32[]{:S(2)}) async-start(bf16[128,2,384]{2,1,0:T(2,128)(2,1)} %reshape.466), calls=%async_computation | async-start | bytes 393216 | tf_op jit(solution)/shard_map/all_to_all | solution.py:123
  26.8 0.5 fusion.5
  27.3 0.3 copy.103
  27.6 0.6 convolution_convert_fusion
  28.1 0.9 copy.129
  29.0 2.0 copy.164
  31.0 0.5 fusion.4
  31.5 0.3 copy.101
  31.8 0.6 convolution_convert_fusion.1
  32.4 0.9 copy.127
  33.3 2.0 copy.165
  35.4 0.5 fusion.3
  35.9 0.3 copy.99
  36.2 0.6 convolution_convert_fusion.2
  36.7 0.9 copy.125
  37.6 2.0 copy.166
  39.6 0.5 fusion.2
  40.1 0.3 copy.97
  40.4 0.6 convolution_convert_fusion.3
  41.0 0.9 copy.123
  41.9 1.1 copy.167
  43.0 0.4 copy-done.2
  43.4 0.5 copy-done.3
  43.9 0.8 pad_maximum_fusion
  44.7 7.5 %copy.105 = bf16[128,4,6,1024]{3,1,2,0:T(4,128)(2,1)} copy(bf16[128,4,6,1024]{3,0,2,1:T(8,128)(2,1)S(1)} %pad_maximum_fusion) | data formatting | bytes 12582912 | tf_op jit(solution)/shard_map/stack | solution.py:120
  52.2 10.2 %all-to-all-start.1 = ((bf16[128,4,6,1024]{3,1,2,0:T(4,128)(2,1)}), bf16[128,4,6,1024]{3,1,2,0:T(4,128)(2,1)}, u32[]{:S(2)}, u32[]{:S(2)}) async-start(bf16[128,4,6,1024]{3,1,2,0:T(4,128)(2,1)} %copy.105), calls=%async_computation.1 | async-start | bytes 12582912 | tf_op jit(solution)/shard_map/all_to_all | solution.py:122
  62.5 0.4 reshape.467
  62.8 0.8 convert_reduce_fusion
  63.7 78.3 %all-to-all-done.1 = bf16[128,4,6,1024]{3,1,2,0:T(4,128)(2,1)} async-done(((bf16[128,4,6,1024]{3,1,2,0:T(4,128)(2,1)}), bf16[128,4,6,1024]{3,1,2,0:T(4,128)(2,1)}, u32[]{:S(2)}, u32[]{:S(2)}) %all-to-all-start.1) | async-done | bytes 6291488 | tf_op jit(solution)/shard_map/all_to_all | solution.py:122
  142.0 9.7 %fusion.6 = f32[4,32,1024]{2,1,0:T(8,128)S(1)} fusion(bf16[128,4,6,1024]{3,1,2,0:T(4,128)(2,1)} %all-to-all-done.1, bf16[128,4,6,32]{3,1,2,0:T(4,128)(2,1)S(1)} %bitcast.206), kind=kOutput, calls=%fused_computation.21 | convolution fusion | flops 201326592 | bytes 7012352 | tf_op jit(solution)/shard_map/dot_general | solution.py:124
  151.7 1.0 convert_bitcast_fusion.3
  152.7 0.1 convert_bitcast_fusion.1
  152.8 0.7 convert_bitcast_fusion
  153.8 0.7 maximum_bitcast_fusion.1
  154.5 3.9 %all-to-all-start.2 = ((bf16[8,4,32,128]{3,2,1,0:T(8,128)(2,1)}), bf16[8,4,32,128]{3,2,1,0:T(8,128)(2,1)S(1)}, u32[]{:S(2)}, u32[]{:S(2)}) async-start(bf16[8,4,32,128]{3,2,1,0:T(8,128)(2,1)} %maximum_bitcast_fusion.1), calls=%async_computation.2 | async-start | bytes 524288 | tf_op jit(solution)/shard_map/all_to_all | solution.py:136
  158.5 0.1 copy.116
  158.6 6.1 %all-to-all-done.2 = bf16[8,4,32,128]{3,2,1,0:T(8,128)(2,1)S(1)} async-done(((bf16[8,4,32,128]{3,2,1,0:T(8,128)(2,1)}), bf16[8,4,32,128]{3,2,1,0:T(8,128)(2,1)S(1)}, u32[]{:S(2)}, u32[]{:S(2)}) %all-to-all-start.2) | async-done | bytes 262176 | tf_op jit(solution)/shard_map/all_to_all | solution.py:136
  164.7 0.3 fusion.23
  165.0 21.5 %all-gather = bf16[4,32,1024]{2,1,0:T(8,128)(2,1)S(1)} all-gather(bf16[4,32,128]{2,1,0:T(8,128)(2,1)S(1)} %convert_element_type.129), channel_id=2, replica_groups=mesh['dom'=16,'cls'=8] {'cls'}, dimensions={2}, use_global_device_ids=true | all-gather | bytes 294912 | tf_op jit(solution)/shard_map/all_gather | solution.py:140
  186.5 0.7 copy.134
  187.3 0.6 fusion.33.sel_ref
  187.9 1.1 convolution_convert_fusion.8
  189.0 14.9 %all-gather.8.cloned.1.call-done = f32[512,1024]{1,0:T(8,128)} async-done(((f32[32,1024]{1,0:T(8,128)}), f32[512,1024]{1,0:T(8,128)}) %all-gather.8.cloned.1.call-update) | async-done | bytes 2097168 | tf_op jit(solution)/shard_map/all_gather | solution.py:143
  203.9 3.2 %copy.119 = f32[16,4,8,1024]{3,2,0,1:T(8,128)} copy(f32[16,4,8,1024]{3,2,1,0:T(8,128)} %bitcast.224) | data formatting | bytes 4194304 | tf_op jit(solution)/shard_map/reshape | solution.py:144
  207.1 56.5 %all-gather.6.cloned.1.call-done.r_ref = bf16[4,32,128,128]{3,2,1,0:T(8,128)(2,1)} async-done(((bf16[4,32,8,128]{3,2,1,0:T(8,128)(2,1)}), bf16[4,32,128,128]{3,2,1,0:T(8,128)(2,1)}) %all-gather.6.cloned.1.call-update) | async-done | bytes 4194320 | tf_op jit(solution)/shard_map/all_gather | solution.py:141
  263.6 37.6 %shard_map.95 = f32[4,32,16,128]{3,2,1,0:T(8,128)} custom-call(bf16[2,1024,128]{2,1,0:T(8,128)(2,1)} %bitcast.228, bf16[128,256]{1,0:T(8,128)(2,1)} %fusion.33.sel_ref, bf16[4,32,128,128]{3,2,1,0:T(8,128)(2,1)} %all-gather.6.cloned.1.call-done.r_ref), custom_call_target="tpu_custom_call" | custom-call | flops 9663676416 | bytes 5767168 | tf_op jit(solution)/shard_map/pallas_call | solution.py:57
  301.2 1.3 fusion.9
  302.5 0.6 copy.112
  303.2 1.8 mul.224
  (61 shorter events, 1.4 us)
Async XLA Ops:
  12.8 13.8 %copy-start.7 = (s32[4,16]{1,0:T(4,128)S(1)}, s32[4,16]{1,0:T(4,128)}, u32[]{:S(2)}) copy-start(s32[4,16]{1,0:T(4,128)} %param.13) | copy-start | bytes 772
  12.8 13.8 %copy-start.5 = (bf16[16,16384]{1,0:T(8,128)(2,1)S(1)}, bf16[16,16384]{1,0:T(8,128)(2,1)}, u32[]{:S(2)}) copy-start(bf16[16,16384]{1,0:T(8,128)(2,1)} %param.8) | copy-start | bytes 1572868
  14.9 37.4 %all-to-all-start = ((bf16[128,2,384]{2,1,0:T(2,128)(2,1)}), bf16[128,2,384]{2,1,0:T(2,128)(2,1)S(1)}, u32[]{:S(2)}, u32[]{:S(2)}) async-start(bf16[128,2,384]{2,1,0:T(2,128)(2,1)} %reshape.466), calls=%async_computation | async-start | bytes 393216 | tf_op jit(solution)/shard_map/all_to_all | solution.py:123
  26.7 13.0 %copy-start = (bf16[2,8,128,128]{3,2,1,0:T(8,128)(2,1)}, bf16[2,8,128,128]{3,2,1,0:T(8,128)(2,1)S(1)}, u32[]{:S(2)}) copy-start(bf16[2,8,128,128]{3,2,1,0:T(8,128)(2,1)S(1)} %copy.120) | copy-start | bytes 1572868
  41.0 2.0 copy-start.4
  41.9 1.5 copy-start.2
  41.9 2.0 copy-start.3
  52.2 11.4 %copy-start.6 = (f32[32]{0:T(128)S(1)}, f32[32]{0:T(128)}, u32[]{:S(2)}) copy-start(f32[32]{0:T(128)} %param.10) | copy-start | bytes 388
  52.2 89.8 %all-to-all-start.1 = ((bf16[128,4,6,1024]{3,1,2,0:T(4,128)(2,1)}), bf16[128,4,6,1024]{3,1,2,0:T(4,128)(2,1)}, u32[]{:S(2)}, u32[]{:S(2)}) async-start(bf16[128,4,6,1024]{3,1,2,0:T(4,128)(2,1)} %copy.105), calls=%async_computation.1 | async-start | bytes 12582912 | tf_op jit(solution)/shard_map/all_to_all | solution.py:122
  62.4 141.5 %all-gather.8.cloned.1.call-start = ((), (), s32[]{:S(2)}) async-start(), calls=%async_computation.4 | async-start | bytes 2228224 | tf_op jit(solution)/shard_map/all_gather | solution.py:143
  151.7 6.8 %copy-start.8 = (s32[4]{0:T(128)S(1)}, s32[4]{0:T(128)}, u32[]{:S(2)}) copy-start(s32[4]{0:T(128)} %param.15) | copy-start | bytes 52
  152.8 35.1 %copy-start.1 = (bf16[2,8,128,128]{3,2,1,0:T(8,128)(2,1)S(1)}, bf16[2,8,128,128]{3,2,1,0:T(8,128)(2,1)}, u32[]{:S(2)}) copy-start(bf16[2,8,128,128]{3,2,1,0:T(8,128)(2,1)} %copy-done) | copy-start | bytes 1572868
  154.5 10.2 %all-to-all-start.2 = ((bf16[8,4,32,128]{3,2,1,0:T(8,128)(2,1)}), bf16[8,4,32,128]{3,2,1,0:T(8,128)(2,1)S(1)}, u32[]{:S(2)}, u32[]{:S(2)}) async-start(bf16[8,4,32,128]{3,2,1,0:T(8,128)(2,1)} %maximum_bitcast_fusion.1), calls=%async_computation.2 | async-start | bytes 524288 | tf_op jit(solution)/shard_map/all_to_all | solution.py:136
  158.4 105.2 %all-gather.6.cloned.1.call-start = ((), (), s32[]{:S(2)}) async-start(), calls=%async_computation.3 | async-start | bytes 4456448 | tf_op jit(solution)/shard_map/all_gather | solution.py:141
Sparse Core Ops, SparseCore 0:
  153.7 50.1 all-gather.7
  206.2 57.4 all-gather.5

commit v10 on v9

--- a/solution.py
+++ b/solution.py
@@ -131,15 +131,15 @@
     for step in range(STEPS):
         current = (prior_mass[:, None] * current + totals[step]) / (prior_mass + mass[step])[:, None]
         ref_chunks.append(current.astype(jnp.bfloat16))
-    rows = chunk // ANGLES
-    ref_chunks = jnp.stack(ref_chunks, axis=0).reshape(STEPS, per_group, groups, rows // groups * ANGLES)
-    got_refs = lax.all_to_all(ref_chunks.transpose(2, 0, 1, 3), "cls", 0, 0, tiled=True)
+    ref_chunks = jnp.stack(ref_chunks, axis=0)
+    ref_chunks = jnp.broadcast_to(ref_chunks[None], (groups,) + ref_chunks.shape)
+    got_refs = lax.all_to_all(ref_chunks, "cls", 0, 0, tiled=True)
     owner_hot = (owners[None, :] == jnp.arange(groups, dtype=jnp.int32)[:, None]).astype(jnp.bfloat16)
-    mine = jnp.einsum("gs,gskp->skp", owner_hot, got_refs, preferred_element_type=jnp.float32)
-    mine = mine.astype(jnp.bfloat16)
-    owner_chunk = lax.all_gather(mine, "cls", axis=2, tiled=False)
+    owner_chunk = jnp.einsum("gs,gskp->skp", owner_hot, got_refs, preferred_element_type=jnp.float32)
+    owner_chunk = owner_chunk.astype(jnp.bfloat16)
     all_refs = lax.all_gather(owner_chunk, "dom", axis=2, tiled=False)
     all_refs = all_refs.reshape(STEPS, per_group, pixels)
+    current = current + 0.0 * all_refs[0, 0, 0].astype(jnp.float32)
     final = lax.all_gather(current, "dom", axis=0, tiled=False)
     final = final.transpose(1, 0, 2).reshape(per_group, pixels)
 

time: 312 us -> 308 us (0.987)
  blocking collectives: 21.5 us -> 0 us
  local copies, waits for them, and re-layouts: 32 us -> 40.2 us
  waiting for transfers between devices: 156 us -> 163 us
    all_gather x1 -> x0, blocking collectives: 21.5 us -> none  [per_device(): owner_chunk = lax.all_gather(mine, 'cls', axis=2, tiled=False)]
    all_to_all x1, waiting for transfers between devices: 6.11 us -> 26.8 us  [per_device(): got_refs = lax.all_to_all(ref_chunks, 'cls', 0, 0, tiled=True)]
    all_gather x1, waiting for transfers between devices: 14.9 us -> 0.01 us  [per_device(): final = lax.all_gather(current, 'dom', axis=0, tiled=False)]
    unnamed x30 -> x26, local copies, waits for them, and re-layouts: 6.93 us -> 11.6 us
  transfers between devices with their start and end apart: 5 -> 5, of which waited for: 4 -> 3; matrix products, arithmetic and copies ran while one was open for 10% -> 12% of each run, Pallas kernels for 0% -> 12%
where the time goes in v10:
time: 308 us; the launch traced here: 307 us
  waiting for transfers between devices  163 us (53%)
  local copies, waits for them, and re-layouts  40.2 us (13%)
  Pallas kernels  37.6 us (12%)
  starting transfers between devices  26 us (8%)
  matrix products  17.4 us (6%)
  between operations  15.2 us (5%)
  other arithmetic  7.42 us (2%)
    all_to_all x1, waiting for transfers between devices, per_device(): got_img = lax.all_to_all(send_img, ('dom', 'cls'), 0, 0, tiled=True)  78.4 us
    all_gather x1, waiting for transfers between devices, per_device(): all_refs = lax.all_gather(owner_chunk, 'dom', axis=2, tiled=False)  58.1 us
    pallas_call x1, Pallas kernels, shift_scores(): pl.pallas_call(_scores_kernel, grid=(steps,), in_specs=[pl.BlockSpec((ast...  37.6 us
    all_to_all x1, waiting for transfers between devices, per_device(): got_refs = lax.all_to_all(ref_chunks, 'cls', 0, 0, tiled=True)  26.8 us
    all_to_all x1, starting transfers between devices, per_device(): got_wts = lax.all_to_all(send_wts, ('dom', 'cls'), 0, 0, tiled=True)  11.7 us
    unnamed x26, local copies, waits for them, and re-layouts  11.6 us
    all_to_all x1, starting transfers between devices, per_device(): got_img = lax.all_to_all(send_img, ('dom', 'cls'), 0, 0, tiled=True)  10.2 us
    dot_general x1, matrix products, per_device(): lax.dot_general(got_wts, got_img, (((0, 2), (0, 2)), ((1,), (1,))), prefe...  9.67 us
  transfers between devices with their start and end apart: 5, of which 3 were waited for; matrix products, arithmetic and copies ran while one was open for 12% of the time, Pallas kernels for 12%

profile of v10, /device:TPU:1, one launch (start us, length us, event | category | flops | bytes accessed | tf_op | source)
XLA Modules:
  0.0 307.0 jit_solution(11559584902829198764)
XLA Ops:
  7.2 0.7 slice_bitcast_fusion.15
  8.3 0.8 slice_bitcast_fusion.14
  9.1 0.8 slice_bitcast_fusion.13
  10.0 0.2 select_reduce_fusion
  10.2 0.2 select_reduce_fusion.2
  10.3 0.7 multiply_add_fusion.3
  11.1 0.2 convolution_convert_fusion.12
  11.3 0.1 copy.80
  11.4 0.3 convolution_convert_fusion.11
  11.8 0.3 convolution_convert_fusion.10
  12.2 0.3 convolution_convert_fusion.9
  12.8 0.2 maximum_bitcast_fusion
  13.0 0.6 copy.154
  13.6 1.3 reshape.465
  14.9 11.7 %all-to-all-start = ((bf16[128,2,384]{2,1,0:T(2,128)(2,1)}), bf16[128,2,384]{2,1,0:T(2,128)(2,1)S(1)}, u32[]{:S(2)}, u32[]{:S(2)}) async-start(bf16[128,2,384]{2,1,0:T(2,128)(2,1)} %reshape.465), calls=%async_computation | async-start | bytes 393216 | tf_op jit(solution)/shard_map/all_to_all | solution.py:123
  26.8 0.5 fusion.7
  27.3 0.3 copy.95
  27.6 0.6 convolution_convert_fusion
  28.1 0.9 copy.117
  29.0 2.0 copy.149
  31.0 0.5 fusion.6
  31.5 0.3 copy.93
  31.8 0.6 convolution_convert_fusion.1
  32.4 0.9 copy.115
  33.3 2.0 copy.150
  35.4 0.5 fusion.5
  35.9 0.3 copy.91
  36.2 0.6 convolution_convert_fusion.2
  36.7 0.9 copy.113
  37.6 2.0 copy.151
  39.6 0.5 fusion.4
  40.1 0.3 copy.89
  40.4 0.6 convolution_convert_fusion.3
  41.0 0.9 copy.111
  41.9 1.1 copy.152
  43.0 0.4 copy-done.2
  43.4 0.5 copy-done.3
  43.9 0.8 pad_maximum_fusion
  44.7 7.5 %copy.97 = bf16[128,4,6,1024]{3,1,2,0:T(4,128)(2,1)} copy(bf16[128,4,6,1024]{3,0,2,1:T(8,128)(2,1)S(1)} %pad_maximum_fusion) | data formatting | bytes 12582912 | tf_op jit(solution)/shard_map/stack | solution.py:120
  52.2 10.2 %all-to-all-start.1 = ((bf16[128,4,6,1024]{3,1,2,0:T(4,128)(2,1)}), bf16[128,4,6,1024]{3,1,2,0:T(4,128)(2,1)}, u32[]{:S(2)}, u32[]{:S(2)}) async-start(bf16[128,4,6,1024]{3,1,2,0:T(4,128)(2,1)} %copy.97), calls=%async_computation.1 | async-start | bytes 12582912 | tf_op jit(solution)/shard_map/all_to_all | solution.py:122
  62.4 0.4 reshape.466
  62.8 0.8 convert_reduce_fusion
  63.6 78.4 %all-to-all-done.1 = bf16[128,4,6,1024]{3,1,2,0:T(4,128)(2,1)} async-done(((bf16[128,4,6,1024]{3,1,2,0:T(4,128)(2,1)}), bf16[128,4,6,1024]{3,1,2,0:T(4,128)(2,1)}, u32[]{:S(2)}, u32[]{:S(2)}) %all-to-all-start.1) | async-done | bytes 6291488 | tf_op jit(solution)/shard_map/all_to_all | solution.py:122
  142.0 9.7 %fusion.8 = f32[4,32,1024]{2,1,0:T(8,128)S(1)} fusion(bf16[128,4,6,1024]{3,1,2,0:T(4,128)(2,1)} %all-to-all-done.1, bf16[128,4,6,32]{3,1,2,0:T(4,128)(2,1)S(1)} %bitcast.198), kind=kOutput, calls=%fused_computation.23 | convolution fusion | flops 201326592 | bytes 7012352 | tf_op jit(solution)/shard_map/dot_general | solution.py:124
  151.7 1.0 convert_bitcast_fusion.3
  152.7 0.1 convert_bitcast_fusion.1
  152.8 0.1 convert_bitcast_fusion
  152.9 1.6 broadcast_in_dim.2
  154.5 4.0 %all-to-all-start.2 = ((bf16[8,4,32,1024]{3,2,1,0:T(8,128)(2,1)}), bf16[8,4,32,1024]{3,2,1,0:T(8,128)(2,1)S(1)}, u32[]{:S(2)}, u32[]{:S(2)}) async-start(bf16[8,4,32,1024]{3,2,1,0:T(8,128)(2,1)} %broadcast_in_dim.2), calls=%async_computation.2 | async-start | bytes 4194304 | tf_op jit(solution)/shard_map/all_to_all | solution.py:136
  158.7 0.1 copy.104
  158.8 26.8 %all-to-all-done.2 = bf16[8,4,32,1024]{3,2,1,0:T(8,128)(2,1)S(1)} async-done(((bf16[8,4,32,1024]{3,2,1,0:T(8,128)(2,1)}), bf16[8,4,32,1024]{3,2,1,0:T(8,128)(2,1)S(1)}, u32[]{:S(2)}, u32[]{:S(2)}) %all-to-all-start.2) | async-done | bytes 2097184 | tf_op jit(solution)/shard_map/all_to_all | solution.py:136
  185.6 1.4 fusion.2
  187.0 0.8 copy.153
  187.9 58.1 %all-gather.5.cloned.1.call-done = bf16[4,32,16384]{2,1,0:T(8,128)(2,1)} async-done(((bf16[4,32,1024]{2,1,0:T(8,128)(2,1)}), bf16[4,32,16384]{2,1,0:T(8,128)(2,1)}) %all-gather.5.cloned.1.call-update) | async-done | bytes 4194320 | tf_op jit(solution)/shard_map/all_gather | solution.py:140
  246.0 1.2 slice.109
  247.8 0.7 broadcast_add_fusion
  248.5 0.6 fusion.33.sel_ref
  249.2 1.1 convolution_convert_fusion.8
  250.3 5.4 %copy.118 = bf16[16,8,128,128]{3,2,1,0:T(8,128)(2,1)} copy(bf16[16,8,128,128]{3,1,2,0:T(8,128)(2,1)} %bitcast.211) | data formatting | bytes 8388608
  255.7 37.6 %shard_map.95 = f32[4,32,16,128]{3,2,1,0:T(8,128)} custom-call(bf16[2,1024,128]{2,1,0:T(8,128)(2,1)} %bitcast.221, bf16[128,256]{1,0:T(8,128)(2,1)} %fusion.33.sel_ref, bf16[4,32,128,128]{3,2,1,0:T(8,128)(2,1)} %bitcast.212), custom_call_target="tpu_custom_call" | custom-call | flops 9663676416 | bytes 5767168 | tf_op jit(solution)/shard_map/pallas_call | solution.py:57
  293.3 1.3 fusion.11
  294.6 0.6 copy.100
  295.3 1.8 mul.230
  297.0 3.2 %copy.107 = f32[16,4,8,1024]{3,2,0,1:T(8,128)} copy(f32[16,4,8,1024]{3,2,1,0:T(8,128)} %bitcast.218) | data formatting | bytes 4194304 | tf_op jit(solution)/shard_map/reshape | solution.py:144
  (55 shorter events, 1.4 us)
Async XLA Ops:
  12.8 13.8 %copy-start.7 = (s32[4,16]{1,0:T(4,128)S(1)}, s32[4,16]{1,0:T(4,128)}, u32[]{:S(2)}) copy-start(s32[4,16]{1,0:T(4,128)} %param.13) | copy-start | bytes 772
  12.8 13.8 %copy-start.5 = (bf16[16,16384]{1,0:T(8,128)(2,1)S(1)}, bf16[16,16384]{1,0:T(8,128)(2,1)}, u32[]{:S(2)}) copy-start(bf16[16,16384]{1,0:T(8,128)(2,1)} %param.8) | copy-start | bytes 1572868
  14.9 37.4 %all-to-all-start = ((bf16[128,2,384]{2,1,0:T(2,128)(2,1)}), bf16[128,2,384]{2,1,0:T(2,128)(2,1)S(1)}, u32[]{:S(2)}, u32[]{:S(2)}) async-start(bf16[128,2,384]{2,1,0:T(2,128)(2,1)} %reshape.465), calls=%async_computation | async-start | bytes 393216 | tf_op jit(solution)/shard_map/all_to_all | solution.py:123
  26.7 13.0 %copy-start = (bf16[2,8,128,128]{3,2,1,0:T(8,128)(2,1)}, bf16[2,8,128,128]{3,2,1,0:T(8,128)(2,1)S(1)}, u32[]{:S(2)}) copy-start(bf16[2,8,128,128]{3,2,1,0:T(8,128)(2,1)S(1)} %copy.108) | copy-start | bytes 1572868
  41.0 2.0 copy-start.4
  41.9 1.5 copy-start.2
  41.9 2.0 copy-start.3
  52.2 11.4 %copy-start.6 = (f32[32]{0:T(128)S(1)}, f32[32]{0:T(128)}, u32[]{:S(2)}) copy-start(f32[32]{0:T(128)} %param.10) | copy-start | bytes 388
  52.2 89.8 %all-to-all-start.1 = ((bf16[128,4,6,1024]{3,1,2,0:T(4,128)(2,1)}), bf16[128,4,6,1024]{3,1,2,0:T(4,128)(2,1)}, u32[]{:S(2)}, u32[]{:S(2)}) async-start(bf16[128,4,6,1024]{3,1,2,0:T(4,128)(2,1)} %copy.97), calls=%async_computation.1 | async-start | bytes 12582912 | tf_op jit(solution)/shard_map/all_to_all | solution.py:122
  154.5 4.1 %copy-start.8 = (s32[4]{0:T(128)S(1)}, s32[4]{0:T(128)}, u32[]{:S(2)}) copy-start(s32[4]{0:T(128)} %param.15) | copy-start | bytes 52
  154.5 31.1 %all-to-all-start.2 = ((bf16[8,4,32,1024]{3,2,1,0:T(8,128)(2,1)}), bf16[8,4,32,1024]{3,2,1,0:T(8,128)(2,1)S(1)}, u32[]{:S(2)}, u32[]{:S(2)}) async-start(bf16[8,4,32,1024]{3,2,1,0:T(8,128)(2,1)} %broadcast_in_dim.2), calls=%async_computation.2 | async-start | bytes 4194304 | tf_op jit(solution)/shard_map/all_to_all | solution.py:136
  158.6 90.6 %copy-start.1 = (bf16[2,8,128,128]{3,2,1,0:T(8,128)(2,1)S(1)}, bf16[2,8,128,128]{3,2,1,0:T(8,128)(2,1)}, u32[]{:S(2)}) copy-start(bf16[2,8,128,128]{3,2,1,0:T(8,128)(2,1)} %copy-done) | copy-start | bytes 1572868
  158.6 87.4 %all-gather.5.cloned.1.call-start = ((), (), s32[]{:S(2)}) async-start(), calls=%async_computation.3 | async-start | bytes 4456448 | tf_op jit(solution)/shard_map/all_gather | solution.py:140
  187.9 109.2 %all-gather.7.cloned.1.call-start = ((), (), s32[]{:S(2)}) async-start(), calls=%async_computation.4 | async-start | bytes 2228224 | tf_op jit(solution)/shard_map/all_gather | solution.py:143
Sparse Core Ops, SparseCore 0:
  188.0 57.9 all-gather.4
  248.6 47.0 all-gather.6

commit v11 on v10

--- a/solution.py
+++ b/solution.py
@@ -131,17 +131,16 @@
     for step in range(STEPS):
         current = (prior_mass[:, None] * current + totals[step]) / (prior_mass + mass[step])[:, None]
         ref_chunks.append(current.astype(jnp.bfloat16))
-    ref_chunks = jnp.stack(ref_chunks, axis=0)
+    ref_chunks = jnp.stack(ref_chunks, axis=0).reshape(STEPS, per_group, chunk // ANGLES, ANGLES)
     ref_chunks = jnp.broadcast_to(ref_chunks[None], (groups,) + ref_chunks.shape)
     got_refs = lax.all_to_all(ref_chunks, "cls", 0, 0, tiled=True)
     owner_hot = (owners[None, :] == jnp.arange(groups, dtype=jnp.int32)[:, None]).astype(jnp.bfloat16)
-    owner_chunk = jnp.einsum("gs,gskp->skp", owner_hot, got_refs, preferred_element_type=jnp.float32)
+    owner_chunk = jnp.einsum("gs,gskrc->skrc", owner_hot, got_refs, preferred_element_type=jnp.float32)
     owner_chunk = owner_chunk.astype(jnp.bfloat16)
     all_refs = lax.all_gather(owner_chunk, "dom", axis=2, tiled=False)
     all_refs = all_refs.reshape(STEPS, per_group, pixels)
     current = current + 0.0 * all_refs[0, 0, 0].astype(jnp.float32)
-    final = lax.all_gather(current, "dom", axis=0, tiled=False)
-    final = final.transpose(1, 0, 2).reshape(per_group, pixels)
+    final = lax.all_gather(current, "dom", axis=1, tiled=False).reshape(per_group, pixels)
 
     shifted = shift_scores(cube, all_refs.reshape(STEPS, per_group, RADII, ANGLES), ASTEP)
     scores = shifted.transpose(0, 2, 3, 1).reshape(STEPS, per_dev, ROT * per_group)

time: 308 us -> 317 us (1.029)
  waiting for transfers between devices: 163 us -> 170 us
    reshape x1, local copies, waits for them, and re-layouts: 3.16 us -> 7.33 us  [per_device(): all_refs = all_refs.reshape(STEPS, per_group, pixels)]
    all_gather x1, waiting for transfers between devices: 0.01 us -> 4.02 us  [per_device(): lax.all_gather(current, 'dom', axis=1, tiled=False)]
    unnamed x26 -> x30, local copies, waits for them, and re-layouts: 11.6 us -> 9.23 us
  transfers between devices with their start and end apart: 5 -> 5, of which waited for: 3 -> 4; matrix products, arithmetic and copies ran while one was open for 12% -> 10% of each run, Pallas kernels for 12% -> 12%
where the time goes in v11:
time: 317 us; the launch traced here: 316 us
  waiting for transfers between devices  170 us (54%)
  local copies, waits for them, and re-layouts  41.4 us (13%)
  Pallas kernels  37.6 us (12%)
  starting transfers between devices  26 us (8%)
  matrix products  17.4 us (5%)
  between operations  15.2 us (5%)
  other arithmetic  8.17 us (3%)
    all_to_all x1, waiting for transfers between devices, per_device(): got_img = lax.all_to_all(send_img, ('dom', 'cls'), 0, 0, tiled=True)  78.4 us
    all_gather x1, waiting for transfers between devices, per_device(): all_refs = lax.all_gather(owner_chunk, 'dom', axis=2, tiled=False)  61.2 us
    pallas_call x1, Pallas kernels, shift_scores(): pl.pallas_call(_scores_kernel, grid=(steps,), in_specs=[pl.BlockSpec((ast...  37.6 us
    all_to_all x1, waiting for transfers between devices, per_device(): got_refs = lax.all_to_all(ref_chunks, 'cls', 0, 0, tiled=True)  26.9 us
    all_to_all x1, starting transfers between devices, per_device(): got_wts = lax.all_to_all(send_wts, ('dom', 'cls'), 0, 0, tiled=True)  11.7 us
    all_to_all x1, starting transfers between devices, per_device(): got_img = lax.all_to_all(send_img, ('dom', 'cls'), 0, 0, tiled=True)  10.2 us
    dot_general x1, matrix products, per_device(): lax.dot_general(got_wts, got_img, (((0, 2), (0, 2)), ((1,), (1,))), prefe...  9.67 us
    unnamed x30, local copies, waits for them, and re-layouts  9.23 us
  transfers between devices with their start and end apart: 5, of which 4 were waited for; matrix products, arithmetic and copies ran while one was open for 10% of the time, Pallas kernels for 12%

profile of v11, /device:TPU:1, one launch (start us, length us, event | category | flops | bytes accessed | tf_op | source)
XLA Modules:
  0.0 316.1 jit_solution(9126314956410507849)
XLA Ops:
  7.2 0.7 slice_bitcast_fusion.15
  8.3 0.8 slice_bitcast_fusion.14
  9.1 0.8 slice_bitcast_fusion.13
  10.0 0.2 select_reduce_fusion
  10.2 0.2 select_reduce_fusion.2
  10.3 0.7 multiply_add_fusion.3
  11.1 0.2 convolution_convert_fusion.12
  11.4 0.3 convolution_convert_fusion.11
  11.8 0.3 convolution_convert_fusion.10
  12.2 0.3 convolution_convert_fusion.9
  12.8 0.2 maximum_bitcast_fusion
  13.0 0.6 copy.149
  13.6 1.3 reshape.473
  14.9 11.7 %all-to-all-start = ((bf16[128,2,384]{2,1,0:T(2,128)(2,1)}), bf16[128,2,384]{2,1,0:T(2,128)(2,1)S(1)}, u32[]{:S(2)}, u32[]{:S(2)}) async-start(bf16[128,2,384]{2,1,0:T(2,128)(2,1)} %reshape.473), calls=%async_computation | async-start | bytes 393216 | tf_op jit(solution)/shard_map/all_to_all | solution.py:123
  26.8 0.5 fusion.7
  27.3 0.3 copy.91
  27.6 0.6 convolution_convert_fusion
  28.1 0.9 copy.111
  29.0 2.0 copy.145
  31.0 0.5 fusion.6
  31.5 0.3 copy.89
  31.8 0.6 convolution_convert_fusion.1
  32.4 0.9 copy.109
  33.3 2.0 copy.146
  35.4 0.5 fusion.5
  35.9 0.3 copy.87
  36.2 0.6 convolution_convert_fusion.2
  36.7 0.9 copy.107
  37.6 2.0 copy.147
  39.6 0.5 fusion.4
  40.1 0.3 copy.85
  40.4 0.6 convolution_convert_fusion.3
  41.0 0.9 copy.105
  41.9 1.1 copy.148
  43.0 0.4 copy-done.2
  43.4 0.5 copy-done.3
  43.9 0.8 pad_maximum_fusion
  44.7 7.5 %copy.93 = bf16[128,4,6,1024]{3,1,2,0:T(4,128)(2,1)} copy(bf16[128,4,6,1024]{3,0,2,1:T(8,128)(2,1)S(1)} %pad_maximum_fusion) | data formatting | bytes 12582912 | tf_op jit(solution)/shard_map/stack | solution.py:120
  52.2 10.2 %all-to-all-start.1 = ((bf16[128,4,6,1024]{3,1,2,0:T(4,128)(2,1)}), bf16[128,4,6,1024]{3,1,2,0:T(4,128)(2,1)}, u32[]{:S(2)}, u32[]{:S(2)}) async-start(bf16[128,4,6,1024]{3,1,2,0:T(4,128)(2,1)} %copy.93), calls=%async_computation.1 | async-start | bytes 12582912 | tf_op jit(solution)/shard_map/all_to_all | solution.py:122
  62.4 0.4 reshape.474
  62.8 0.8 convert_reduce_fusion
  63.6 78.4 %all-to-all-done.1 = bf16[128,4,6,1024]{3,1,2,0:T(4,128)(2,1)} async-done(((bf16[128,4,6,1024]{3,1,2,0:T(4,128)(2,1)}), bf16[128,4,6,1024]{3,1,2,0:T(4,128)(2,1)}, u32[]{:S(2)}, u32[]{:S(2)}) %all-to-all-start.1) | async-done | bytes 6291488 | tf_op jit(solution)/shard_map/all_to_all | solution.py:122
  142.0 9.7 %fusion.8 = f32[4,32,1024]{2,1,0:T(8,128)S(1)} fusion(bf16[128,4,6,1024]{3,1,2,0:T(4,128)(2,1)} %all-to-all-done.1, bf16[128,4,6,32]{3,1,2,0:T(4,128)(2,1)S(1)} %bitcast.200), kind=kOutput, calls=%fused_computation.23 | convolution fusion | flops 201326592 | bytes 7012352 | tf_op jit(solution)/shard_map/dot_general | solution.py:124
  151.7 1.0 convert_bitcast_fusion.3
  152.7 0.1 convert_bitcast_fusion.1
  152.8 0.1 convert_bitcast_fusion
  153.0 1.8 broadcast_in_dim.5
  154.8 4.0 %all-to-all-start.2 = ((bf16[8,4,32,8,128]{4,3,2,1,0:T(8,128)(2,1)}), bf16[8,4,32,8,128]{4,3,2,1,0:T(8,128)(2,1)S(1)}, u32[]{:S(2)}, u32[]{:S(2)}) async-start(bf16[8,4,32,8,128]{4,3,2,1,0:T(8,128)(2,1)} %broadcast_in_dim.5), calls=%async_computation.2 | async-start | bytes 4194304 | tf_op jit(solution)/shard_map/all_to_all | solution.py:136
  158.9 0.1 copy.99
  159.1 26.9 %all-to-all-done.2 = bf16[8,4,32,8,128]{4,3,2,1,0:T(8,128)(2,1)S(1)} async-done(((bf16[8,4,32,8,128]{4,3,2,1,0:T(8,128)(2,1)}), bf16[8,4,32,8,128]{4,3,2,1,0:T(8,128)(2,1)S(1)}, u32[]{:S(2)}, u32[]{:S(2)}) %all-to-all-start.2) | async-done | bytes 2097184 | tf_op jit(solution)/shard_map/all_to_all | solution.py:136
  185.9 1.4 fusion.2
  187.3 0.7 convert_element_type.133
  188.2 61.2 %all-gather.5.cloned.1.call-done.r_ref = bf16[4,32,128,128]{3,2,1,0:T(8,128)(2,1)} async-done(((bf16[4,32,8,128]{3,2,1,0:T(8,128)(2,1)}), bf16[4,32,128,128]{3,2,1,0:T(8,128)(2,1)}) %all-gather.5.cloned.1.call-update) | async-done | bytes 4194320 | tf_op jit(solution)/shard_map/all_gather | solution.py:140
  249.3 7.3 %reshape.460 = bf16[4,32,16384]{2,1,0:T(8,128)(2,1)} reshape(bf16[4,32,128,128]{3,2,1,0:T(8,128)(2,1)} %all-gather.5.cloned.1.call-done.r_ref) | data formatting | bytes 8388608 | tf_op jit(solution)/shard_map/reshape | solution.py:141
  256.6 1.2 slice.109
  258.5 0.7 broadcast_add_fusion
  259.2 0.6 fusion.33.sel_ref
  259.8 1.1 convolution_convert_fusion.8
  261.0 37.6 %shard_map.95 = f32[4,32,16,128]{3,2,1,0:T(8,128)} custom-call(bf16[2,1024,128]{2,1,0:T(8,128)(2,1)} %bitcast.219, bf16[128,256]{1,0:T(8,128)(2,1)} %fusion.33.sel_ref, bf16[4,32,128,128]{3,2,1,0:T(8,128)(2,1)} %all-gather.5.cloned.1.call-done.r_ref), custom_call_target="tpu_custom_call" | custom-call | flops 9663676416 | bytes 5767168 | tf_op jit(solution)/shard_map/pallas_call | solution.py:57
  298.5 1.3 fusion.11
  299.9 0.6 copy.96
  300.5 1.8 mul.230
  302.2 4.0 %all-gather.7.cloned.1.call-done = f32[32,16384]{1,0:T(8,128)} async-done(((f32[32,1024]{1,0:T(8,128)}), f32[32,16384]{1,0:T(8,128)}) %all-gather.7.cloned.1.call-update) | async-done | bytes 2097168 | tf_op jit(solution)/shard_map/all_gather | solution.py:143
  306.3 3.0 copy.151
  (59 shorter events, 1.6 us)
Async XLA Ops:
  12.8 13.8 %copy-start.7 = (s32[4,16]{1,0:T(4,128)S(1)}, s32[4,16]{1,0:T(4,128)}, u32[]{:S(2)}) copy-start(s32[4,16]{1,0:T(4,128)} %param.13) | copy-start | bytes 772
  12.8 13.8 %copy-start.5 = (bf16[16,16384]{1,0:T(8,128)(2,1)S(1)}, bf16[16,16384]{1,0:T(8,128)(2,1)}, u32[]{:S(2)}) copy-start(bf16[16,16384]{1,0:T(8,128)(2,1)} %param.8) | copy-start | bytes 1572868
  14.9 37.4 %all-to-all-start = ((bf16[128,2,384]{2,1,0:T(2,128)(2,1)}), bf16[128,2,384]{2,1,0:T(2,128)(2,1)S(1)}, u32[]{:S(2)}, u32[]{:S(2)}) async-start(bf16[128,2,384]{2,1,0:T(2,128)(2,1)} %reshape.473), calls=%async_computation | async-start | bytes 393216 | tf_op jit(solution)/shard_map/all_to_all | solution.py:123
  26.7 13.0 %copy-start = (bf16[2,8,128,128]{3,2,1,0:T(8,128)(2,1)}, bf16[2,8,128,128]{3,2,1,0:T(8,128)(2,1)S(1)}, u32[]{:S(2)}) copy-start(bf16[2,8,128,128]{3,2,1,0:T(8,128)(2,1)S(1)} %copy.102) | copy-start | bytes 1572868
  41.0 2.0 copy-start.4
  41.9 1.5 copy-start.2
  41.9 2.0 copy-start.3
  52.2 11.4 %copy-start.6 = (f32[32]{0:T(128)S(1)}, f32[32]{0:T(128)}, u32[]{:S(2)}) copy-start(f32[32]{0:T(128)} %param.10) | copy-start | bytes 388
  52.2 89.8 %all-to-all-start.1 = ((bf16[128,4,6,1024]{3,1,2,0:T(4,128)(2,1)}), bf16[128,4,6,1024]{3,1,2,0:T(4,128)(2,1)}, u32[]{:S(2)}, u32[]{:S(2)}) async-start(bf16[128,4,6,1024]{3,1,2,0:T(4,128)(2,1)} %copy.93), calls=%async_computation.1 | async-start | bytes 12582912 | tf_op jit(solution)/shard_map/all_to_all | solution.py:122
  154.8 4.1 %copy-start.8 = (s32[4]{0:T(128)S(1)}, s32[4]{0:T(128)}, u32[]{:S(2)}) copy-start(s32[4]{0:T(128)} %param.15) | copy-start | bytes 52
  154.8 31.1 %all-to-all-start.2 = ((bf16[8,4,32,8,128]{4,3,2,1,0:T(8,128)(2,1)}), bf16[8,4,32,8,128]{4,3,2,1,0:T(8,128)(2,1)S(1)}, u32[]{:S(2)}, u32[]{:S(2)}) async-start(bf16[8,4,32,8,128]{4,3,2,1,0:T(8,128)(2,1)} %broadcast_in_dim.5), calls=%async_computation.2 | async-start | bytes 4194304 | tf_op jit(solution)/shard_map/all_to_all | solution.py:136
  158.9 90.4 %all-gather.5.cloned.1.call-start = ((), (), s32[]{:S(2)}) async-start(), calls=%async_computation.3 | async-start | bytes 4456448 | tf_op jit(solution)/shard_map/all_gather | solution.py:140
  188.1 71.7 %copy-start.1 = (bf16[2,8,128,128]{3,2,1,0:T(8,128)(2,1)S(1)}, bf16[2,8,128,128]{3,2,1,0:T(8,128)(2,1)}, u32[]{:S(2)}) copy-start(bf16[2,8,128,128]{3,2,1,0:T(8,128)(2,1)} %copy-done) | copy-start | bytes 1572868
  188.1 118.2 %all-gather.7.cloned.1.call-start = ((), (), s32[]{:S(2)}) async-start(), calls=%async_computation.4 | async-start | bytes 2228224 | tf_op jit(solution)/shard_map/all_gather | solution.py:143
Sparse Core Ops, SparseCore 0:
  188.2 61.0 all-gather.4
  259.3 46.9 all-gather.6

commit v12 on v10

--- a/solution.py
+++ b/solution.py
@@ -92,7 +92,6 @@
     scale = 1.0 / math.sqrt(pixels)
 
     send_img = []
-    send_wts = []
     for step in range(STEPS):
         shifts = rot_ids[step] * ASTEP
         rotated = rotate_each(cube, shifts).reshape(per_dev, pixels)
@@ -108,19 +107,26 @@
         images = jnp.dot(placing, rotated, preferred_element_type=jnp.float32).astype(jnp.bfloat16)
         images = images.reshape(groups, capacity, doms, chunk).transpose(2, 0, 1, 3)
         send_img.append(images)
-        class_hot = (
-            class_ids[step][:, None] == jnp.arange(per_group, dtype=jnp.int32)[None, :]
-        ).astype(jnp.bfloat16)
-        weighted_hot = class_hot * weights[step][:, None]
-        wts = jnp.dot(placing, weighted_hot, preferred_element_type=jnp.float32).astype(
-            jnp.bfloat16
-        )
-        wts = jnp.broadcast_to(wts.reshape(1, groups, capacity, per_group), (doms, groups, capacity, per_group))
-        send_wts.append(wts)
     send_img = jnp.stack(send_img, axis=2).reshape(doms * groups, STEPS, capacity, chunk)
-    send_wts = jnp.stack(send_wts, axis=2).reshape(doms * groups, STEPS, capacity, per_group)
     got_img = lax.all_to_all(send_img, ("dom", "cls"), 0, 0, tiled=True)
-    got_wts = lax.all_to_all(send_wts, ("dom", "cls"), 0, 0, tiled=True)
+    meta = jnp.stack(
+        [group_ids[:, :, 0].astype(jnp.float32), class_ids.astype(jnp.float32), weights.astype(jnp.float32)]
+    )
+    meta = lax.all_gather(meta, ("dom", "cls"), axis=1, tiled=False)
+    src_group = meta[0].astype(jnp.int32)
+    src_class = meta[1].astype(jnp.int32)
+    src_weight = meta[2].astype(jnp.bfloat16)
+    hot = (src_group[..., None] == jnp.arange(groups, dtype=jnp.int32)).astype(jnp.int32)
+    src_rank = jnp.sum((jnp.cumsum(hot, axis=2) - 1) * hot, axis=3)
+    in_slot = (src_group == me_cls)[:, :, None, :] & (
+        src_rank[:, :, None, :] == jnp.arange(capacity, dtype=jnp.int32)[None, None, :, None]
+    )
+    weighted_hot = (
+        src_class[..., None] == jnp.arange(per_group, dtype=jnp.int32)
+    ).astype(jnp.bfloat16) * src_weight[..., None]
+    got_wts = jnp.einsum(
+        "jsqp,jspk->jsqk", in_slot.astype(jnp.bfloat16), weighted_hot, preferred_element_type=jnp.float32
+    ).astype(jnp.bfloat16)
     totals = lax.dot_general(
         got_wts, got_img, (((0, 2), (0, 2)), ((1,), (1,))), preferred_element_type=jnp.float32
     )

time: 308 us -> 592 us (1.92)
  blocking collectives: 0 us -> 373 us
  waiting for transfers between devices: 163 us -> 85.3 us
  starting transfers between devices: 26 us -> 15.9 us
    all_gather x0 -> x1, blocking collectives: none -> 373 us  [per_device(): meta = lax.all_gather(meta, ('dom', 'cls'), axis=1, tiled=False)]
    all_to_all x1, waiting for transfers between devices: 78.4 us -> 0.01 us  [per_device(): got_img = lax.all_to_all(send_img, ('dom', 'cls'), 0, 0, tiled=True)]
    all_to_all x1 -> x0, starting transfers between devices: 11.7 us -> none  [per_device(): got_wts = lax.all_to_all(send_wts, ('dom', 'cls'), 0, 0, tiled=True)]
    all_gather x1, waiting for transfers between devices: 58.1 us -> 69.5 us  [per_device(): all_refs = lax.all_gather(owner_chunk, 'dom', axis=2, tiled=False)]
    all_to_all x1, waiting for transfers between devices: 26.8 us -> 15.7 us  [per_device(): got_refs = lax.all_to_all(ref_chunks, 'cls', 0, 0, tiled=True)]
  transfers between devices with their start and end apart: 5 -> 4, of which waited for: 3 -> 2; matrix products, arithmetic and copies ran while one was open for 12% -> 3% of each run, Pallas kernels for 12% -> 6%
where the time goes in v12:
time: 592 us; the launch traced here: 591 us
  blocking collectives  373 us (63%)
  waiting for transfers between devices  85.3 us (14%)
  Pallas kernels  37.6 us (6%)
  local copies, waits for them, and re-layouts  37.3 us (6%)
  matrix products  20.3 us (3%)
  starting transfers between devices  15.9 us (3%)
  between operations  15.1 us (3%)
  other arithmetic  7.16 us (1%)
    all_gather x1, blocking collectives, per_device(): meta = lax.all_gather(meta, ('dom', 'cls'), axis=1, tiled=False)  373 us
    all_gather x1, waiting for transfers between devices, per_device(): all_refs = lax.all_gather(owner_chunk, 'dom', axis=2, tiled=False)  69.5 us
    pallas_call x1, Pallas kernels, shift_scores(): pl.pallas_call(_scores_kernel, grid=(steps,), in_specs=[pl.BlockSpec((ast...  37.6 us
    all_to_all x1, waiting for transfers between devices, per_device(): got_refs = lax.all_to_all(ref_chunks, 'cls', 0, 0, tiled=True)  15.7 us
    all_to_all x1, starting transfers between devices, per_device(): got_img = lax.all_to_all(send_img, ('dom', 'cls'), 0, 0, tiled=True)  11.9 us
  transfers between devices with their start and end apart: 4, of which 2 were waited for; matrix products, arithmetic and copies ran while one was open for 3% of the time, Pallas kernels for 6%

profile of v12, /device:TPU:1, one launch (start us, length us, event | category | flops | bytes accessed | tf_op | source)
XLA Modules:
  0.0 591.5 jit_solution(3649263594814704599)
XLA Ops:
  7.2 0.7 slice_bitcast_fusion.7
  7.9 0.1 fusion.68
  8.1 0.1 fusion.74
  8.2 0.1 fusion.71
  8.3 0.8 multiply_bitcast_fusion.3
  9.2 1.1 copy.97
  10.3 0.1 add_select_fusion
  10.4 0.5 fusion.18
  10.9 0.3 copy.83
  11.2 0.2 select_reduce_fusion
  11.4 0.2 select_reduce_fusion.2
  11.6 0.6 convolution_convert_fusion
  12.1 0.9 copy.106
  13.0 2.0 copy.137
  15.0 0.5 fusion.17
  15.5 0.3 copy.81
  15.8 0.6 convolution_convert_fusion.1
  16.4 0.9 copy.104
  17.3 2.0 copy.138
  19.3 0.1 add_select_fusion.2
  19.4 0.5 fusion.16
  19.9 0.3 copy.79
  20.2 0.6 convolution_convert_fusion.2
  20.7 0.9 copy.102
  21.6 2.0 copy.139
  23.7 0.5 fusion.15
  24.1 0.3 copy.77
  24.4 0.6 convolution_convert_fusion.3
  25.0 0.9 copy.100
  25.9 1.1 copy.140
  27.0 0.4 copy-done.2
  27.4 0.5 copy-done.3
  27.9 0.8 pad_maximum_fusion
  28.7 7.5 %copy.85 = bf16[128,4,6,1024]{3,1,2,0:T(4,128)(2,1)} copy(bf16[128,4,6,1024]{3,0,2,1:T(8,128)(2,1)S(1)} %pad_maximum_fusion) | data formatting | bytes 12582912 | tf_op jit(solution)/shard_map/stack | solution.py:110
  36.3 11.9 %all-to-all-start = ((bf16[128,4,6,1024]{3,1,2,0:T(4,128)(2,1)}), bf16[128,4,6,1024]{3,1,2,0:T(4,128)(2,1)}, u32[]{:S(2)}, u32[]{:S(2)}) async-start(bf16[128,4,6,1024]{3,1,2,0:T(4,128)(2,1)} %copy.85), calls=%async_computation | async-start | bytes 12582912 | tf_op jit(solution)/shard_map/all_to_all | solution.py:111
  48.2 372.8 %all-gather = f32[3,512,16]{2,0,1:T(4,128)S(1)} all-gather(f32[3,4,16]{2,0,1:T(4,128)S(1)} %copy.74), channel_id=2, replica_groups=mesh['dom'=16,'cls'=8] {'dom','cls'}, dimensions={1}, use_global_device_ids=true | all-gather | bytes 99072 | tf_op jit(solution)/shard_map/all_gather | solution.py:115
  421.1 0.3 slice.147
  421.4 0.4 slice_convert_fusion.2
  421.8 0.1 copy.75
  421.9 0.2 fusion.91
  422.0 0.2 copy.76
  422.3 3.7 convert_reduce_fusion
  426.1 9.8 %fusion.19 = f32[4,32,1024]{2,1,0:T(8,128)S(1)} fusion(bf16[128,4,6,1024]{3,1,2,0:T(4,128)(2,1)} %all-to-all-done, bf16[128,4,6,32]{3,2,1,0:T(8,128)(2,1)S(1)} %get-tuple-element.28), kind=kOutput, calls=%fused_computation.30 | convolution fusion | flops 201326592 | bytes 7012352 | tf_op jit(solution)/shard_map/dot_general | solution.py:130
  435.9 1.0 convert_bitcast_fusion.3
  436.9 0.1 convert_bitcast_fusion.1
  437.0 0.1 convert_bitcast_fusion
  437.1 1.6 broadcast_in_dim.2
  438.7 3.7 all-to-all-start.1
  442.6 0.1 copy.92
  442.7 15.7 %all-to-all-done.1 = bf16[8,4,32,1024]{3,2,1,0:T(8,128)(2,1)S(1)} async-done(((bf16[8,4,32,1024]{3,2,1,0:T(8,128)(2,1)}), bf16[8,4,32,1024]{3,2,1,0:T(8,128)(2,1)S(1)}, u32[]{:S(2)}, u32[]{:S(2)}) %all-to-all-start.1) | async-done | bytes 2097184 | tf_op jit(solution)/shard_map/all_to_all | solution.py:142
  458.4 1.4 fusion.5
  459.8 0.8 copy.141
  460.6 0.3 all-gather.8.cloned.1.call-start
  460.9 69.5 %all-gather.6.cloned.1.call-done = bf16[4,32,16384]{2,1,0:T(8,128)(2,1)} async-done(((bf16[4,32,1024]{2,1,0:T(8,128)(2,1)}), bf16[4,32,16384]{2,1,0:T(8,128)(2,1)}) %all-gather.6.cloned.1.call-update) | async-done | bytes 4194320 | tf_op jit(solution)/shard_map/all_gather | solution.py:146
  530.4 1.2 slice.96
  532.3 0.7 broadcast_add_fusion
  533.0 0.6 fusion.51.sel_ref
  533.6 1.1 convolution_convert_fusion.8
  534.8 5.4 copy.107
  540.2 37.6 %shard_map.95 = f32[4,32,16,128]{3,2,1,0:T(8,128)} custom-call(bf16[2,1024,128]{2,1,0:T(8,128)(2,1)} %bitcast.209, bf16[128,256]{1,0:T(8,128)(2,1)} %fusion.51.sel_ref, bf16[4,32,128,128]{3,2,1,0:T(8,128)(2,1)} %bitcast.199), custom_call_target="tpu_custom_call" | custom-call | flops 9663676416 | bytes 5767168 | tf_op jit(solution)/shard_map/pallas_call | solution.py:57
  577.8 1.3 fusion.23
  579.1 0.6 copy.88
  579.7 1.8 mul.192
  581.5 3.2 copy.96
  (42 shorter events, 0.5 us)
Async XLA Ops:
  7.2 4.4 copy-start.5
  10.3 13.3 %copy-start = (bf16[2,8,128,128]{3,2,1,0:T(8,128)(2,1)}, bf16[2,8,128,128]{3,2,1,0:T(8,128)(2,1)S(1)}, u32[]{:S(2)}) copy-start(bf16[2,8,128,128]{3,2,1,0:T(8,128)(2,1)S(1)} %copy.97) | copy-start | bytes 1572868
  25.0 2.0 copy-start.4
  25.9 1.5 copy-start.2
  25.9 2.0 copy-start.3
  36.2 11.9 %copy-start.8 = (bf16[4,16]{1,0:T(4,128)(2,1)S(1)}, bf16[4,16]{1,0:T(4,128)(2,1)}, u32[]{:S(2)}) copy-start(bf16[4,16]{1,0:T(4,128)(2,1)} %param.14) | copy-start | bytes 388
  36.3 11.9 %copy-start.7 = (s32[4,16]{1,0:T(4,128)S(1)}, s32[4,16]{1,0:T(4,128)}, u32[]{:S(2)}) copy-start(s32[4,16]{1,0:T(4,128)} %param.12) | copy-start | bytes 772
  36.3 389.8 %all-to-all-start = ((bf16[128,4,6,1024]{3,1,2,0:T(4,128)(2,1)}), bf16[128,4,6,1024]{3,1,2,0:T(4,128)(2,1)}, u32[]{:S(2)}, u32[]{:S(2)}) async-start(bf16[128,4,6,1024]{3,1,2,0:T(4,128)(2,1)} %copy.85), calls=%async_computation | async-start | bytes 12582912 | tf_op jit(solution)/shard_map/all_to_all | solution.py:111
  422.3 3.8 copy-start.6
  438.7 3.8 copy-start.9
  438.7 19.6 %all-to-all-start.1 = ((bf16[8,4,32,1024]{3,2,1,0:T(8,128)(2,1)}), bf16[8,4,32,1024]{3,2,1,0:T(8,128)(2,1)S(1)}, u32[]{:S(2)}, u32[]{:S(2)}) async-start(bf16[8,4,32,1024]{3,2,1,0:T(8,128)(2,1)} %broadcast_in_dim.2), calls=%async_computation.1 | async-start | bytes 4194304 | tf_op jit(solution)/shard_map/all_to_all | solution.py:142
  442.5 91.2 %copy-start.1 = (bf16[2,8,128,128]{3,2,1,0:T(8,128)(2,1)S(1)}, bf16[2,8,128,128]{3,2,1,0:T(8,128)(2,1)}, u32[]{:S(2)}) copy-start(bf16[2,8,128,128]{3,2,1,0:T(8,128)(2,1)} %copy-done) | copy-start | bytes 1572868
  442.5 87.9 %all-gather.6.cloned.1.call-start = ((), (), s32[]{:S(2)}) async-start(), calls=%async_computation.2 | async-start | bytes 4456448 | tf_op jit(solution)/shard_map/all_gather | solution.py:146
  460.6 120.9 %all-gather.8.cloned.1.call-start = ((), (), s32[]{:S(2)}) async-start(), calls=%async_computation.3 | async-start | bytes 2228224 | tf_op jit(solution)/shard_map/all_gather | solution.py:149
Sparse Core Ops, SparseCore 0:
  460.7 69.6 all-gather.5
  533.1 47.0 all-gather.7

commit v13 on v10

--- a/solution.py
+++ b/solution.py
@@ -91,23 +91,22 @@
     cube = particles.reshape(per_dev, RADII, ANGLES)
     scale = 1.0 / math.sqrt(pixels)
 
-    send_img = []
+    rot_all = []
+    placing_all = []
     send_wts = []
     for step in range(STEPS):
         shifts = rot_ids[step] * ASTEP
-        rotated = rotate_each(cube, shifts).reshape(per_dev, pixels)
+        rot_all.append(rotate_each(cube, shifts).reshape(per_dev, pixels))
         target = group_ids[step, :, 0]
         onehot_group = (target[:, None] == jnp.arange(groups, dtype=jnp.int32)[None, :]).astype(
             jnp.int32
         )
         rank = jnp.sum((jnp.cumsum(onehot_group, axis=0) - 1) * onehot_group, axis=1)
-        slot_of = target * capacity + rank
+        slot_of = rank * groups + target
         placing = (slot_of[None, :] == jnp.arange(slots, dtype=jnp.int32)[:, None]).astype(
             jnp.bfloat16
         )
-        images = jnp.dot(placing, rotated, preferred_element_type=jnp.float32).astype(jnp.bfloat16)
-        images = images.reshape(groups, capacity, doms, chunk).transpose(2, 0, 1, 3)
-        send_img.append(images)
+        placing_all.append(placing)
         class_hot = (
             class_ids[step][:, None] == jnp.arange(per_group, dtype=jnp.int32)[None, :]
         ).astype(jnp.bfloat16)
@@ -115,16 +114,20 @@
         wts = jnp.dot(placing, weighted_hot, preferred_element_type=jnp.float32).astype(
             jnp.bfloat16
         )
-        wts = jnp.broadcast_to(wts.reshape(1, groups, capacity, per_group), (doms, groups, capacity, per_group))
-        send_wts.append(wts)
-    send_img = jnp.stack(send_img, axis=2).reshape(doms * groups, STEPS, capacity, chunk)
-    send_wts = jnp.stack(send_wts, axis=2).reshape(doms * groups, STEPS, capacity, per_group)
-    got_img = lax.all_to_all(send_img, ("dom", "cls"), 0, 0, tiled=True)
-    got_wts = lax.all_to_all(send_wts, ("dom", "cls"), 0, 0, tiled=True)
+        wts = jnp.broadcast_to(wts.reshape(capacity, groups, 1, per_group), (capacity, groups, doms, per_group))
+        send_wts.append(wts.reshape(capacity, groups * doms, per_group))
+    send_img = jnp.einsum(
+        "sqi,sip->sqp", jnp.stack(placing_all), jnp.stack(rot_all), preferred_element_type=jnp.float32
+    ).astype(jnp.bfloat16)
+    send_img = send_img.reshape(STEPS, capacity, groups * doms, chunk)
+    send_wts = jnp.stack(send_wts)
+    got_img = lax.all_to_all(send_img, ("cls", "dom"), 2, 2, tiled=True)
+    got_wts = lax.all_to_all(send_wts, ("cls", "dom"), 2, 2, tiled=True)
     totals = lax.dot_general(
-        got_wts, got_img, (((0, 2), (0, 2)), ((1,), (1,))), preferred_element_type=jnp.float32
+        got_wts, got_img, (((1, 2), (1, 2)), ((0,), (0,))), preferred_element_type=jnp.float32
     )
-    mass = jnp.sum(got_wts.astype(jnp.float32), axis=(0, 2))
+    mass = jnp.sum(got_wts.astype(jnp.float32), axis=(1, 2))
+
 
     current = lax.dynamic_slice_in_dim(averages, me_dom * chunk, chunk, axis=1)
     ref_chunks = []

time: 308 us -> 324 us (1.052)
  starting transfers between devices: 26 us -> 33.9 us
  local copies, waits for them, and re-layouts: 40.2 us -> 43.8 us
    reshape x5 -> x2, local copies, waits for them, and re-layouts: 7.8 us -> 20.7 us  [per_device(): send_img = send_img.reshape(STEPS, capacity, groups * doms, chunk)]
    all_to_all x1, starting transfers between devices: 4.04 us -> 11.8 us  [per_device(): got_refs = lax.all_to_all(ref_chunks, 'cls', 0, 0, tiled=True)]
    all_gather x1, waiting for transfers between devices: 58.1 us -> 64.5 us  [per_device(): all_refs = lax.all_gather(owner_chunk, 'dom', axis=2, tiled=False)]
    another operation x13 -> x5, local copies, waits for them, and re-layouts: 7.74 us -> 1.51 us  [the longest x4 0.9 us: per_device(): jnp.stack(rot_all)]
    all_to_all x2, waiting for transfers between devices: 78.4 us -> 73.6 us  [the longest x1 73.6 us: per_device(): got_img = lax.all_to_all(send_img, ('cls', 'dom'), 2, 2, tiled=True)]
    unnamed x26 -> x12, local copies, waits for them, and re-layouts: 11.6 us -> 7.15 us
    dot_general x5 -> x2, matrix products: 11.9 us -> 14.2 us  [the longest x1 9.67 us: per_device(): lax.dot_general(got_wts, got_img, (((1, 2), (1, 2)), ((0,), (0,))), prefe...]
  transfers between devices with their start and end apart: 5 -> 5, of which waited for: 3 -> 3; matrix products, arithmetic and copies ran while one was open for 12% -> 14% of each run, Pallas kernels for 12% -> 12%
where the time goes in v13:
time: 324 us; the launch traced here: 323 us
  waiting for transfers between devices  165 us (51%)
  local copies, waits for them, and re-layouts  43.8 us (14%)
  Pallas kernels  37.6 us (12%)
  starting transfers between devices  33.9 us (10%)
  matrix products  19.7 us (6%)
  between operations  15 us (5%)
  other arithmetic  7.88 us (2%)
    all_to_all x1, waiting for transfers between devices, per_device(): got_img = lax.all_to_all(send_img, ('cls', 'dom'), 2, 2, tiled=True)  73.6 us
    all_gather x1, waiting for transfers between devices, per_device(): all_refs = lax.all_gather(owner_chunk, 'dom', axis=2, tiled=False)  64.5 us
    pallas_call x1, Pallas kernels, shift_scores(): pl.pallas_call(_scores_kernel, grid=(steps,), in_specs=[pl.BlockSpec((ast...  37.6 us
    all_to_all x1, waiting for transfers between devices, per_device(): got_refs = lax.all_to_all(ref_chunks, 'cls', 0, 0, tiled=True)  26.9 us
    reshape x2, local copies, waits for them, and re-layouts, per_device(): send_img = send_img.reshape(STEPS, capacity, groups * doms, chunk)  20.7 us
    all_to_all x1, starting transfers between devices, per_device(): got_refs = lax.all_to_all(ref_chunks, 'cls', 0, 0, tiled=True)  11.8 us
    all_to_all x1, starting transfers between devices, per_device(): got_wts = lax.all_to_all(send_wts, ('cls', 'dom'), 2, 2, tiled=True)  11.5 us
    all_to_all x1, starting transfers between devices, per_device(): got_img = lax.all_to_all(send_img, ('cls', 'dom'), 2, 2, tiled=True)  10.2 us
  transfers between devices with their start and end apart: 5, of which 3 were waited for; matrix products, arithmetic and copies ran while one was open for 14% of the time, Pallas kernels for 12%

profile of v13, /device:TPU:1, one launch (start us, length us, event | category | flops | bytes accessed | tf_op | source)
XLA Modules:
  0.0 322.8 jit_solution(11238863036129547536)
XLA Ops:
  7.2 0.7 slice_bitcast_fusion.15
  8.3 0.8 slice_bitcast_fusion.14
  9.1 0.8 slice_bitcast_fusion.13
  10.0 0.2 select_reduce_fusion
  10.2 0.2 select_reduce_fusion.2
  10.3 0.7 multiply_add_fusion.3
  11.1 0.2 convolution_convert_fusion.8
  11.3 0.1 copy.62
  11.4 0.3 convolution_convert_fusion.7
  11.7 0.1 copy.63
  11.8 0.3 convolution_convert_fusion.6
  12.0 0.1 copy.64
  12.1 0.3 convolution_convert_fusion.9
  12.4 0.1 copy.61
  12.7 0.2 pad_maximum_fusion
  12.9 0.6 copy.95
  13.5 1.3 reshape.540
  14.8 11.5 %all-to-all-start = ((bf16[128,2,384]{2,1,0:T(2,128)(2,1)}), bf16[128,2,384]{2,1,0:T(2,128)(2,1)S(1)}, u32[]{:S(2)}, u32[]{:S(2)}) async-start(bf16[128,2,384]{2,1,0:T(2,128)(2,1)} %reshape.540), calls=%async_computation | async-start | bytes 393216 | tf_op jit(solution)/shard_map/all_to_all | solution.py:125
  26.3 0.1 iota_compare_fusion.18
  26.4 0.1 iota_compare_fusion.19
  26.6 0.1 copy.81
  26.7 0.1 add_select_fusion.2
  26.8 0.5 fusion.11
  27.3 0.3 copy.66
  27.6 0.2 stack_reshape.28
  27.8 0.5 fusion.12
  28.3 0.3 copy.67
  28.6 0.2 stack_reshape.29
  28.8 0.1 add_select_fusion
  28.9 0.5 fusion.13
  29.4 0.3 copy.68
  29.7 0.2 stack_reshape.30
  29.9 0.5 fusion.14
  30.4 0.3 copy.69
  30.7 0.2 stack_reshape.31
  30.9 4.5 %convolution_convert_fusion = bf16[4,48,16384]{2,1,0:T(8,128)(2,1)} fusion(bf16[1,16,16384]{2,1,0:T(8,128)(2,1)S(1)} %stack_reshape.31, bf16[1,16,16384]{2,1,0:T(8,128)(2,1)S(1)} %stack_reshape.30, bf16[1,16,16384]{2,1,0:T(8,128)(2,1)S(1)} %stack_reshape.29, bf16[1,16,16384]{2,1,0:T(8,128)(2,1)S(1)} %stack_reshape.28, ...), kind=kOutput, calls=%fused_computation | convolution fusion | flops 106963968 | bytes 8391680 | tf_op jit(solution)/shard_map/sqi,sip->sqp/dot_general | solution.py:119
  35.4 10.4 %reshape.527 = bf16[4,6,128,1024]{3,2,1,0:T(8,128)(2,1)} reshape(bf16[4,48,16384]{2,1,0:T(8,128)(2,1)} %convolution_convert_fusion) | data formatting | bytes 12582912 | tf_op jit(solution)/shard_map/reshape | solution.py:122
  45.8 10.3 %copy.70 = bf16[4,6,128,1024]{3,0,1,2:T(4,128)(2,1)} copy(bf16[4,6,128,1024]{3,2,1,0:T(8,128)(2,1)} %reshape.527) | data formatting | bytes 12582912 | tf_op jit(solution)/shard_map/reshape | solution.py:122
  56.1 10.2 %all-to-all-start.1 = ((bf16[4,6,128,1024]{3,0,1,2:T(4,128)(2,1)}), bf16[4,6,128,1024]{3,0,1,2:T(4,128)(2,1)}, u32[]{:S(2)}, u32[]{:S(2)}) async-start(bf16[4,6,128,1024]{3,0,1,2:T(4,128)(2,1)} %copy.70), calls=%async_computation.1 | async-start | bytes 12582912 | tf_op jit(solution)/shard_map/all_to_all | solution.py:124
  66.3 0.4 reshape.541
  66.6 0.8 convert_reduce_fusion
  67.5 73.6 %all-to-all-done.1 = bf16[4,6,128,1024]{3,0,1,2:T(4,128)(2,1)} async-done(((bf16[4,6,128,1024]{3,0,1,2:T(4,128)(2,1)}), bf16[4,6,128,1024]{3,0,1,2:T(4,128)(2,1)}, u32[]{:S(2)}, u32[]{:S(2)}) %all-to-all-start.1) | async-done | bytes 6291488 | tf_op jit(solution)/shard_map/all_to_all | solution.py:124
  141.1 9.7 %fusion.15 = f32[4,32,1024]{2,1,0:T(8,128)S(1)} fusion(bf16[4,6,128,1024]{3,0,1,2:T(4,128)(2,1)} %all-to-all-done.1, bf16[4,6,128,32]{3,0,1,2:T(4,128)(2,1)S(1)} %bitcast.156), kind=kOutput, calls=%fused_computation.22 | convolution fusion | flops 201326592 | bytes 7012352 | tf_op jit(solution)/shard_map/dot_general | solution.py:126
  150.7 1.0 convert_bitcast_fusion.3
  151.8 0.1 convert_bitcast_fusion.1
  151.9 0.1 convert_bitcast_fusion
  152.0 1.6 broadcast_in_dim.26
  153.6 11.8 %all-to-all-start.2 = ((bf16[8,4,32,1024]{3,2,1,0:T(8,128)(2,1)}), bf16[8,4,32,1024]{3,2,1,0:T(8,128)(2,1)S(1)}, u32[]{:S(2)}, u32[]{:S(2)}) async-start(bf16[8,4,32,1024]{3,2,1,0:T(8,128)(2,1)} %broadcast_in_dim.26), calls=%async_computation.2 | async-start | bytes 4194304 | tf_op jit(solution)/shard_map/all_to_all | solution.py:139
  165.5 0.1 copy.77
  165.6 26.9 %all-to-all-done.2 = bf16[8,4,32,1024]{3,2,1,0:T(8,128)(2,1)S(1)} async-done(((bf16[8,4,32,1024]{3,2,1,0:T(8,128)(2,1)}), bf16[8,4,32,1024]{3,2,1,0:T(8,128)(2,1)S(1)}, u32[]{:S(2)}, u32[]{:S(2)}) %all-to-all-start.2) | async-done | bytes 2097184 | tf_op jit(solution)/shard_map/all_to_all | solution.py:139
  192.5 1.4 fusion.9
  193.9 0.8 copy.94
  194.7 0.3 all-gather.7.cloned.1.call-start
  195.0 64.5 %all-gather.5.cloned.1.call-done = bf16[4,32,16384]{2,1,0:T(8,128)(2,1)} async-done(((bf16[4,32,1024]{2,1,0:T(8,128)(2,1)}), bf16[4,32,16384]{2,1,0:T(8,128)(2,1)}) %all-gather.5.cloned.1.call-update) | async-done | bytes 4194320 | tf_op jit(solution)/shard_map/all_gather | solution.py:143
  259.6 1.2 slice.109
  261.4 0.7 broadcast_add_fusion
  262.2 0.6 fusion.32.sel_ref
  262.8 1.1 convolution_convert_fusion.5
  263.9 5.4 %copy.83 = bf16[16,8,128,128]{3,2,1,0:T(8,128)(2,1)} copy(bf16[16,8,128,128]{3,1,2,0:T(8,128)(2,1)} %bitcast.157) | data formatting | bytes 8388608
  269.3 37.6 %shard_map.95 = f32[4,32,16,128]{3,2,1,0:T(8,128)} custom-call(bf16[2,1024,128]{2,1,0:T(8,128)(2,1)} %bitcast.167, bf16[128,256]{1,0:T(8,128)(2,1)} %fusion.32.sel_ref, bf16[4,32,128,128]{3,2,1,0:T(8,128)(2,1)} %bitcast.158), custom_call_target="tpu_custom_call" | custom-call | flops 9663676416 | bytes 5767168 | tf_op jit(solution)/shard_map/pallas_call | solution.py:57
  306.9 2.3 fusion.18
  309.2 1.8 copy.73
  311.1 1.7 mul.230
  312.8 3.2 copy.80
  (34 shorter events, 0.9 us)
Async XLA Ops:
  12.6 13.9 %copy-start.2 = (s32[4,16]{1,0:T(4,128)S(1)}, s32[4,16]{1,0:T(4,128)}, u32[]{:S(2)}) copy-start(s32[4,16]{1,0:T(4,128)} %param.13) | copy-start | bytes 772
  12.7 13.9 %copy-start = (bf16[16,16384]{1,0:T(8,128)(2,1)S(1)}, bf16[16,16384]{1,0:T(8,128)(2,1)}, u32[]{:S(2)}) copy-start(bf16[16,16384]{1,0:T(8,128)(2,1)} %param.8) | copy-start | bytes 1572868
  14.8 41.3 %all-to-all-start = ((bf16[128,2,384]{2,1,0:T(2,128)(2,1)}), bf16[128,2,384]{2,1,0:T(2,128)(2,1)S(1)}, u32[]{:S(2)}, u32[]{:S(2)}) async-start(bf16[128,2,384]{2,1,0:T(2,128)(2,1)} %reshape.540), calls=%async_computation | async-start | bytes 393216 | tf_op jit(solution)/shard_map/all_to_all | solution.py:125
  56.1 11.4 %copy-start.1 = (f32[32]{0:T(128)S(1)}, f32[32]{0:T(128)}, u32[]{:S(2)}) copy-start(f32[32]{0:T(128)} %param.10) | copy-start | bytes 388
  56.1 85.0 %all-to-all-start.1 = ((bf16[4,6,128,1024]{3,0,1,2:T(4,128)(2,1)}), bf16[4,6,128,1024]{3,0,1,2:T(4,128)(2,1)}, u32[]{:S(2)}, u32[]{:S(2)}) async-start(bf16[4,6,128,1024]{3,0,1,2:T(4,128)(2,1)} %copy.70), calls=%async_computation.1 | async-start | bytes 12582912 | tf_op jit(solution)/shard_map/all_to_all | solution.py:124
  153.6 11.9 %copy-start.3 = (s32[4]{0:T(128)S(1)}, s32[4]{0:T(128)}, u32[]{:S(2)}) copy-start(s32[4]{0:T(128)} %param.15) | copy-start | bytes 52
  153.6 38.9 %all-to-all-start.2 = ((bf16[8,4,32,1024]{3,2,1,0:T(8,128)(2,1)}), bf16[8,4,32,1024]{3,2,1,0:T(8,128)(2,1)S(1)}, u32[]{:S(2)}, u32[]{:S(2)}) async-start(bf16[8,4,32,1024]{3,2,1,0:T(8,128)(2,1)} %broadcast_in_dim.26), calls=%async_computation.2 | async-start | bytes 4194304 | tf_op jit(solution)/shard_map/all_to_all | solution.py:139
  165.5 94.1 %all-gather.5.cloned.1.call-start = ((), (), s32[]{:S(2)}) async-start(), calls=%async_computation.3 | async-start | bytes 4456448 | tf_op jit(solution)/shard_map/all_gather | solution.py:143
  194.7 118.1 %all-gather.7.cloned.1.call-start = ((), (), s32[]{:S(2)}) async-start(), calls=%async_computation.4 | async-start | bytes 2228224 | tf_op jit(solution)/shard_map/all_gather | solution.py:146
Sparse Core Ops, SparseCore 0:
  194.9 64.6 all-gather.4
  262.2 47.0 all-gather.6

commit v14 on v11

--- a/solution.py
+++ b/solution.py
@@ -137,9 +137,9 @@
     owner_hot = (owners[None, :] == jnp.arange(groups, dtype=jnp.int32)[:, None]).astype(jnp.bfloat16)
     owner_chunk = jnp.einsum("gs,gskrc->skrc", owner_hot, got_refs, preferred_element_type=jnp.float32)
     owner_chunk = owner_chunk.astype(jnp.bfloat16)
-    all_refs = lax.all_gather(owner_chunk, "dom", axis=2, tiled=False)
-    all_refs = all_refs.reshape(STEPS, per_group, pixels)
-    current = current + 0.0 * all_refs[0, 0, 0].astype(jnp.float32)
+    gathered = lax.all_gather(owner_chunk, "dom", axis=2, tiled=False)
+    current = current + 0.0 * gathered[0, 0, 0, 0, 0].astype(jnp.float32)
+    all_refs = gathered.reshape(STEPS, per_group, pixels)
     final = lax.all_gather(current, "dom", axis=1, tiled=False).reshape(per_group, pixels)
 
     shifted = shift_scores(cube, all_refs.reshape(STEPS, per_group, RADII, ANGLES), ASTEP)

time: 317 us -> 309 us (0.975)
  local copies, waits for them, and re-layouts: 41.4 us -> 34.1 us
    reshape x1 -> x0, local copies, waits for them, and re-layouts: 7.33 us -> none  [per_device(): all_refs = all_refs.reshape(STEPS, per_group, pixels)]
where the time goes in v14:
time: 309 us
  waiting for transfers between devices  170 us (55%)
  Pallas kernels  37.6 us (12%)
  local copies, waits for them, and re-layouts  34.1 us (11%)
  starting transfers between devices  26 us (8%)
  matrix products  17.4 us (6%)
  between operations  15.2 us (5%)
  other arithmetic  8.17 us (3%)
    all_to_all x1, waiting for transfers between devices, per_device(): got_img = lax.all_to_all(send_img, ('dom', 'cls'), 0, 0, tiled=True)  78.4 us
    all_gather x1, waiting for transfers between devices, per_device(): gathered = lax.all_gather(owner_chunk, 'dom', axis=2, tiled=False)  61.2 us
    pallas_call x1, Pallas kernels, shift_scores(): pl.pallas_call(_scores_kernel, grid=(steps,), in_specs=[pl.BlockSpec((ast...  37.6 us
    all_to_all x1, waiting for transfers between devices, per_device(): got_refs = lax.all_to_all(ref_chunks, 'cls', 0, 0, tiled=True)  26.8 us
    all_to_all x1, starting transfers between devices, per_device(): got_wts = lax.all_to_all(send_wts, ('dom', 'cls'), 0, 0, tiled=True)  11.7 us
    all_to_all x1, starting transfers between devices, per_device(): got_img = lax.all_to_all(send_img, ('dom', 'cls'), 0, 0, tiled=True)  10.2 us
    dot_general x1, matrix products, per_device(): lax.dot_general(got_wts, got_img, (((0, 2), (0, 2)), ((1,), (1,))), prefe...  9.67 us
    unnamed x30, local copies, waits for them, and re-layouts  9.23 us
  transfers between devices with their start and end apart: 5, of which 4 were waited for; matrix products, arithmetic and copies ran while one was open for 10% of the time, Pallas kernels for 12%

profile of v14, /device:TPU:1, one launch (start us, length us, event | category | flops | bytes accessed | tf_op | source)
XLA Modules:
  0.0 308.8 jit_solution(14144209394506461448)
XLA Ops:
  7.2 0.7 slice_bitcast_fusion.15
  8.3 0.8 slice_bitcast_fusion.14
  9.1 0.8 slice_bitcast_fusion.13
  10.0 0.2 select_reduce_fusion
  10.2 0.2 select_reduce_fusion.2
  10.3 0.7 multiply_add_fusion.3
  11.1 0.2 convolution_convert_fusion.12
  11.3 0.1 copy.76
  11.4 0.3 convolution_convert_fusion.11
  11.8 0.3 convolution_convert_fusion.10
  12.2 0.3 convolution_convert_fusion.9
  12.8 0.2 maximum_bitcast_fusion
  13.0 0.6 copy.149
  13.6 1.3 reshape.468
  14.9 11.7 %all-to-all-start = ((bf16[128,2,384]{2,1,0:T(2,128)(2,1)}), bf16[128,2,384]{2,1,0:T(2,128)(2,1)S(1)}, u32[]{:S(2)}, u32[]{:S(2)}) async-start(bf16[128,2,384]{2,1,0:T(2,128)(2,1)} %reshape.468), calls=%async_computation | async-start | bytes 393216 | tf_op jit(solution)/shard_map/all_to_all | solution.py:123
  26.8 0.5 fusion.7
  27.3 0.3 copy.91
  27.6 0.6 convolution_convert_fusion
  28.1 0.9 copy.111
  29.0 2.0 copy.145
  31.0 0.5 fusion.6
  31.5 0.3 copy.89
  31.8 0.6 convolution_convert_fusion.1
  32.4 0.9 copy.109
  33.3 2.0 copy.146
  35.4 0.5 fusion.5
  35.9 0.3 copy.87
  36.2 0.6 convolution_convert_fusion.2
  36.7 0.9 copy.107
  37.6 2.0 copy.147
  39.6 0.5 fusion.4
  40.1 0.3 copy.85
  40.4 0.6 convolution_convert_fusion.3
  41.0 0.9 copy.105
  41.9 1.1 copy.148
  43.0 0.4 copy-done.2
  43.4 0.5 copy-done.3
  43.9 0.8 pad_maximum_fusion
  44.7 7.5 %copy.93 = bf16[128,4,6,1024]{3,1,2,0:T(4,128)(2,1)} copy(bf16[128,4,6,1024]{3,0,2,1:T(8,128)(2,1)S(1)} %pad_maximum_fusion) | data formatting | bytes 12582912 | tf_op jit(solution)/shard_map/stack | solution.py:120
  52.2 10.2 %all-to-all-start.1 = ((bf16[128,4,6,1024]{3,1,2,0:T(4,128)(2,1)}), bf16[128,4,6,1024]{3,1,2,0:T(4,128)(2,1)}, u32[]{:S(2)}, u32[]{:S(2)}) async-start(bf16[128,4,6,1024]{3,1,2,0:T(4,128)(2,1)} %copy.93), calls=%async_computation.1 | async-start | bytes 12582912 | tf_op jit(solution)/shard_map/all_to_all | solution.py:122
  62.4 0.4 reshape.469
  62.8 0.8 convert_reduce_fusion
  63.6 78.4 %all-to-all-done.1 = bf16[128,4,6,1024]{3,1,2,0:T(4,128)(2,1)} async-done(((bf16[128,4,6,1024]{3,1,2,0:T(4,128)(2,1)}), bf16[128,4,6,1024]{3,1,2,0:T(4,128)(2,1)}, u32[]{:S(2)}, u32[]{:S(2)}) %all-to-all-start.1) | async-done | bytes 6291488 | tf_op jit(solution)/shard_map/all_to_all | solution.py:122
  142.0 9.7 %fusion.8 = f32[4,32,1024]{2,1,0:T(8,128)S(1)} fusion(bf16[128,4,6,1024]{3,1,2,0:T(4,128)(2,1)} %all-to-all-done.1, bf16[128,4,6,32]{3,1,2,0:T(4,128)(2,1)S(1)} %bitcast.199), kind=kOutput, calls=%fused_computation.23 | convolution fusion | flops 201326592 | bytes 7012352 | tf_op jit(solution)/shard_map/dot_general | solution.py:124
  151.7 1.0 convert_bitcast_fusion.3
  152.7 0.1 convert_bitcast_fusion.1
  152.8 0.1 convert_bitcast_fusion
  153.0 1.8 broadcast_in_dim.5
  154.8 4.0 %all-to-all-start.2 = ((bf16[8,4,32,8,128]{4,3,2,1,0:T(8,128)(2,1)}), bf16[8,4,32,8,128]{4,3,2,1,0:T(8,128)(2,1)S(1)}, u32[]{:S(2)}, u32[]{:S(2)}) async-start(bf16[8,4,32,8,128]{4,3,2,1,0:T(8,128)(2,1)} %broadcast_in_dim.5), calls=%async_computation.2 | async-start | bytes 4194304 | tf_op jit(solution)/shard_map/all_to_all | solution.py:136
  159.0 0.1 copy.99
  159.1 26.8 %all-to-all-done.2 = bf16[8,4,32,8,128]{4,3,2,1,0:T(8,128)(2,1)S(1)} async-done(((bf16[8,4,32,8,128]{4,3,2,1,0:T(8,128)(2,1)}), bf16[8,4,32,8,128]{4,3,2,1,0:T(8,128)(2,1)S(1)}, u32[]{:S(2)}, u32[]{:S(2)}) %all-to-all-start.2) | async-done | bytes 2097184 | tf_op jit(solution)/shard_map/all_to_all | solution.py:136
  185.9 1.4 fusion.2
  187.3 0.7 convert_element_type.133
  188.1 61.2 %all-gather.5.cloned.1.call-done.r_ref = bf16[4,32,128,128]{3,2,1,0:T(8,128)(2,1)} async-done(((bf16[4,32,8,128]{3,2,1,0:T(8,128)(2,1)}), bf16[4,32,128,128]{3,2,1,0:T(8,128)(2,1)}) %all-gather.5.cloned.1.call-update) | async-done | bytes 4194320 | tf_op jit(solution)/shard_map/all_gather | solution.py:140
  249.3 1.2 slice.109
  251.2 0.7 broadcast_add_fusion
  251.9 0.6 fusion.33.sel_ref
  252.5 1.1 convolution_convert_fusion.8
  253.7 37.6 %shard_map.95 = f32[4,32,16,128]{3,2,1,0:T(8,128)} custom-call(bf16[2,1024,128]{2,1,0:T(8,128)(2,1)} %bitcast.218, bf16[128,256]{1,0:T(8,128)(2,1)} %fusion.33.sel_ref, bf16[4,32,128,128]{3,2,1,0:T(8,128)(2,1)} %all-gather.5.cloned.1.call-done.r_ref), custom_call_target="tpu_custom_call" | custom-call | flops 9663676416 | bytes 5767168 | tf_op jit(solution)/shard_map/pallas_call | solution.py:57
  291.2 1.3 fusion.11
  292.5 0.6 copy.96
  293.2 1.8 mul.230
  294.9 4.0 %all-gather.7.cloned.1.call-done = f32[32,16384]{1,0:T(8,128)} async-done(((f32[32,1024]{1,0:T(8,128)}), f32[32,16384]{1,0:T(8,128)}) %all-gather.7.cloned.1.call-update) | async-done | bytes 2097168 | tf_op jit(solution)/shard_map/all_gather | solution.py:143
  298.9 3.0 copy.151
  (58 shorter events, 1.5 us)
Async XLA Ops:
  12.8 13.8 %copy-start.7 = (s32[4,16]{1,0:T(4,128)S(1)}, s32[4,16]{1,0:T(4,128)}, u32[]{:S(2)}) copy-start(s32[4,16]{1,0:T(4,128)} %param.13) | copy-start | bytes 772
  12.8 13.8 %copy-start.5 = (bf16[16,16384]{1,0:T(8,128)(2,1)S(1)}, bf16[16,16384]{1,0:T(8,128)(2,1)}, u32[]{:S(2)}) copy-start(bf16[16,16384]{1,0:T(8,128)(2,1)} %param.8) | copy-start | bytes 1572868
  14.9 37.4 %all-to-all-start = ((bf16[128,2,384]{2,1,0:T(2,128)(2,1)}), bf16[128,2,384]{2,1,0:T(2,128)(2,1)S(1)}, u32[]{:S(2)}, u32[]{:S(2)}) async-start(bf16[128,2,384]{2,1,0:T(2,128)(2,1)} %reshape.468), calls=%async_computation | async-start | bytes 393216 | tf_op jit(solution)/shard_map/all_to_all | solution.py:123
  26.7 13.0 %copy-start = (bf16[2,8,128,128]{3,2,1,0:T(8,128)(2,1)}, bf16[2,8,128,128]{3,2,1,0:T(8,128)(2,1)S(1)}, u32[]{:S(2)}) copy-start(bf16[2,8,128,128]{3,2,1,0:T(8,128)(2,1)S(1)} %copy.102) | copy-start | bytes 1572868
  41.0 2.0 copy-start.4
  41.9 1.5 copy-start.2
  41.9 2.0 copy-start.3
  52.2 11.4 %copy-start.6 = (f32[32]{0:T(128)S(1)}, f32[32]{0:T(128)}, u32[]{:S(2)}) copy-start(f32[32]{0:T(128)} %param.10) | copy-start | bytes 388
  52.2 89.8 %all-to-all-start.1 = ((bf16[128,4,6,1024]{3,1,2,0:T(4,128)(2,1)}), bf16[128,4,6,1024]{3,1,2,0:T(4,128)(2,1)}, u32[]{:S(2)}, u32[]{:S(2)}) async-start(bf16[128,4,6,1024]{3,1,2,0:T(4,128)(2,1)} %copy.93), calls=%async_computation.1 | async-start | bytes 12582912 | tf_op jit(solution)/shard_map/all_to_all | solution.py:122
  154.8 4.1 %copy-start.8 = (s32[4]{0:T(128)S(1)}, s32[4]{0:T(128)}, u32[]{:S(2)}) copy-start(s32[4]{0:T(128)} %param.15) | copy-start | bytes 52
  154.8 31.1 %all-to-all-start.2 = ((bf16[8,4,32,8,128]{4,3,2,1,0:T(8,128)(2,1)}), bf16[8,4,32,8,128]{4,3,2,1,0:T(8,128)(2,1)S(1)}, u32[]{:S(2)}, u32[]{:S(2)}) async-start(bf16[8,4,32,8,128]{4,3,2,1,0:T(8,128)(2,1)} %broadcast_in_dim.5), calls=%async_computation.2 | async-start | bytes 4194304 | tf_op jit(solution)/shard_map/all_to_all | solution.py:136
  158.9 93.6 %copy-start.1 = (bf16[2,8,128,128]{3,2,1,0:T(8,128)(2,1)S(1)}, bf16[2,8,128,128]{3,2,1,0:T(8,128)(2,1)}, u32[]{:S(2)}) copy-start(bf16[2,8,128,128]{3,2,1,0:T(8,128)(2,1)} %copy-done) | copy-start | bytes 1572868
  158.9 90.4 %all-gather.5.cloned.1.call-start = ((), (), s32[]{:S(2)}) async-start(), calls=%async_computation.3 | async-start | bytes 4456448 | tf_op jit(solution)/shard_map/all_gather | solution.py:140
  188.1 110.8 %all-gather.7.cloned.1.call-start = ((), (), s32[]{:S(2)}) async-start(), calls=%async_computation.4 | async-start | bytes 2228224 | tf_op jit(solution)/shard_map/all_gather | solution.py:143
Sparse Core Ops, SparseCore 0:
  188.2 61.0 all-gather.4
  252.0 46.9 all-gather.6

commit v15 on v10

--- a/solution.py
+++ b/solution.py
@@ -119,8 +119,21 @@
         send_wts.append(wts)
     send_img = jnp.stack(send_img, axis=2).reshape(doms * groups, STEPS, capacity, chunk)
     send_wts = jnp.stack(send_wts, axis=2).reshape(doms * groups, STEPS, capacity, per_group)
-    got_img = lax.all_to_all(send_img, ("dom", "cls"), 0, 0, tiled=True)
-    got_wts = lax.all_to_all(send_wts, ("dom", "cls"), 0, 0, tiled=True)
+    dests = doms * groups
+    img_len = capacity * chunk
+    wts_len = capacity * per_group
+    pad = -wts_len % 128
+    packed = jnp.concatenate(
+        [
+            send_img.reshape(dests, STEPS, img_len),
+            send_wts.reshape(dests, STEPS, wts_len),
+            jnp.zeros((dests, STEPS, pad), jnp.bfloat16),
+        ],
+        axis=2,
+    )
+    got = lax.all_to_all(packed, ("dom", "cls"), 0, 0, tiled=True)
+    got_img = got[:, :, :img_len].reshape(dests, STEPS, capacity, chunk)
+    got_wts = got[:, :, img_len:img_len + wts_len].reshape(dests, STEPS, capacity, per_group)
     totals = lax.dot_general(
         got_wts, got_img, (((0, 2), (0, 2)), ((1,), (1,))), preferred_element_type=jnp.float32
     )

time: 308 us -> 333 us (1.081)
  local copies, waits for them, and re-layouts: 40.2 us -> 70.5 us
  starting transfers between devices: 26 us -> 16.1 us
  other arithmetic: 7.42 us -> 13 us
  matrix products: 17.4 us -> 12.4 us
  waiting for transfers between devices: 163 us -> 167 us
    concatenate x0 -> x2, local copies, waits for them, and re-layouts: none -> 20.7 us  [per_device(): jnp.concatenate([send_img.reshape(dests, STEPS, img_len), send_wts.reshap...]
    all_to_all x2 -> x1, starting transfers between devices: 21.8 us -> 11.9 us  [per_device(): got = lax.all_to_all(packed, ('dom', 'cls'), 0, 0, tiled=True)]
    unnamed x26 -> x17, local copies, waits for them, and re-layouts: 11.6 us -> 21.3 us
    slice x0 -> x3, local copies, waits for them, and re-layouts: none -> 9.71 us  [the longest x1 8.44 us: per_device(): got_img = got[:, :, :img_len].reshape(dests, STEPS, capacity, chunk)]
    another operation x1, local copies, waits for them, and re-layouts: 7.51 us -> 0.6 us  [per_device(): send_wts.reshape(dests, STEPS, wts_len)]
    dot_general x1, matrix products: 9.67 us -> 4.7 us  [per_device(): lax.dot_general(got_wts, got_img, (((0, 2), (0, 2)), ((1,), (1,))), prefe...]
    another operation x1, other arithmetic: 0.82 us -> 5.79 us  [per_device(): jnp.stack(send_img, axis=2).reshape(doms * groups, STEPS, capacity, chunk)]
    all_to_all x2 -> x1, waiting for transfers between devices: 78.4 us -> 82.7 us  [per_device(): got = lax.all_to_all(packed, ('dom', 'cls'), 0, 0, tiled=True)]
  transfers between devices with their start and end apart: 5 -> 4, of which waited for: 3 -> 3; matrix products, arithmetic and copies ran while one was open for 12% -> 3% of each run, Pallas kernels for 12% -> 11%
where the time goes in v15:
time: 333 us; the launch traced here: 332 us
  waiting for transfers between devices  167 us (50%)
  local copies, waits for them, and re-layouts  70.5 us (21%)
  Pallas kernels  37.6 us (11%)
  starting transfers between devices  16.1 us (5%)
  between operations  15.1 us (5%)
  other arithmetic  13 us (4%)
  matrix products  12.4 us (4%)
    all_to_all x1, waiting for transfers between devices, per_device(): got = lax.all_to_all(packed, ('dom', 'cls'), 0, 0, tiled=True)  82.7 us
    all_gather x1, waiting for transfers between devices, per_device(): all_refs = lax.all_gather(owner_chunk, 'dom', axis=2, tiled=False)  57.5 us
    pallas_call x1, Pallas kernels, shift_scores(): pl.pallas_call(_scores_kernel, grid=(steps,), in_specs=[pl.BlockSpec((ast...  37.6 us
    all_to_all x1, waiting for transfers between devices, per_device(): got_refs = lax.all_to_all(ref_chunks, 'cls', 0, 0, tiled=True)  26.9 us
    unnamed x17, local copies, waits for them, and re-layouts  21.3 us
    concatenate x2, local copies, waits for them, and re-layouts, per_device(): jnp.concatenate([send_img.reshape(dests, STEPS, img_len), send_wts.reshap...  20.7 us
    all_to_all x1, starting transfers between devices, per_device(): got = lax.all_to_all(packed, ('dom', 'cls'), 0, 0, tiled=True)  11.9 us
    slice x1, local copies, waits for them, and re-layouts, per_device(): got_img = got[:, :, :img_len].reshape(dests, STEPS, capacity, chunk)  8.44 us
  transfers between devices with their start and end apart: 4, of which 3 were waited for; matrix products, arithmetic and copies ran while one was open for 3% of the time, Pallas kernels for 11%

profile of v15, /device:TPU:1, one launch (start us, length us, event | category | flops | bytes accessed | tf_op | source)
XLA Modules:
  0.0 331.8 jit_solution(6560817477597136478)
XLA Ops:
  7.2 1.1 copy.58
  8.3 0.8 multiply_bitcast_fusion.3
  9.2 0.5 fusion.5
  9.7 0.3 copy.38
  10.5 0.2 select_reduce_fusion.2
  10.6 0.2 select_reduce_fusion
  10.8 0.6 convolution_convert_fusion
  11.4 0.9 copy.67
  12.3 0.9 copy.39
  13.2 0.5 fusion.4
  13.7 0.3 copy.36
  13.9 0.6 convolution_convert_fusion.1
  14.5 0.9 copy.65
  15.4 2.0 copy.37
  17.5 0.5 fusion.3
  18.0 0.3 copy.34
  18.3 0.6 convolution_convert_fusion.2
  18.8 0.9 copy.63
  19.7 2.0 copy.35
  21.7 0.5 fusion.2
  22.2 0.3 copy.32
  22.5 0.6 convolution_convert_fusion.3
  23.1 0.9 copy.61
  24.0 2.2 copy.33
  26.2 0.3 convolution_convert_fusion.9
  26.5 0.1 copy.43
  26.6 0.3 convolution_convert_fusion.10
  26.8 0.1 copy.42
  27.0 0.3 convolution_convert_fusion.11
  27.2 0.1 copy.41
  27.3 0.3 convolution_convert_fusion.12
  27.9 0.3 pad_maximum_fusion.1
  28.3 0.6 reshape_reshape.7
  28.9 5.8 %pad_maximum_fusion = bf16[128,4,6144]{2,0,1:T(8,128)(2,1)} fusion(bf16[128,1,6144]{2,0,1:T(8,128)(2,1)S(1)} %bitcast.190, bf16[128,1,6144]{2,0,1:T(8,128)(2,1)} %bitcast.191, bf16[128,1,6144]{2,0,1:T(8,128)(2,1)} %bitcast.192, bf16[128,1,6144]{2,0,1:T(8,128)(2,1)} %bitcast.193), kind=kLoop, calls=%fused_computation.4 | loop fusion | flops 9437184 | bytes 12582912 | tf_op jit(solution)/shard_map/stack | solution.py:120
  34.7 10.1 %concatenate.4 = bf16[128,4,6400]{2,0,1:T(8,128)(2,1)} concatenate(bf16[128,4,6144]{2,0,1:T(8,128)(2,1)} %pad_maximum_fusion, bf16[128,4,192]{2,0,1:T(8,128)(2,1)S(1)} %reshape_reshape.7, bf16[128,4,64]{2,0,1:T(8,128)(2,1)S(1)} %broadcast_in_dim.4), dimensions={2} | concatenate | bytes 13107200 | tf_op jit(solution)/shard_map/concatenate | solution.py:126
  44.8 10.6 %copy.44 = bf16[128,4,6400]{2,1,0:T(4,128)(2,1)} copy(bf16[128,4,6400]{2,0,1:T(8,128)(2,1)} %concatenate.4) | data formatting | bytes 13107200 | tf_op jit(solution)/shard_map/concatenate | solution.py:126
  55.4 11.9 %all-to-all-start = ((bf16[128,4,6400]{2,1,0:T(4,128)(2,1)}), bf16[128,4,6400]{2,1,0:T(4,128)(2,1)}, u32[]{:S(2)}, u32[]{:S(2)}) async-start(bf16[128,4,6400]{2,1,0:T(4,128)(2,1)} %copy.44), calls=%async_computation | async-start | bytes 13107200 | tf_op jit(solution)/shard_map/all_to_all | solution.py:134
  67.3 82.7 %all-to-all-done = bf16[128,4,6400]{2,1,0:T(4,128)(2,1)} async-done(((bf16[128,4,6400]{2,1,0:T(4,128)(2,1)}), bf16[128,4,6400]{2,1,0:T(4,128)(2,1)}, u32[]{:S(2)}, u32[]{:S(2)}) %all-to-all-start) | async-done | bytes 6553632 | tf_op jit(solution)/shard_map/all_to_all | solution.py:134
  150.0 1.1 convert_reduce_fusion
  151.2 1.0 slice.112
  152.3 0.2 copy.45
  152.5 8.4 %slice.113 = bf16[128,4,6144]{2,1,0:T(4,128)(2,1)} slice(bf16[128,4,6400]{2,1,0:T(4,128)(2,1)} %all-to-all-done), slice={[0:128], [0:4], [0:6144]} | slice | bytes 12582912 | tf_op jit(solution)/shard_map/slice | solution.py:135
  160.9 11.2 %copy.56 = bf16[128,4,6144]{0,2,1:T(8,128)(2,1)} copy(bf16[128,4,6144]{2,1,0:T(4,128)(2,1)} %slice.113) | data formatting | bytes 12582912
  172.2 4.7 %convolution_bitcast_fusion = f32[4,32,1024]{2,1,0:T(8,128)S(1)} fusion(bf16[128,4,6,32]{0,3,2,1:T(8,128)(2,1)S(1)} %bitcast.211, bf16[128,4,6,1024]{0,3,2,1:T(8,128)(2,1)} %bitcast.184), kind=kOutput, calls=%fused_computation.16 | convolution fusion | flops 201326592 | bytes 7012352 | tf_op jit(solution)/shard_map/dot_general | solution.py:137
  176.9 1.0 convert_bitcast_fusion.3
  177.9 0.1 convert_bitcast_fusion.1
  178.0 0.1 convert_bitcast_fusion
  178.2 1.6 broadcast_in_dim.5
  179.8 4.1 %all-to-all-start.1 = ((bf16[8,4,32,1024]{3,2,1,0:T(8,128)(2,1)}), bf16[8,4,32,1024]{3,2,1,0:T(8,128)(2,1)S(1)}, u32[]{:S(2)}, u32[]{:S(2)}) async-start(bf16[8,4,32,1024]{3,2,1,0:T(8,128)(2,1)} %broadcast_in_dim.5), calls=%async_computation.1 | async-start | bytes 4194304 | tf_op jit(solution)/shard_map/all_to_all | solution.py:149
  184.0 0.1 copy.53
  184.1 26.9 %all-to-all-done.1 = bf16[8,4,32,1024]{3,2,1,0:T(8,128)(2,1)S(1)} async-done(((bf16[8,4,32,1024]{3,2,1,0:T(8,128)(2,1)}), bf16[8,4,32,1024]{3,2,1,0:T(8,128)(2,1)S(1)}, u32[]{:S(2)}, u32[]{:S(2)}) %all-to-all-start.1) | async-done | bytes 2097184 | tf_op jit(solution)/shard_map/all_to_all | solution.py:149
  210.9 1.4 fusion
  212.4 0.8 copy.88
  213.2 57.5 %all-gather.5.cloned.1.call-done = bf16[4,32,16384]{2,1,0:T(8,128)(2,1)} async-done(((bf16[4,32,1024]{2,1,0:T(8,128)(2,1)}), bf16[4,32,16384]{2,1,0:T(8,128)(2,1)}) %all-gather.5.cloned.1.call-update) | async-done | bytes 4194320 | tf_op jit(solution)/shard_map/all_gather | solution.py:153
  270.7 1.2 slice.119
  272.6 0.7 broadcast_add_fusion
  273.3 0.6 fusion.27.sel_ref
  274.0 1.1 convolution_convert_fusion.8
  275.1 5.4 %copy.68 = bf16[16,8,128,128]{3,2,1,0:T(8,128)(2,1)} copy(bf16[16,8,128,128]{3,1,2,0:T(8,128)(2,1)} %bitcast.202) | data formatting | bytes 8388608
  280.5 37.6 %shard_map.95 = f32[4,32,16,128]{3,2,1,0:T(8,128)} custom-call(bf16[2,1024,128]{2,1,0:T(8,128)(2,1)} %bitcast.212, bf16[128,256]{1,0:T(8,128)(2,1)} %fusion.27.sel_ref, bf16[4,32,128,128]{3,2,1,0:T(8,128)(2,1)} %bitcast.203), custom_call_target="tpu_custom_call" | custom-call | flops 9663676416 | bytes 5767168 | tf_op jit(solution)/shard_map/pallas_call | solution.py:57
  318.1 1.3 fusion.6
  319.4 0.6 copy.48
  320.0 1.8 mul.230
  321.8 3.2 copy.57
  (47 shorter events, 1.3 us)
Async XLA Ops:
  7.2 2.8 copy-start
  24.0 2.2 copy-start.3
  24.0 2.2 copy-start.2
  55.4 94.7 %all-to-all-start = ((bf16[128,4,6400]{2,1,0:T(4,128)(2,1)}), bf16[128,4,6400]{2,1,0:T(4,128)(2,1)}, u32[]{:S(2)}, u32[]{:S(2)}) async-start(bf16[128,4,6400]{2,1,0:T(4,128)(2,1)} %copy.44), calls=%async_computation | async-start | bytes 13107200 | tf_op jit(solution)/shard_map/all_to_all | solution.py:134
  160.9 11.2 %copy-start.1 = (f32[32]{0:T(128)S(1)}, f32[32]{0:T(128)}, u32[]{:S(2)}) copy-start(f32[32]{0:T(128)} %param.10) | copy-start | bytes 388
  179.8 4.2 %copy-start.4 = (s32[4]{0:T(128)S(1)}, s32[4]{0:T(128)}, u32[]{:S(2)}) copy-start(s32[4]{0:T(128)} %param.15) | copy-start | bytes 52
  179.8 31.2 %all-to-all-start.1 = ((bf16[8,4,32,1024]{3,2,1,0:T(8,128)(2,1)}), bf16[8,4,32,1024]{3,2,1,0:T(8,128)(2,1)S(1)}, u32[]{:S(2)}, u32[]{:S(2)}) async-start(bf16[8,4,32,1024]{3,2,1,0:T(8,128)(2,1)} %broadcast_in_dim.5), calls=%async_computation.1 | async-start | bytes 4194304 | tf_op jit(solution)/shard_map/all_to_all | solution.py:149
  183.9 86.8 %all-gather.5.cloned.1.call-start = ((), (), s32[]{:S(2)}) async-start(), calls=%async_computation.2 | async-start | bytes 4456448 | tf_op jit(solution)/shard_map/all_gather | solution.py:153
  213.2 108.6 %all-gather.7.cloned.1.call-start = ((), (), s32[]{:S(2)}) async-start(), calls=%async_computation.3 | async-start | bytes 2228224 | tf_op jit(solution)/shard_map/all_gather | solution.py:156
Sparse Core Ops, SparseCore 0:
  213.3 57.3 all-gather.4
  273.4 47.0 all-gather.6

commit v16 on v10

--- a/solution.py
+++ b/solution.py
@@ -1,3 +1,4 @@
+import functools
 import math
 
 import jax
@@ -14,7 +15,7 @@
 ASTEP = 2
 
 
-def _scores_kernel(pt_ref, sel_ref, r_ref, o_ref, split_ref):
+def _scores_kernel(scale, pt_ref, sel_ref, r_ref, o_ref, split_ref):
     classes = r_ref.shape[1]
     radii = r_ref.shape[2]
     per_dev = o_ref.shape[2]
@@ -35,7 +36,7 @@
         g = jnp.dot(pt, rhs, preferred_element_type=jnp.float32)
         for h in range(2):
             gh = pltpu.roll(g[:, h * lanes:(h + 1) * lanes], 0, 1, stride=1, stride_axis=0)
-            o_ref[0, 2 * j + h] = jnp.sum(gh.reshape(per_dev, rows, lanes), axis=1)
+            o_ref[0, 2 * j + h] = jnp.sum(gh.reshape(per_dev, rows, lanes), axis=1) * scale
         return carry
 
     lax.fori_loop(0, classes // 2, body, 0)
@@ -55,7 +56,7 @@
     sel = (b == astep * ((col % 128) % turns) + col // 128).astype(cube.dtype)
     flops = 2 * steps * classes * (n * turns * radii * astep * 128 + radii * angles * astep * 128)
     return pl.pallas_call(
-        _scores_kernel,
+        functools.partial(_scores_kernel, 1.0 / math.sqrt(radii * angles)),
         grid=(steps,),
         in_specs=[
             pl.BlockSpec((astep, n * turns, radii), lambda s: (0, 0, 0)),
@@ -145,7 +146,7 @@
 
     shifted = shift_scores(cube, all_refs.reshape(STEPS, per_group, RADII, ANGLES), ASTEP)
     scores = shifted.transpose(0, 2, 3, 1).reshape(STEPS, per_dev, ROT * per_group)
-    return (scores * scale, final)
+    return (scores, final)
 
 
 def solution(mesh):

time: 308 us -> 308 us (level)
  no operation moved by 1% of the time
where the time goes in v16:
time: 308 us; the launch traced here: 307 us
  waiting for transfers between devices  163 us (53%)
  local copies, waits for them, and re-layouts  41.5 us (13%)
  Pallas kernels  37.8 us (12%)
  starting transfers between devices  26 us (8%)
  matrix products  17.4 us (6%)
  between operations  15.1 us (5%)
  other arithmetic  6.11 us (2%)
    all_to_all x1, waiting for transfers between devices, per_device(): got_img = lax.all_to_all(send_img, ('dom', 'cls'), 0, 0, tiled=True)  78.4 us
    all_gather x1, waiting for transfers between devices, per_device(): all_refs = lax.all_gather(owner_chunk, 'dom', axis=2, tiled=False)  58.1 us
    pallas_call x1, Pallas kernels, shift_scores(): pl.pallas_call(functools.partial(_scores_kernel, 1.0 / math.sqrt(radii *...  37.8 us
    all_to_all x1, waiting for transfers between devices, per_device(): got_refs = lax.all_to_all(ref_chunks, 'cls', 0, 0, tiled=True)  26.8 us
    all_to_all x1, starting transfers between devices, per_device(): got_wts = lax.all_to_all(send_wts, ('dom', 'cls'), 0, 0, tiled=True)  11.7 us
    unnamed x26, local copies, waits for them, and re-layouts  11.6 us
    all_to_all x1, starting transfers between devices, per_device(): got_img = lax.all_to_all(send_img, ('dom', 'cls'), 0, 0, tiled=True)  10.2 us
    dot_general x1, matrix products, per_device(): lax.dot_general(got_wts, got_img, (((0, 2), (0, 2)), ((1,), (1,))), prefe...  9.67 us
  transfers between devices with their start and end apart: 5, of which 3 were waited for; matrix products, arithmetic and copies ran while one was open for 12% of the time, Pallas kernels for 12%

profile of v16, /device:TPU:1, one launch (start us, length us, event | category | flops | bytes accessed | tf_op | source)
XLA Modules:
  0.0 307.3 jit_solution(6586238110512605115)
XLA Ops:
  7.2 0.7 slice_bitcast_fusion.16
  8.3 0.8 slice_bitcast_fusion.15
  9.1 0.8 slice_bitcast_fusion.14
  10.0 0.2 select_reduce_fusion
  10.2 0.2 select_reduce_fusion.2
  10.3 0.7 multiply_add_fusion.3
  11.1 0.2 convolution_convert_fusion.12
  11.3 0.1 copy.80
  11.4 0.3 convolution_convert_fusion.11
  11.8 0.3 convolution_convert_fusion.10
  12.2 0.3 convolution_convert_fusion.9
  12.8 0.2 maximum_bitcast_fusion
  13.0 0.6 copy.154
  13.6 1.3 reshape.466
  14.9 11.7 %all-to-all-start = ((bf16[128,2,384]{2,1,0:T(2,128)(2,1)}), bf16[128,2,384]{2,1,0:T(2,128)(2,1)S(1)}, u32[]{:S(2)}, u32[]{:S(2)}) async-start(bf16[128,2,384]{2,1,0:T(2,128)(2,1)} %reshape.466), calls=%async_computation | async-start | bytes 393216 | tf_op jit(solution)/shard_map/all_to_all | solution.py:124
  26.8 0.5 fusion.7
  27.3 0.3 copy.95
  27.6 0.6 convolution_convert_fusion
  28.1 0.9 copy.117
  29.0 2.0 copy.149
  31.0 0.5 fusion.6
  31.5 0.3 copy.93
  31.8 0.6 convolution_convert_fusion.1
  32.4 0.9 copy.115
  33.3 2.0 copy.150
  35.4 0.5 fusion.5
  35.9 0.3 copy.91
  36.2 0.6 convolution_convert_fusion.2
  36.7 0.9 copy.113
  37.6 2.0 copy.151
  39.6 0.5 fusion.4
  40.1 0.3 copy.89
  40.4 0.6 convolution_convert_fusion.3
  41.0 0.9 copy.111
  41.9 1.1 copy.152
  43.0 0.4 copy-done.2
  43.4 0.5 copy-done.3
  43.9 0.8 pad_maximum_fusion
  44.7 7.5 %copy.97 = bf16[128,4,6,1024]{3,1,2,0:T(4,128)(2,1)} copy(bf16[128,4,6,1024]{3,0,2,1:T(8,128)(2,1)S(1)} %pad_maximum_fusion) | data formatting | bytes 12582912 | tf_op jit(solution)/shard_map/stack | solution.py:121
  52.2 10.2 %all-to-all-start.1 = ((bf16[128,4,6,1024]{3,1,2,0:T(4,128)(2,1)}), bf16[128,4,6,1024]{3,1,2,0:T(4,128)(2,1)}, u32[]{:S(2)}, u32[]{:S(2)}) async-start(bf16[128,4,6,1024]{3,1,2,0:T(4,128)(2,1)} %copy.97), calls=%async_computation.1 | async-start | bytes 12582912 | tf_op jit(solution)/shard_map/all_to_all | solution.py:123
  62.4 0.4 reshape.467
  62.8 0.8 convert_reduce_fusion
  63.6 78.4 %all-to-all-done.1 = bf16[128,4,6,1024]{3,1,2,0:T(4,128)(2,1)} async-done(((bf16[128,4,6,1024]{3,1,2,0:T(4,128)(2,1)}), bf16[128,4,6,1024]{3,1,2,0:T(4,128)(2,1)}, u32[]{:S(2)}, u32[]{:S(2)}) %all-to-all-start.1) | async-done | bytes 6291488 | tf_op jit(solution)/shard_map/all_to_all | solution.py:123
  142.0 9.7 %fusion.8 = f32[4,32,1024]{2,1,0:T(8,128)S(1)} fusion(bf16[128,4,6,1024]{3,1,2,0:T(4,128)(2,1)} %all-to-all-done.1, bf16[128,4,6,32]{3,1,2,0:T(4,128)(2,1)S(1)} %bitcast.198), kind=kOutput, calls=%fused_computation.23 | convolution fusion | flops 201326592 | bytes 7012352 | tf_op jit(solution)/shard_map/dot_general | solution.py:125
  151.7 1.0 convert_bitcast_fusion.3
  152.7 0.1 convert_bitcast_fusion.1
  152.8 0.1 convert_bitcast_fusion
  152.9 1.6 broadcast_in_dim.2
  154.5 4.0 %all-to-all-start.2 = ((bf16[8,4,32,1024]{3,2,1,0:T(8,128)(2,1)}), bf16[8,4,32,1024]{3,2,1,0:T(8,128)(2,1)S(1)}, u32[]{:S(2)}, u32[]{:S(2)}) async-start(bf16[8,4,32,1024]{3,2,1,0:T(8,128)(2,1)} %broadcast_in_dim.2), calls=%async_computation.2 | async-start | bytes 4194304 | tf_op jit(solution)/shard_map/all_to_all | solution.py:137
  158.7 0.1 copy.104
  158.8 26.8 %all-to-all-done.2 = bf16[8,4,32,1024]{3,2,1,0:T(8,128)(2,1)S(1)} async-done(((bf16[8,4,32,1024]{3,2,1,0:T(8,128)(2,1)}), bf16[8,4,32,1024]{3,2,1,0:T(8,128)(2,1)S(1)}, u32[]{:S(2)}, u32[]{:S(2)}) %all-to-all-start.2) | async-done | bytes 2097184 | tf_op jit(solution)/shard_map/all_to_all | solution.py:137
  185.6 1.4 fusion.2
  187.0 0.8 copy.153
  187.9 58.1 %all-gather.5.cloned.1.call-done = bf16[4,32,16384]{2,1,0:T(8,128)(2,1)} async-done(((bf16[4,32,1024]{2,1,0:T(8,128)(2,1)}), bf16[4,32,16384]{2,1,0:T(8,128)(2,1)}) %all-gather.5.cloned.1.call-update) | async-done | bytes 4194320 | tf_op jit(solution)/shard_map/all_gather | solution.py:141
  246.0 1.2 slice.109
  247.8 0.7 broadcast_add_fusion
  248.5 0.6 fusion.32.sel_ref
  249.2 1.1 convolution_convert_fusion.8
  250.3 5.4 %copy.118 = bf16[16,8,128,128]{3,2,1,0:T(8,128)(2,1)} copy(bf16[16,8,128,128]{3,1,2,0:T(8,128)(2,1)} %bitcast.211) | data formatting | bytes 8388608
  255.7 37.8 %shard_map.95 = f32[4,32,16,128]{3,2,1,0:T(8,128)} custom-call(bf16[2,1024,128]{2,1,0:T(8,128)(2,1)} %bitcast.221, bf16[128,256]{1,0:T(8,128)(2,1)} %fusion.32.sel_ref, bf16[4,32,128,128]{3,2,1,0:T(8,128)(2,1)} %bitcast.212), custom_call_target="tpu_custom_call" | custom-call | flops 9663676416 | bytes 5767168 | tf_op jit(solution)/shard_map/pallas_call | solution.py:58
  293.6 1.3 slice_bitcast_fusion
  294.9 0.6 copy.100
  295.5 1.7 reshape.453
  297.3 3.2 %copy.107 = f32[16,4,8,1024]{3,2,0,1:T(8,128)} copy(f32[16,4,8,1024]{3,2,1,0:T(8,128)} %bitcast.218) | data formatting | bytes 4194304 | tf_op jit(solution)/shard_map/reshape | solution.py:145
  (55 shorter events, 1.4 us)
Async XLA Ops:
  12.8 13.8 %copy-start.7 = (s32[4,16]{1,0:T(4,128)S(1)}, s32[4,16]{1,0:T(4,128)}, u32[]{:S(2)}) copy-start(s32[4,16]{1,0:T(4,128)} %param.13) | copy-start | bytes 772
  12.8 13.8 %copy-start.5 = (bf16[16,16384]{1,0:T(8,128)(2,1)S(1)}, bf16[16,16384]{1,0:T(8,128)(2,1)}, u32[]{:S(2)}) copy-start(bf16[16,16384]{1,0:T(8,128)(2,1)} %param.8) | copy-start | bytes 1572868
  14.9 37.4 %all-to-all-start = ((bf16[128,2,384]{2,1,0:T(2,128)(2,1)}), bf16[128,2,384]{2,1,0:T(2,128)(2,1)S(1)}, u32[]{:S(2)}, u32[]{:S(2)}) async-start(bf16[128,2,384]{2,1,0:T(2,128)(2,1)} %reshape.466), calls=%async_computation | async-start | bytes 393216 | tf_op jit(solution)/shard_map/all_to_all | solution.py:124
  26.7 13.0 %copy-start = (bf16[2,8,128,128]{3,2,1,0:T(8,128)(2,1)}, bf16[2,8,128,128]{3,2,1,0:T(8,128)(2,1)S(1)}, u32[]{:S(2)}) copy-start(bf16[2,8,128,128]{3,2,1,0:T(8,128)(2,1)S(1)} %copy.108) | copy-start | bytes 1572868
  41.0 2.0 copy-start.4
  41.9 1.5 copy-start.2
  41.9 2.0 copy-start.3
  52.2 11.4 %copy-start.6 = (f32[32]{0:T(128)S(1)}, f32[32]{0:T(128)}, u32[]{:S(2)}) copy-start(f32[32]{0:T(128)} %param.10) | copy-start | bytes 388
  52.2 89.8 %all-to-all-start.1 = ((bf16[128,4,6,1024]{3,1,2,0:T(4,128)(2,1)}), bf16[128,4,6,1024]{3,1,2,0:T(4,128)(2,1)}, u32[]{:S(2)}, u32[]{:S(2)}) async-start(bf16[128,4,6,1024]{3,1,2,0:T(4,128)(2,1)} %copy.97), calls=%async_computation.1 | async-start | bytes 12582912 | tf_op jit(solution)/shard_map/all_to_all | solution.py:123
  154.5 4.1 %copy-start.8 = (s32[4]{0:T(128)S(1)}, s32[4]{0:T(128)}, u32[]{:S(2)}) copy-start(s32[4]{0:T(128)} %param.15) | copy-start | bytes 52
  154.5 31.1 %all-to-all-start.2 = ((bf16[8,4,32,1024]{3,2,1,0:T(8,128)(2,1)}), bf16[8,4,32,1024]{3,2,1,0:T(8,128)(2,1)S(1)}, u32[]{:S(2)}, u32[]{:S(2)}) async-start(bf16[8,4,32,1024]{3,2,1,0:T(8,128)(2,1)} %broadcast_in_dim.2), calls=%async_computation.2 | async-start | bytes 4194304 | tf_op jit(solution)/shard_map/all_to_all | solution.py:137
  158.6 90.6 %copy-start.1 = (bf16[2,8,128,128]{3,2,1,0:T(8,128)(2,1)S(1)}, bf16[2,8,128,128]{3,2,1,0:T(8,128)(2,1)}, u32[]{:S(2)}) copy-start(bf16[2,8,128,128]{3,2,1,0:T(8,128)(2,1)} %copy-done) | copy-start | bytes 1572868
  158.6 87.4 %all-gather.5.cloned.1.call-start = ((), (), s32[]{:S(2)}) async-start(), calls=%async_computation.3 | async-start | bytes 4456448 | tf_op jit(solution)/shard_map/all_gather | solution.py:141
  187.9 109.4 %all-gather.7.cloned.1.call-start = ((), (), s32[]{:S(2)}) async-start(), calls=%async_computation.4 | async-start | bytes 2228224 | tf_op jit(solution)/shard_map/all_gather | solution.py:144
Sparse Core Ops, SparseCore 0:
  188.0 57.9 all-gather.4
  248.6 47.0 all-gather.6

commit v17 on v10

--- a/solution.py
+++ b/solution.py
@@ -38,7 +38,7 @@
             o_ref[0, 2 * j + h] = jnp.sum(gh.reshape(per_dev, rows, lanes), axis=1)
         return carry
 
-    lax.fori_loop(0, classes // 2, body, 0)
+    lax.fori_loop(0, classes // 2, body, 0, unroll=2)
 
 def shift_scores(cube, refs, astep):
     n, radii, angles = cube.shape

time: 308 us -> 306 us (level)
  Pallas kernels: 37.6 us -> 30.1 us
  waiting for transfers between devices: 163 us -> 169 us
    pallas_call x1, Pallas kernels: 37.6 us -> 30.1 us  [shift_scores(): pl.pallas_call(_scores_kernel, grid=(steps,), in_specs=[pl.BlockSpec((ast...]
    all_gather x1, waiting for transfers between devices: 0.01 us -> 6.17 us  [per_device(): final = lax.all_gather(current, 'dom', axis=0, tiled=False)]
  transfers between devices with their start and end apart: 5 -> 5, of which waited for: 3 -> 4; matrix products, arithmetic and copies ran while one was open for 12% -> 12% of each run, Pallas kernels for 12% -> 10%
where the time goes in v17:
time: 306 us
  waiting for transfers between devices  169 us (55%)
  local copies, waits for them, and re-layouts  40.2 us (13%)
  Pallas kernels  30.1 us (10%)
  starting transfers between devices  26 us (8%)
  matrix products  17.4 us (6%)
  between operations  15.2 us (5%)
  other arithmetic  7.42 us (2%)
    all_to_all x1, waiting for transfers between devices, per_device(): got_img = lax.all_to_all(send_img, ('dom', 'cls'), 0, 0, tiled=True)  78.4 us
    all_gather x1, waiting for transfers between devices, per_device(): all_refs = lax.all_gather(owner_chunk, 'dom', axis=2, tiled=False)  58.1 us
    pallas_call x1, Pallas kernels, shift_scores(): pl.pallas_call(_scores_kernel, grid=(steps,), in_specs=[pl.BlockSpec((ast...  30.1 us
    all_to_all x1, waiting for transfers between devices, per_device(): got_refs = lax.all_to_all(ref_chunks, 'cls', 0, 0, tiled=True)  26.8 us
    all_to_all x1, starting transfers between devices, per_device(): got_wts = lax.all_to_all(send_wts, ('dom', 'cls'), 0, 0, tiled=True)  11.7 us
    unnamed x26, local copies, waits for them, and re-layouts  11.6 us
    all_to_all x1, starting transfers between devices, per_device(): got_img = lax.all_to_all(send_img, ('dom', 'cls'), 0, 0, tiled=True)  10.2 us
    dot_general x1, matrix products, per_device(): lax.dot_general(got_wts, got_img, (((0, 2), (0, 2)), ((1,), (1,))), prefe...  9.67 us
  transfers between devices with their start and end apart: 5, of which 4 were waited for; matrix products, arithmetic and copies ran while one was open for 12% of the time, Pallas kernels for 10%

profile of v17, /device:TPU:1, one launch (start us, length us, event | category | flops | bytes accessed | tf_op | source)
XLA Modules:
  0.0 305.7 jit_solution(9828523111747239221)
XLA Ops:
  7.2 0.7 slice_bitcast_fusion.15
  8.3 0.8 slice_bitcast_fusion.14
  9.1 0.8 slice_bitcast_fusion.13
  10.0 0.2 select_reduce_fusion
  10.2 0.2 select_reduce_fusion.2
  10.3 0.7 multiply_add_fusion.3
  11.1 0.2 convolution_convert_fusion.12
  11.4 0.3 convolution_convert_fusion.11
  11.8 0.3 convolution_convert_fusion.10
  12.2 0.3 convolution_convert_fusion.9
  12.8 0.2 maximum_bitcast_fusion
  13.0 0.6 copy.154
  13.6 1.3 reshape.465
  14.9 11.7 %all-to-all-start = ((bf16[128,2,384]{2,1,0:T(2,128)(2,1)}), bf16[128,2,384]{2,1,0:T(2,128)(2,1)S(1)}, u32[]{:S(2)}, u32[]{:S(2)}) async-start(bf16[128,2,384]{2,1,0:T(2,128)(2,1)} %reshape.465), calls=%async_computation | async-start | bytes 393216 | tf_op jit(solution)/shard_map/all_to_all | solution.py:123
  26.8 0.5 fusion.7
  27.3 0.3 copy.95
  27.6 0.6 convolution_convert_fusion
  28.1 0.9 copy.117
  29.0 2.0 copy.149
  31.0 0.5 fusion.6
  31.5 0.3 copy.93
  31.8 0.6 convolution_convert_fusion.1
  32.4 0.9 copy.115
  33.3 2.0 copy.150
  35.4 0.5 fusion.5
  35.9 0.3 copy.91
  36.2 0.6 convolution_convert_fusion.2
  36.7 0.9 copy.113
  37.6 2.0 copy.151
  39.6 0.5 fusion.4
  40.1 0.3 copy.89
  40.4 0.6 convolution_convert_fusion.3
  41.0 0.9 copy.111
  41.9 1.1 copy.152
  43.0 0.4 copy-done.2
  43.4 0.5 copy-done.3
  43.9 0.8 pad_maximum_fusion
  44.7 7.5 %copy.97 = bf16[128,4,6,1024]{3,1,2,0:T(4,128)(2,1)} copy(bf16[128,4,6,1024]{3,0,2,1:T(8,128)(2,1)S(1)} %pad_maximum_fusion) | data formatting | bytes 12582912 | tf_op jit(solution)/shard_map/stack | solution.py:120
  52.2 10.2 %all-to-all-start.1 = ((bf16[128,4,6,1024]{3,1,2,0:T(4,128)(2,1)}), bf16[128,4,6,1024]{3,1,2,0:T(4,128)(2,1)}, u32[]{:S(2)}, u32[]{:S(2)}) async-start(bf16[128,4,6,1024]{3,1,2,0:T(4,128)(2,1)} %copy.97), calls=%async_computation.1 | async-start | bytes 12582912 | tf_op jit(solution)/shard_map/all_to_all | solution.py:122
  62.4 0.4 reshape.466
  62.8 0.8 convert_reduce_fusion
  63.6 78.4 %all-to-all-done.1 = bf16[128,4,6,1024]{3,1,2,0:T(4,128)(2,1)} async-done(((bf16[128,4,6,1024]{3,1,2,0:T(4,128)(2,1)}), bf16[128,4,6,1024]{3,1,2,0:T(4,128)(2,1)}, u32[]{:S(2)}, u32[]{:S(2)}) %all-to-all-start.1) | async-done | bytes 6291488 | tf_op jit(solution)/shard_map/all_to_all | solution.py:122
  142.0 9.7 %fusion.8 = f32[4,32,1024]{2,1,0:T(8,128)S(1)} fusion(bf16[128,4,6,1024]{3,1,2,0:T(4,128)(2,1)} %all-to-all-done.1, bf16[128,4,6,32]{3,1,2,0:T(4,128)(2,1)S(1)} %bitcast.198), kind=kOutput, calls=%fused_computation.23 | convolution fusion | flops 201326592 | bytes 7012352 | tf_op jit(solution)/shard_map/dot_general | solution.py:124
  151.7 1.0 convert_bitcast_fusion.3
  152.7 0.1 convert_bitcast_fusion.1
  152.8 0.1 convert_bitcast_fusion
  152.9 1.6 broadcast_in_dim.2
  154.5 4.0 %all-to-all-start.2 = ((bf16[8,4,32,1024]{3,2,1,0:T(8,128)(2,1)}), bf16[8,4,32,1024]{3,2,1,0:T(8,128)(2,1)S(1)}, u32[]{:S(2)}, u32[]{:S(2)}) async-start(bf16[8,4,32,1024]{3,2,1,0:T(8,128)(2,1)} %broadcast_in_dim.2), calls=%async_computation.2 | async-start | bytes 4194304 | tf_op jit(solution)/shard_map/all_to_all | solution.py:136
  158.7 0.1 copy.104
  158.8 26.8 %all-to-all-done.2 = bf16[8,4,32,1024]{3,2,1,0:T(8,128)(2,1)S(1)} async-done(((bf16[8,4,32,1024]{3,2,1,0:T(8,128)(2,1)}), bf16[8,4,32,1024]{3,2,1,0:T(8,128)(2,1)S(1)}, u32[]{:S(2)}, u32[]{:S(2)}) %all-to-all-start.2) | async-done | bytes 2097184 | tf_op jit(solution)/shard_map/all_to_all | solution.py:136
  185.6 1.4 fusion.2
  187.0 0.8 copy.153
  187.9 58.1 %all-gather.5.cloned.1.call-done = bf16[4,32,16384]{2,1,0:T(8,128)(2,1)} async-done(((bf16[4,32,1024]{2,1,0:T(8,128)(2,1)}), bf16[4,32,16384]{2,1,0:T(8,128)(2,1)}) %all-gather.5.cloned.1.call-update) | async-done | bytes 4194320 | tf_op jit(solution)/shard_map/all_gather | solution.py:140
  246.0 1.2 slice.109
  247.8 0.7 broadcast_add_fusion
  248.5 0.6 fusion.33.sel_ref
  249.2 1.1 convolution_convert_fusion.8
  250.3 5.4 %copy.118 = bf16[16,8,128,128]{3,2,1,0:T(8,128)(2,1)} copy(bf16[16,8,128,128]{3,1,2,0:T(8,128)(2,1)} %bitcast.211) | data formatting | bytes 8388608
  255.7 30.1 %shard_map.95 = f32[4,32,16,128]{3,2,1,0:T(8,128)} custom-call(bf16[2,1024,128]{2,1,0:T(8,128)(2,1)} %bitcast.221, bf16[128,256]{1,0:T(8,128)(2,1)} %fusion.33.sel_ref, bf16[4,32,128,128]{3,2,1,0:T(8,128)(2,1)} %bitcast.212), custom_call_target="tpu_custom_call" | custom-call | flops 9663676416 | bytes 5767168 | tf_op jit(solution)/shard_map/pallas_call | solution.py:57
  285.9 1.3 fusion.11
  287.2 0.6 copy.100
  287.8 1.8 mul.230
  289.6 6.2 %all-gather.7.cloned.1.call-done = f32[512,1024]{1,0:T(8,128)} async-done(((f32[32,1024]{1,0:T(8,128)}), f32[512,1024]{1,0:T(8,128)}) %all-gather.7.cloned.1.call-update) | async-done | bytes 2097168 | tf_op jit(solution)/shard_map/all_gather | solution.py:143
  295.7 3.2 %copy.107 = f32[16,4,8,1024]{3,2,0,1:T(8,128)} copy(f32[16,4,8,1024]{3,2,1,0:T(8,128)} %bitcast.218) | data formatting | bytes 4194304 | tf_op jit(solution)/shard_map/reshape | solution.py:144
  (55 shorter events, 1.5 us)
Async XLA Ops:
  12.8 13.8 %copy-start.7 = (s32[4,16]{1,0:T(4,128)S(1)}, s32[4,16]{1,0:T(4,128)}, u32[]{:S(2)}) copy-start(s32[4,16]{1,0:T(4,128)} %param.13) | copy-start | bytes 772
  12.8 13.8 %copy-start.5 = (bf16[16,16384]{1,0:T(8,128)(2,1)S(1)}, bf16[16,16384]{1,0:T(8,128)(2,1)}, u32[]{:S(2)}) copy-start(bf16[16,16384]{1,0:T(8,128)(2,1)} %param.8) | copy-start | bytes 1572868
  14.9 37.4 %all-to-all-start = ((bf16[128,2,384]{2,1,0:T(2,128)(2,1)}), bf16[128,2,384]{2,1,0:T(2,128)(2,1)S(1)}, u32[]{:S(2)}, u32[]{:S(2)}) async-start(bf16[128,2,384]{2,1,0:T(2,128)(2,1)} %reshape.465), calls=%async_computation | async-start | bytes 393216 | tf_op jit(solution)/shard_map/all_to_all | solution.py:123
  26.7 13.0 %copy-start = (bf16[2,8,128,128]{3,2,1,0:T(8,128)(2,1)}, bf16[2,8,128,128]{3,2,1,0:T(8,128)(2,1)S(1)}, u32[]{:S(2)}) copy-start(bf16[2,8,128,128]{3,2,1,0:T(8,128)(2,1)S(1)} %copy.108) | copy-start | bytes 1572868
  41.0 2.0 copy-start.4
  41.9 1.5 copy-start.2
  41.9 2.0 copy-start.3
  52.2 11.4 %copy-start.6 = (f32[32]{0:T(128)S(1)}, f32[32]{0:T(128)}, u32[]{:S(2)}) copy-start(f32[32]{0:T(128)} %param.10) | copy-start | bytes 388
  52.2 89.8 %all-to-all-start.1 = ((bf16[128,4,6,1024]{3,1,2,0:T(4,128)(2,1)}), bf16[128,4,6,1024]{3,1,2,0:T(4,128)(2,1)}, u32[]{:S(2)}, u32[]{:S(2)}) async-start(bf16[128,4,6,1024]{3,1,2,0:T(4,128)(2,1)} %copy.97), calls=%async_computation.1 | async-start | bytes 12582912 | tf_op jit(solution)/shard_map/all_to_all | solution.py:122
  154.5 4.1 %copy-start.8 = (s32[4]{0:T(128)S(1)}, s32[4]{0:T(128)}, u32[]{:S(2)}) copy-start(s32[4]{0:T(128)} %param.15) | copy-start | bytes 52
  154.5 31.1 %all-to-all-start.2 = ((bf16[8,4,32,1024]{3,2,1,0:T(8,128)(2,1)}), bf16[8,4,32,1024]{3,2,1,0:T(8,128)(2,1)S(1)}, u32[]{:S(2)}, u32[]{:S(2)}) async-start(bf16[8,4,32,1024]{3,2,1,0:T(8,128)(2,1)} %broadcast_in_dim.2), calls=%async_computation.2 | async-start | bytes 4194304 | tf_op jit(solution)/shard_map/all_to_all | solution.py:136
  158.6 90.6 %copy-start.1 = (bf16[2,8,128,128]{3,2,1,0:T(8,128)(2,1)S(1)}, bf16[2,8,128,128]{3,2,1,0:T(8,128)(2,1)}, u32[]{:S(2)}) copy-start(bf16[2,8,128,128]{3,2,1,0:T(8,128)(2,1)} %copy-done) | copy-start | bytes 1572868
  158.6 87.4 %all-gather.5.cloned.1.call-start = ((), (), s32[]{:S(2)}) async-start(), calls=%async_computation.3 | async-start | bytes 4456448 | tf_op jit(solution)/shard_map/all_gather | solution.py:140
  187.9 107.9 %all-gather.7.cloned.1.call-start = ((), (), s32[]{:S(2)}) async-start(), calls=%async_computation.4 | async-start | bytes 2228224 | tf_op jit(solution)/shard_map/all_gather | solution.py:143
Sparse Core Ops, SparseCore 0:
  188.0 57.9 all-gather.4
  248.6 47.0 all-gather.6

commit v18 on v17

--- a/solution.py
+++ b/solution.py
@@ -139,8 +139,7 @@
     owner_chunk = owner_chunk.astype(jnp.bfloat16)
     all_refs = lax.all_gather(owner_chunk, "dom", axis=2, tiled=False)
     all_refs = all_refs.reshape(STEPS, per_group, pixels)
-    current = current + 0.0 * all_refs[0, 0, 0].astype(jnp.float32)
-    final = lax.all_gather(current, "dom", axis=0, tiled=False)
+    final = lax.all_to_all(jnp.broadcast_to(current[None], (doms,) + current.shape), "dom", 0, 0, tiled=True)
     final = final.transpose(1, 0, 2).reshape(per_group, pixels)
 
     shifted = shift_scores(cube, all_refs.reshape(STEPS, per_group, RADII, ANGLES), ASTEP)

time: 306 us -> 316 us (1.033)
  local copies, waits for them, and re-layouts: 40.2 us -> 49.6 us
  starting transfers between devices: 26 us -> 33.5 us
    all_to_all x0 -> x1, waiting for transfers between devices: none -> 29.7 us  [per_device(): lax.all_to_all(jnp.broadcast_to(current[None], (doms,) + current.shape),...]
    all_gather x1, waiting for transfers between devices: 58.1 us -> 30.8 us  [per_device(): all_refs = lax.all_gather(owner_chunk, 'dom', axis=2, tiled=False)]
    reshape x4, local copies, waits for them, and re-layouts: 7.19 us -> 18.8 us  [per_device(): images = images.reshape(groups, capacity, doms, chunk).transpose(2, 0, 1, 3)]
    all_to_all x0 -> x1, starting transfers between devices: none -> 7.37 us  [per_device(): lax.all_to_all(jnp.broadcast_to(current[None], (doms,) + current.shape),...]
    all_gather x1 -> x0, waiting for transfers between devices: 6.17 us -> none  [per_device(): final = lax.all_gather(current, 'dom', axis=0, tiled=False)]
  transfers between devices with their start and end apart: 5 -> 5, of which waited for: 4 -> 4; matrix products, arithmetic and copies ran while one was open for 12% -> 13% of each run, Pallas kernels for 10% -> 0%
where the time goes in v18:
time: 316 us; the launch traced here: 318 us
  waiting for transfers between devices  166 us (53%)
  local copies, waits for them, and re-layouts  49.6 us (16%)
  starting transfers between devices  33.5 us (11%)
  Pallas kernels  30.1 us (10%)
  matrix products  17.4 us (6%)
  between operations  14.7 us (5%)
  other arithmetic  6.8 us (2%)
    all_to_all x1, waiting for transfers between devices, per_device(): got_img = lax.all_to_all(send_img, ('dom', 'cls'), 0, 0, tiled=True)  78.4 us
    all_gather x1, waiting for transfers between devices, per_device(): all_refs = lax.all_gather(owner_chunk, 'dom', axis=2, tiled=False)  30.8 us
    pallas_call x1, Pallas kernels, shift_scores(): pl.pallas_call(_scores_kernel, grid=(steps,), in_specs=[pl.BlockSpec((ast...  30.1 us
    all_to_all x1, waiting for transfers between devices, per_device(): lax.all_to_all(jnp.broadcast_to(current[None], (doms,) + current.shape),...  29.7 us
    all_to_all x1, waiting for transfers between devices, per_device(): got_refs = lax.all_to_all(ref_chunks, 'cls', 0, 0, tiled=True)  26.9 us
    reshape x4, local copies, waits for them, and re-layouts, per_device(): images = images.reshape(groups, capacity, doms, chunk).transpose(2, 0, 1, 3)  18.8 us
    all_to_all x1, starting transfers between devices, per_device(): got_wts = lax.all_to_all(send_wts, ('dom', 'cls'), 0, 0, tiled=True)  11.9 us
    unnamed x26, local copies, waits for them, and re-layouts  10.7 us
  transfers between devices with their start and end apart: 5, of which 4 were waited for; matrix products, arithmetic and copies ran while one was open for 13% of the time, Pallas kernels for 0%

profile of v18, /device:TPU:1, one launch (start us, length us, event | category | flops | bytes accessed | tf_op | source)
XLA Modules:
  0.0 318.0 jit_solution(18256376533171956744)
XLA Ops:
  7.2 0.7 slice_bitcast_fusion.15
  8.3 0.8 slice_bitcast_fusion.14
  9.1 0.8 slice_bitcast_fusion.13
  10.0 0.2 select_reduce_fusion
  10.2 0.2 select_reduce_fusion.2
  10.3 0.7 multiply_add_fusion.3
  11.1 0.2 convolution_convert_fusion.12
  11.3 0.1 copy.98
  11.4 0.3 convolution_convert_fusion.11
  11.7 0.1 copy.100
  11.8 0.3 convolution_convert_fusion.10
  12.2 0.3 convolution_convert_fusion.9
  12.8 0.2 maximum_bitcast_fusion
  13.0 0.6 copy.172
  13.6 1.3 reshape.457
  14.9 11.9 %all-to-all-start = ((bf16[128,2,384]{2,1,0:T(2,128)(2,1)}), bf16[128,2,384]{2,1,0:T(2,128)(2,1)S(1)}, u32[]{:S(2)}, u32[]{:S(2)}) async-start(bf16[128,2,384]{2,1,0:T(2,128)(2,1)} %reshape.457), calls=%async_computation | async-start | bytes 393216 | tf_op jit(solution)/shard_map/all_to_all | solution.py:123
  27.0 0.5 fusion.7
  27.5 0.3 copy.113
  27.8 0.6 convolution_convert_fusion
  28.3 0.9 copy.135
  29.2 2.0 copy.167
  31.3 0.5 fusion.6
  31.7 0.3 copy.111
  32.0 0.6 convolution_convert_fusion.1
  32.6 0.9 copy.133
  33.5 2.0 copy.168
  35.6 0.5 fusion.5
  36.1 0.3 copy.109
  36.4 0.6 convolution_convert_fusion.2
  36.9 0.9 copy.131
  37.8 2.0 copy.169
  39.9 0.5 fusion.4
  40.4 0.3 copy.107
  40.6 0.6 convolution_convert_fusion.3
  41.2 0.9 copy.129
  42.1 12.7 %copy.170 = bf16[8,6,16,1024]{3,0,2,1:T(8,128)(2,1)S(1)} copy(bf16[8,6,16,1024]{3,2,1,0:T(8,128)(2,1)S(1)} %bitcast.208) | data formatting | bytes 3145728 | tf_op jit(solution)/shard_map/reshape | solution.py:109
  54.9 0.8 pad_maximum_fusion
  55.7 7.5 %copy.115 = bf16[128,4,6,1024]{3,1,2,0:T(4,128)(2,1)} copy(bf16[128,4,6,1024]{3,0,2,1:T(8,128)(2,1)S(1)} %pad_maximum_fusion) | data formatting | bytes 12582912 | tf_op jit(solution)/shard_map/stack | solution.py:120
  63.2 10.2 %all-to-all-start.1 = ((bf16[128,4,6,1024]{3,1,2,0:T(4,128)(2,1)}), bf16[128,4,6,1024]{3,1,2,0:T(4,128)(2,1)}, u32[]{:S(2)}, u32[]{:S(2)}) async-start(bf16[128,4,6,1024]{3,1,2,0:T(4,128)(2,1)} %copy.115), calls=%async_computation.1 | async-start | bytes 12582912 | tf_op jit(solution)/shard_map/all_to_all | solution.py:122
  73.4 0.4 reshape.458
  73.8 0.8 convert_reduce_fusion
  74.6 78.4 %all-to-all-done.1 = bf16[128,4,6,1024]{3,1,2,0:T(4,128)(2,1)} async-done(((bf16[128,4,6,1024]{3,1,2,0:T(4,128)(2,1)}), bf16[128,4,6,1024]{3,1,2,0:T(4,128)(2,1)}, u32[]{:S(2)}, u32[]{:S(2)}) %all-to-all-start.1) | async-done | bytes 6291488 | tf_op jit(solution)/shard_map/all_to_all | solution.py:122
  153.0 9.7 %fusion.8 = f32[4,32,1024]{2,1,0:T(8,128)S(1)} fusion(bf16[128,4,6,1024]{3,1,2,0:T(4,128)(2,1)} %all-to-all-done.1, bf16[128,4,6,32]{3,1,2,0:T(4,128)(2,1)S(1)} %bitcast.196), kind=kOutput, calls=%fused_computation.23 | convolution fusion | flops 201326592 | bytes 7012352 | tf_op jit(solution)/shard_map/dot_general | solution.py:124
  162.7 1.0 convert_bitcast_fusion.3
  163.7 0.1 convert_bitcast_fusion.1
  163.8 0.1 convert_bitcast_fusion
  163.9 1.6 broadcast_in_dim.4
  165.5 4.0 %all-to-all-start.2 = ((bf16[8,4,32,1024]{3,2,1,0:T(8,128)(2,1)}), bf16[8,4,32,1024]{3,2,1,0:T(8,128)(2,1)S(1)}, u32[]{:S(2)}, u32[]{:S(2)}) async-start(bf16[8,4,32,1024]{3,2,1,0:T(8,128)(2,1)} %broadcast_in_dim.4), calls=%async_computation.2 | async-start | bytes 4194304 | tf_op jit(solution)/shard_map/all_to_all | solution.py:136
  169.6 0.1 copy.122
  169.8 26.9 %all-to-all-done.2 = bf16[8,4,32,1024]{3,2,1,0:T(8,128)(2,1)S(1)} async-done(((bf16[8,4,32,1024]{3,2,1,0:T(8,128)(2,1)}), bf16[8,4,32,1024]{3,2,1,0:T(8,128)(2,1)S(1)}, u32[]{:S(2)}, u32[]{:S(2)}) %all-to-all-start.2) | async-done | bytes 2097184 | tf_op jit(solution)/shard_map/all_to_all | solution.py:136
  196.6 1.4 fusion.2
  198.0 0.8 copy.171
  198.9 1.6 broadcast_in_dim.5
  200.4 7.4 %all-to-all-start.3 = ((f32[16,32,1024]{2,1,0:T(8,128)}), f32[16,32,1024]{2,1,0:T(8,128)S(1)}, u32[]{:S(2)}, u32[]{:S(2)}) async-start(f32[16,32,1024]{2,1,0:T(8,128)} %broadcast_in_dim.5), calls=%async_computation.3 | async-start | bytes 4194304 | tf_op jit(solution)/shard_map/all_to_all | solution.py:142
  207.9 0.6 fusion.33.sel_ref
  208.5 1.1 convolution_convert_fusion.8
  209.6 29.7 %all-to-all-done.3 = f32[16,32,1024]{2,1,0:T(8,128)S(1)} async-done(((f32[16,32,1024]{2,1,0:T(8,128)}), f32[16,32,1024]{2,1,0:T(8,128)S(1)}, u32[]{:S(2)}, u32[]{:S(2)}) %all-to-all-start.3) | async-done | bytes 2097184 | tf_op jit(solution)/shard_map/all_to_all | solution.py:142
  239.4 1.5 copy.125
  240.8 30.8 %all-gather.3.cloned.1.call-done = bf16[4,32,16384]{2,1,0:T(8,128)(2,1)} async-done(((bf16[4,32,1024]{2,1,0:T(8,128)(2,1)}), bf16[4,32,16384]{2,1,0:T(8,128)(2,1)}) %all-gather.3.cloned.1.call-update) | async-done | bytes 4194320 | tf_op jit(solution)/shard_map/all_gather | solution.py:140
  271.7 5.4 %copy.136 = bf16[16,8,128,128]{3,2,1,0:T(8,128)(2,1)} copy(bf16[16,8,128,128]{3,1,2,0:T(8,128)(2,1)} %bitcast.209) | data formatting | bytes 8388608
  277.1 30.1 %shard_map.95 = f32[4,32,16,128]{3,2,1,0:T(8,128)} custom-call(bf16[2,1024,128]{2,1,0:T(8,128)(2,1)} %bitcast.218, bf16[128,256]{1,0:T(8,128)(2,1)} %fusion.33.sel_ref, bf16[4,32,128,128]{3,2,1,0:T(8,128)(2,1)} %bitcast.210), custom_call_target="tpu_custom_call" | custom-call | flops 9663676416 | bytes 5767168 | tf_op jit(solution)/shard_map/pallas_call | solution.py:57
  307.2 1.3 fusion.11
  308.5 0.6 copy.118
  309.2 1.8 mul.224
  (53 shorter events, 1.3 us)
Async XLA Ops:
  12.8 14.0 %copy-start.7 = (s32[4,16]{1,0:T(4,128)S(1)}, s32[4,16]{1,0:T(4,128)}, u32[]{:S(2)}) copy-start(s32[4,16]{1,0:T(4,128)} %param.13) | copy-start | bytes 772
  12.8 14.0 %copy-start.5 = (bf16[16,16384]{1,0:T(8,128)(2,1)S(1)}, bf16[16,16384]{1,0:T(8,128)(2,1)}, u32[]{:S(2)}) copy-start(bf16[16,16384]{1,0:T(8,128)(2,1)} %param.8) | copy-start | bytes 1572868
  14.9 48.3 %all-to-all-start = ((bf16[128,2,384]{2,1,0:T(2,128)(2,1)}), bf16[128,2,384]{2,1,0:T(2,128)(2,1)S(1)}, u32[]{:S(2)}, u32[]{:S(2)}) async-start(bf16[128,2,384]{2,1,0:T(2,128)(2,1)} %reshape.457), calls=%async_computation | async-start | bytes 393216 | tf_op jit(solution)/shard_map/all_to_all | solution.py:123
  26.9 13.0 %copy-start = (bf16[2,8,128,128]{3,2,1,0:T(8,128)(2,1)}, bf16[2,8,128,128]{3,2,1,0:T(8,128)(2,1)S(1)}, u32[]{:S(2)}) copy-start(bf16[2,8,128,128]{3,2,1,0:T(8,128)(2,1)S(1)} %copy.126) | copy-start | bytes 1572868
  41.2 13.6 %copy-start.4 = (bf16[8,6,16,1024]{3,0,2,1:T(8,128)(2,1)S(1)}, bf16[8,6,16,1024]{3,0,2,1:T(8,128)(2,1)}, u32[]{:S(2)}) copy-start(bf16[8,6,16,1024]{3,0,2,1:T(8,128)(2,1)} %copy.169) | copy-start | bytes 4718596
  42.1 12.7 %copy-start.2 = (bf16[8,6,16,1024]{3,0,2,1:T(8,128)(2,1)S(1)}, bf16[8,6,16,1024]{3,0,2,1:T(8,128)(2,1)}, u32[]{:S(2)}) copy-start(bf16[8,6,16,1024]{3,0,2,1:T(8,128)(2,1)} %copy.167) | copy-start | bytes 4718596
  42.1 12.7 %copy-start.3 = (bf16[8,6,16,1024]{3,0,2,1:T(8,128)(2,1)S(1)}, bf16[8,6,16,1024]{3,0,2,1:T(8,128)(2,1)}, u32[]{:S(2)}) copy-start(bf16[8,6,16,1024]{3,0,2,1:T(8,128)(2,1)} %copy.168) | copy-start | bytes 4718596
  63.2 11.4 %copy-start.6 = (f32[32]{0:T(128)S(1)}, f32[32]{0:T(128)}, u32[]{:S(2)}) copy-start(f32[32]{0:T(128)} %param.10) | copy-start | bytes 388
  63.2 89.8 %all-to-all-start.1 = ((bf16[128,4,6,1024]{3,1,2,0:T(4,128)(2,1)}), bf16[128,4,6,1024]{3,1,2,0:T(4,128)(2,1)}, u32[]{:S(2)}, u32[]{:S(2)}) async-start(bf16[128,4,6,1024]{3,1,2,0:T(4,128)(2,1)} %copy.115), calls=%async_computation.1 | async-start | bytes 12582912 | tf_op jit(solution)/shard_map/all_to_all | solution.py:122
  165.5 4.1 %copy-start.8 = (s32[4]{0:T(128)S(1)}, s32[4]{0:T(128)}, u32[]{:S(2)}) copy-start(s32[4]{0:T(128)} %param.15) | copy-start | bytes 52
  165.5 31.1 %all-to-all-start.2 = ((bf16[8,4,32,1024]{3,2,1,0:T(8,128)(2,1)}), bf16[8,4,32,1024]{3,2,1,0:T(8,128)(2,1)S(1)}, u32[]{:S(2)}, u32[]{:S(2)}) async-start(bf16[8,4,32,1024]{3,2,1,0:T(8,128)(2,1)} %broadcast_in_dim.4), calls=%async_computation.2 | async-start | bytes 4194304 | tf_op jit(solution)/shard_map/all_to_all | solution.py:136
  169.6 102.1 %all-gather.3.cloned.1.call-start = ((), (), s32[]{:S(2)}) async-start(), calls=%async_computation.4 | async-start | bytes 4456448 | tf_op jit(solution)/shard_map/all_gather | solution.py:140
  200.4 8.1 %copy-start.1 = (bf16[2,8,128,128]{3,2,1,0:T(8,128)(2,1)S(1)}, bf16[2,8,128,128]{3,2,1,0:T(8,128)(2,1)}, u32[]{:S(2)}) copy-start(bf16[2,8,128,128]{3,2,1,0:T(8,128)(2,1)} %copy-done) | copy-start | bytes 1572868
  200.4 38.9 %all-to-all-start.3 = ((f32[16,32,1024]{2,1,0:T(8,128)}), f32[16,32,1024]{2,1,0:T(8,128)S(1)}, u32[]{:S(2)}, u32[]{:S(2)}) async-start(f32[16,32,1024]{2,1,0:T(8,128)} %broadcast_in_dim.5), calls=%async_computation.3 | async-start | bytes 4194304 | tf_op jit(solution)/shard_map/all_to_all | solution.py:142
Sparse Core Ops, SparseCore 0:
  199.0 72.6 all-gather.2
